TPU v7x, 1024 devices: a whole 8x8x8 slice. The times are simulated.
1024 devices in a mesh: gx: 16 (over x_hi, y), gy: 16 (over z, core), gz: 4 (over x_lo).
Axes of the slice: x: 8 (x_hi: 2, x_lo: 4; x = x_hi * 4 + x_lo), y: 8, z: 8, core: 2. Of those that a mesh axis runs over, the one named last changes fastest.
Arguments:
- positions: float32 [16, 16, 4, 3, 256], P('gx', 'gy', 'gz'), may hold values from 0.3 to 7.7, as said below
- velocities: float32 [16, 16, 4, 3, 256], P('gx', 'gy', 'gz'), may hold values from -6 to 6
- species: int32 [16, 16, 4, 256], P('gx', 'gy', 'gz'), may hold values from 0 to 3
- pair_table: int32 [16, 16, 4, 3, 1536], P('gx', 'gy', 'gz'), may hold values from 0 to 6911, as said below
- live_blocks: int32 [16, 16, 4], P('gx', 'gy', 'gz'), may hold values from 6 to 12, as said below
- owners: int32 [16, 16, 4, 2], P('gx', 'gy', 'gz'), may hold values from 0 to 3, as said below
- radial_weight: float32 [256, 8], replicated, may hold values from -2 to 2
- center_embed: float32 [256, 4], replicated, may hold values from -3 to 3
- neighbour_embed: float32 [256, 4], replicated, may hold values from -3 to 3
- vector_weight: float32 [32, 8], replicated, may hold values from -2 to 2
- env_weight: float32 [2, 32, 256], replicated, may hold values from -0.375 to 0.375
- vector_gate: float32 [32, 256], replicated, may hold values from -0.375 to 0.375
- latent_weight: float32 [2, 256, 288], replicated, may hold values from -0.375 to 0.375
- energy_weight: float32 [256], replicated, may hold values from -0.375 to 0.375
Outputs:
- migrated: float32 [16, 16, 4, 4, 9, 128], P('gx', 'gy', 'gz')
Inputs may be any that keep to these rules, and one draw needn't show every extreme that they name: `positions`: atom k of a domain lies within 0.2 in each coordinate of the point (ix + 0.5, iy + 0.5, iz + 0.5) with k = (8 ix + iy) (4) + iz. `pair_table`: row 0 is a centre atom index below 256; row 1 a neighbour index as in the statement, never the centre itself; row 2 equals the species of that neighbour atom in its own domain. `live_blocks`: some device uses all 12 blocks. The owners of one device's blocks are distinct; in every gz group some device is the owner of one block of every device of the group.
All inputs are finite; a program needn't handle non-finite values.
Results may differ from a plain program's by a relative error of at most 0.0003.
Values sent between devices are 32-bit elements; how exact they have to be, the bound alone decides.
No kernel may reach another device: no remote copies, remote signals or barrier semaphores. Data moves between devices by JAX's collectives and lax.ppermute only.
A program may use at most 32 MiB of HBM per device.

v0:
```python
import jax
import jax.numpy as jnp
from jax import lax
from jax.sharding import PartitionSpec as P

CUTOFF = 5.0
ENV_SCALE = 0.4
TIME_STEP = 0.2


def extended_2(block, sides, width):
    for axis, dim in sides:
        count = lax.axis_size(axis)
        forward = [(i, i + 1) for i in range(count - 1)]
        forward.append((count - 1, 0))
        backward = [(target, source) for source, target in forward]
        low = lax.ppermute(
            lax.slice_in_dim(block, block.shape[dim] - width, None, axis=dim), axis, forward
        )
        high = lax.ppermute(lax.slice_in_dim(block, 0, width, axis=dim), axis, backward)
        block = jnp.concatenate([low, block, high], axis=dim)
    return block


def matmul(left, right):
    return jnp.dot(left, right, precision=lax.Precision.HIGHEST)


def pair_energy(
    extended,
    pair_rows,
    live_count,
    own_species,
    radial_weight,
    center_embed,
    neighbour_embed,
    vector_weight,
    env_weight,
    vector_gate,
    latent_weight,
    energy_weight,
):
    atoms_here = own_species.shape[0]
    pair_count = pair_rows.shape[1]
    depth = atoms_here // 64
    centres = pair_rows[0]
    neighbour = pair_rows[1]
    other_species = pair_rows[2]
    slot_index = neighbour // atoms_here
    atom_index = neighbour - slot_index * atoms_here
    offset_x = (slot_index // 9 - 1).astype(jnp.float32) * 8.0
    offset_y = (slot_index // 3 % 3 - 1).astype(jnp.float32) * 8.0
    offset_z = (slot_index % 3 - 1).astype(jnp.float32) * float(depth)
    shifts = jnp.stack([offset_x, offset_y, offset_z])
    far_end = extended[slot_index, :, atom_index].T
    near_end = extended[13, :, centres].T
    displace = far_end + shifts - near_end
    distance = jnp.sqrt(jnp.sum(displace * displace, axis=0))
    unit = displace / distance
    orders = jnp.arange(1, radial_weight.shape[1] + 1).astype(jnp.float32)
    basis = (
        jnp.sqrt(2.0 / CUTOFF)
        * jnp.sin(orders[:, None] * jnp.pi * distance[None] / CUTOFF)
        / distance[None]
    )
    ratio = distance / CUTOFF
    in_use = (jnp.arange(pair_count) < live_count * 128).astype(jnp.float32)
    envelope = (1.0 - ratio * ratio) ** 2 * in_use
    kinds = jnp.arange(center_embed.shape[1])[:, None]
    centre_hot = (kinds == own_species[centres][None]).astype(jnp.float32)
    other_hot = (kinds == other_species[None]).astype(jnp.float32)
    latent = envelope[None] * jax.nn.silu(
        matmul(radial_weight, basis)
        + matmul(center_embed, centre_hot)
        + matmul(neighbour_embed, other_hot)
    )
    channels = vector_weight.shape[0]
    vectors = envelope[None, None] * matmul(vector_weight, basis)[None] * unit[:, None, :]
    member = (centres[:, None] == jnp.arange(atoms_here)[None]).astype(jnp.float32)
    n_layers = env_weight.shape[0]
    for layer in range(n_layers):
        env_pairs = matmul(env_weight[layer], latent)
        spread = (unit[:, None, :] * env_pairs[None]).reshape(3 * channels, pair_count)
        environment = ENV_SCALE * matmul(spread, member)
        at_pairs = lax.dot_general(
            environment, member, (((1,), (1,)), ((), ())), precision=lax.Precision.HIGHEST
        )
        at_pairs = at_pairs.reshape(3, channels, pair_count)
        scalars = jnp.sum(vectors * at_pairs, axis=0)
        update = matmul(latent_weight[layer], jnp.concatenate([latent, scalars], axis=0))
        if layer + 1 < n_layers:
            vectors = vectors + at_pairs * matmul(vector_gate, latent)[None]
        latent = latent + envelope[None] * jax.nn.silu(update)
    return jnp.sum(matmul(energy_weight[None], latent))


def per_device(
    positions,
    velocities,
    species,
    pair_table,
    live_blocks,
    owners,
    radial_weight,
    center_embed,
    neighbour_embed,
    vector_weight,
    env_weight,
    vector_gate,
    latent_weight,
    energy_weight,
):
    atoms_here = positions.shape[4]
    depth = atoms_here // 64
    zcount = lax.axis_size("gz")
    beside_all = extended_2(positions, (("gx", 0), ("gy", 1), ("gz", 2)), 1)
    extended = beside_all.reshape(27, 3, atoms_here)
    own_species = species[0, 0, 0]
    grad = jax.grad(pair_energy)(
        extended,
        pair_table[0, 0, 0],
        live_blocks[0, 0, 0],
        own_species,
        radial_weight,
        center_embed,
        neighbour_embed,
        vector_weight,
        env_weight,
        vector_gate,
        latent_weight,
        energy_weight,
    )
    grad = grad.reshape(3, 3, 3, 3, atoms_here)
    rim = extended_2(grad, (("gx", 0), ("gy", 1), ("gz", 2)), 1)
    total = jnp.sum(rim[0::2, 0::2, 0::2], axis=(0, 1, 2))
    forces = -total
    inverse_mass = 1.0 / (1.0 + own_species.astype(jnp.float32))
    new_vel = velocities[0, 0, 0] + TIME_STEP * forces * inverse_mass[None]
    new_pos = positions[0, 0, 0] + TIME_STEP * new_vel
    state = jnp.concatenate([new_pos, new_vel, forces], axis=0)
    blocks_count = atoms_here // 128
    blocks = state.reshape(9, blocks_count, 128).transpose(1, 0, 2)
    hits = (owners[0, 0, 0][:, None] == jnp.arange(zcount)[None]).astype(jnp.float32)
    outgoing = jnp.einsum("bd,bcq->dcq", hits, blocks, precision=lax.Precision.HIGHEST)
    flags = jnp.sum(hits, axis=0)[:, None]
    arrived, arrived_flags = (
        lax.all_to_all(outgoing, "gz", split_axis=0, concat_axis=0, tiled=True),
        lax.all_to_all(flags, "gz", split_axis=0, concat_axis=0, tiled=True),
    )
    myself = lax.axis_index("gz")
    source = jnp.arange(zcount, dtype=jnp.int32)
    rise = arrived_flags[:, 0] * (source - myself).astype(jnp.float32) * float(depth)
    arrived = arrived.at[:, 2, :].add(rise[:, None])
    return arrived[None, None, None]


def solution(mesh):
    in_specs = (
        P("gx", "gy", "gz", None, None),
        P("gx", "gy", "gz", None, None),
        P("gx", "gy", "gz", None),
        P("gx", "gy", "gz", None, None),
        P("gx", "gy", "gz"),
        P("gx", "gy", "gz", None),
        P(),
        P(),
        P(),
        P(),
        P(),
        P(),
        P(),
        P(),
    )
    out_specs = P("gx", "gy", "gz", None, None, None)
    return jax.shard_map(
        per_device, mesh=mesh, in_specs=in_specs, out_specs=out_specs, check_vma=False
    )
```

profile of v0, /device:TPU:112, one launch (start us, length us, event | category | flops | bytes accessed | tf_op | source)
XLA Modules:
  0.0 197.4 jit_solution(16199839315724310500)
XLA Ops:
  0.0 5.9 %collective-permute-start = (f32[1,1,1,3,256]{4,2,3,1,0:T(1,128)}, f32[1,1,1,3,256]{4,2,3,1,0:T(1,128)S(1)}, u32[]{:S(2)}, u32[]{:S(2)}) collective-permute-start(f32[1,1,1,3,256]{4,2,3,1,0:T(1,128)} %param.16), channel_id=1, source_target_pairs={{0,64},{64,128},{128,192},{192,256},{256,320},{320,384},{384,448},... | collective-permute-start | bytes 9224 | tf_op jit(solution)/shard_map/ppermute | solution.py:17
  5.9 1.9 collective-permute-start.1
  11.9 9.5 %gather_fusion.2 = s32[1536]{0:T(1024)S(1)} fusion(s32[256]{0:T(256)S(1)} %bitcast.180, s32[2048]{0:T(1024)S(1)} %pad_clamp_fusion), kind=kCustom, calls=%fused_computation.2 | custom fusion | bytes 18432 | tf_op jit(solution)/shard_map/jvp()/gather | solution.py:70
  21.4 2.0 %fusion.96 = f32[1536,256]{0,1:T(8,128)} fusion(f32[256,4]{0,1:T(4,128)S(1)} %copy-done.5, s32[1536]{0:T(1024)S(1)} %gather_fusion.2), kind=kOutput, calls=%fused_computation.168 | convolution fusion | flops 18880512 | bytes 1583104 | tf_op jit(solution)/shard_map/jvp()/dot_general | solution.py:26
  23.7 14.6 %collective-permute-start.3 = (f32[3,1,1,3,256]{4,2,3,1,0:T(1,128)S(1)}, f32[3,1,1,3,256]{4,2,3,1,0:T(1,128)S(1)}, u32[]{:S(2)}, u32[]{:S(2)}) collective-permute-start(f32[3,1,1,3,256]{4,2,3,1,0:T(1,128)S(1)} %constant_dynamic-update-slice_fusion), channel_id=1, source_target_pairs={{4,0},{8,4},{12,8},{16,12},{20,16},{24,20},{28,24},{32,28},{36,32}... | collective-permute-start | bytes 27656 | tf_op jit(solution)/shard_map/ppermute | solution.py:20
  39.7 2.9 %collective-permute-done.2 = f32[3,1,1,3,256]{4,2,3,1,0:T(1,128)S(1)} collective-permute-done((f32[3,1,1,3,256]{4,2,3,1,0:T(1,128)S(1)}, f32[3,1,1,3,256]{4,2,3,1,0:T(1,128)S(1)}, u32[]{:S(2)}, u32[]{:S(2)}) %collective-permute-start.2) | collective-permute-done | bytes 9248 | tf_op jit(solution)/shard_map/ppermute | solution.py:17
  42.6 3.1 %collective-permute-start.5 = (f32[3,3,1,3,256]{4,2,3,1,0:T(1,128)S(1)}, f32[3,3,1,3,256]{4,2,3,1,0:T(1,128)S(1)}, u32[]{:S(2)}, u32[]{:S(2)}) collective-permute-start(f32[3,3,1,3,256]{4,2,3,1,0:T(1,128)S(1)} %pad_maximum_fusion.4), channel_id=1, source_target_pairs={{1,0},{2,1},{3,2},{0,3},{5,4},{6,5},{7,6},{4,7},{9,8},{10,9},{11,1... | collective-permute-start | bytes 82952 | tf_op jit(solution)/shard_map/ppermute | solution.py:20
  45.7 3.0 %collective-permute-start.4 = (f32[3,3,1,3,256]{4,2,3,1,0:T(1,128)S(1)}, f32[3,3,1,3,256]{4,2,3,1,0:T(1,128)S(1)}, u32[]{:S(2)}, u32[]{:S(2)}) collective-permute-start(f32[3,3,1,3,256]{4,2,3,1,0:T(1,128)S(1)} %pad_maximum_fusion.4), channel_id=1, source_target_pairs={{0,1},{1,2},{2,3},{3,0},{4,5},{5,6},{6,7},{7,4},{8,9},{9,10},{10,1... | collective-permute-start | bytes 82952 | tf_op jit(solution)/shard_map/ppermute | solution.py:17
  49.4 3.8 %collective-permute-done.4 = f32[3,3,1,3,256]{4,2,3,1,0:T(1,128)S(1)} collective-permute-done((f32[3,3,1,3,256]{4,2,3,1,0:T(1,128)S(1)}, f32[3,3,1,3,256]{4,2,3,1,0:T(1,128)S(1)}, u32[]{:S(2)}, u32[]{:S(2)}) %collective-permute-start.4) | collective-permute-done | bytes 27680 | tf_op jit(solution)/shard_map/ppermute | solution.py:17
  53.3 2.4 %copy.126 = f32[3,3,3,3,256]{3,4,2,1,0:T(8,128)} copy(f32[3,3,3,3,256]{4,2,3,1,0:T(4,128)S(1)} %pad_maximum_fusion.2) | data formatting | bytes 165888 | tf_op jit(solution)/shard_map/concatenate | solution.py:21
  55.8 15.5 %gather_fusion.1 = f32[1536,3]{1,0:T(8,128)S(1)} fusion(f32[27,3,256]{1,2,0:T(8,128)} %bitcast.181, s32[1536]{0:T(1024)S(1)} %get-tuple-element.29), kind=kCustom, calls=%fused_computation.1 | custom fusion | bytes 49152 | tf_op jit(solution)/shard_map/jvp()/gather | solution.py:56
  71.6 15.5 %gather_fusion = f32[1536,3]{1,0:T(8,128)S(1)} fusion(f32[27,3,256]{1,2,0:T(8,128)} %bitcast.182, s32[1536]{0:T(1024)S(1)} %get-tuple-element.55), kind=kCustom, calls=%fused_computation | custom fusion | bytes 49152 | tf_op jit(solution)/shard_map/jvp()/gather | solution.py:55
  87.5 3.4 %broadcast_multiply_fusion = (f32[256,1536]{1,0:T(8,128)S(1)}, f32[256,1536]{1,0:T(8,128)S(1)}) fusion(f32[1536]{0:T(1024)S(1)} %get-tuple-element.59, f32[1536,256]{0,1:T(8,128)S(1)} %fusion.97, f32[1536,256]{0,1:T(8,128)} %fusion.96, f32[256,8]{0,1:T(8,128)S(1)} %copy-done.10, f32[1536]{0:T(1024)S(1)} %get-tuple-element.60, f32[8]{0:T(128)S(1)} %get-tuple-element.76), kind=kOutput, calls=%fused_computation.90 | convolution fusion | flops 40550400 | bytes 6311968 | tf_op jit(solution)/shard_map/jvp()/dot_general | solution.py:26
  94.9 3.1 %multiply_add_fusion = (f32[256,1536]{1,0:T(8,128)S(1)}, f32[256,1536]{1,0:T(8,128)S(1)}) fusion(f32[256,1536]{1,0:T(8,128)S(1)} %get-tuple-element.63, f32[1536]{0:T(1024)S(1)} %get-tuple-element.59, f32[2,256,288]{1,2,0:T(8,128)S(1)} %copy-done.9, f32[32,1536]{1,0:T(8,128)S(1)} %multiply_reduce_fusion.11), kind=kOutput, calls=%fused_computation.53 | convolution fusion | flops 1361756160 | bytes 6791168 | tf_op jit(solution)/shard_map/jvp()/dot_general | solution.py:26
  99.9 2.0 %fusion.35 = f32[96,1536]{1,0:T(8,128)S(1)} fusion(f32[96,256]{1,0:T(8,128)S(1)} %fusion.41, s32[1536]{0:T(1024)S(1)} %get-tuple-element.26), kind=kOutput, calls=%fused_computation.61 | convolution fusion | flops 453378048 | bytes 694272 | tf_op jit(solution)/shard_map/jvp()/dot_general | solution.py:85
  103.6 3.1 %multiply_reduce_fusion.2 = (f32[1536]{0:T(1024)S(1)}, f32[256,1536]{1,0:T(8,128)S(1)}) fusion(f32[256]{0:T(256)S(1)} %copy-done.11, f32[2,256,288]{1,2,0:T(8,128)S(1)} %copy-done.9, f32[32,1536]{1,0:T(8,128)S(1)} %get-tuple-element.46, f32[256,1536]{1,0:T(8,128)S(1)} %get-tuple-element.67), kind=kOutput, calls=%fused_computation.48 | convolution fusion | flops 1361754624 | bytes 3644416 | tf_op jit(solution)/shard_map/jvp()/dot_general | solution.py:26
  106.7 2.3 %convolution_bitcast_fusion.1 = f32[288,1536]{1,0:T(8,128)S(1)} fusion(f32[256,1536]{1,0:T(8,128)S(1)} %get-tuple-element.72, f32[256]{0:T(256)S(1)} %copy-done.11, f32[1536]{0:T(1024)S(1)} %get-tuple-element.59, f32[2,256,288]{1,2,0:T(8,128)S(1)} %copy-done.9), kind=kOutput, calls=%fused_computation.7 | convolution fusion | flops 1362886656 | bytes 3646464 | tf_op jit(solution)/shard_map/transpose(jvp())/dot_general | solution.py:26
  109.9 1.7 fusion.33
  111.7 1.9 multiply_reduce_fusion.1
  113.6 2.3 %convolution_bitcast_fusion = f32[288,1536]{1,0:T(8,128)S(1)} fusion(f32[256,1536]{1,0:T(8,128)S(1)} %get-tuple-element.68, f32[256,1536]{1,0:T(8,128)S(1)} %get-tuple-element.74, f32[1536]{0:T(1024)S(1)} %get-tuple-element.59, f32[2,256,288]{1,2,0:T(8,128)S(1)} %copy-done.9), kind=kOutput, calls=%fused_computation.6 | convolution fusion | flops 1362886656 | bytes 5218304 | tf_op jit(solution)/shard_map/transpose(jvp())/dot_general | solution.py:26
  120.7 1.8 multiply_reduce_fusion
  124.7 19.1 %scatter_custom_fusion = f32[3,6912]{0,1:T(8,128)} fusion(s32[3072]{0:T(1024)S(1)} %broadcast_select_fusion, f32[3072,3]{1,0:T(8,128)S(1)} %copy.129, f32[]{:T(128)} %constant.103.clone.1), kind=kCustom, calls=%fused_computation.34 | custom fusion | flops 9216 | bytes 82948
  143.8 2.7 %copy.130 = f32[3,27,256]{2,1,0:T(8,128)S(1)} copy(f32[3,27,256]{0,2,1:T(8,128)} %bitcast.186) | data formatting | bytes 165888
  146.6 9.1 %collective-permute-start.6 = (f32[1,3,3,3,256]{4,0,3,2,1:T(1,128)S(1)}, f32[1,3,3,3,256]{4,0,3,2,1:T(1,128)S(1)}, u32[]{:S(2)}, u32[]{:S(2)}) collective-permute-start(f32[1,3,3,3,256]{4,0,3,2,1:T(1,128)S(1)} %copy.150), channel_id=1, source_target_pairs={{0,64},{64,128},{128,192},{192,256},{256,320},{320,384},{384,448},... | collective-permute-start | bytes 82952 | tf_op jit(solution)/shard_map/ppermute | solution.py:17
  155.8 1.9 collective-permute-start.7
  157.8 9.8 %collective-permute-done.7 = f32[1,3,3,3,256]{4,0,3,2,1:T(1,128)S(1)} collective-permute-done((f32[1,3,3,3,256]{4,0,3,2,1:T(1,128)S(1)}, f32[1,3,3,3,256]{4,0,3,2,1:T(1,128)S(1)}, u32[]{:S(2)}, u32[]{:S(2)}) %collective-permute-start.7) | collective-permute-done | bytes 27680 | tf_op jit(solution)/shard_map/ppermute | solution.py:20
  169.0 3.2 %all-to-all-start.1 = ((f32[4,1,1]{2,1,0:T(1,128)}), f32[4,1,1]{2,1,0:T(1,128)S(1)}, u32[]{:S(2)}, u32[]{:S(2)}) async-start(f32[4,1,1]{2,1,0:T(1,128)} %copy.147), calls=%async_computation.1 | async-start | bytes 4096 | tf_op jit(solution)/shard_map/all_to_all | solution.py:148
  172.8 5.5 %collective-permute-start.11 = (f32[5,5,1,3,256]{4,2,3,1,0:T(1,128)S(1)}, f32[5,5,1,3,256]{4,2,3,1,0:T(1,128)S(1)}, u32[]{:S(2)}, u32[]{:S(2)}) collective-permute-start(f32[5,5,1,3,256]{4,2,3,1,0:T(1,128)S(1)} %copy.140), channel_id=1, source_target_pairs={{1,0},{2,1},{3,2},{0,3},{5,4},{6,5},{7,6},{4,7},{9,8},{10,9},{11,1... | collective-permute-start | bytes 230408 | tf_op jit(solution)/shard_map/ppermute | solution.py:20
  178.3 1.9 collective-permute-start.10
  180.5 5.9 %collective-permute-done.10 = f32[5,5,1,3,256]{4,2,3,1,0:T(1,128)S(1)} collective-permute-done((f32[5,5,1,3,256]{4,2,3,1,0:T(1,128)S(1)}, f32[5,5,1,3,256]{4,2,3,1,0:T(1,128)S(1)}, u32[]{:S(2)}, u32[]{:S(2)}) %collective-permute-start.10) | collective-permute-done | bytes 76832 | tf_op jit(solution)/shard_map/ppermute | solution.py:17
  187.5 3.3 %all-to-all-start = ((f32[4,9,128]{2,1,0:T(8,128)}), f32[4,9,128]{2,1,0:T(8,128)S(1)}, u32[]{:S(2)}, u32[]{:S(2)}) async-start(f32[4,9,128]{2,1,0:T(8,128)} %copy.146), calls=%async_computation | async-start | bytes 65536 | tf_op jit(solution)/shard_map/all_to_all | solution.py:147
  190.8 5.6 %all-to-all-done = f32[4,9,128]{2,1,0:T(8,128)S(1)} async-done(((f32[4,9,128]{2,1,0:T(8,128)}), f32[4,9,128]{2,1,0:T(8,128)S(1)}, u32[]{:S(2)}, u32[]{:S(2)}) %all-to-all-start) | async-done | bytes 18464 | tf_op jit(solution)/shard_map/all_to_all | solution.py:147
  (124 shorter events, 25.8 us)
Async XLA Ops:
  0.0 101.9 %copy-start = (f32[32,256]{1,0:T(8,128)S(1)}, f32[32,256]{1,0:T(8,128)}, u32[]{:S(2)}) copy-start(f32[32,256]{1,0:T(8,128)} %param.27) | copy-start | bytes 98308
  0.0 11.9 %copy-start.1 = (s32[1,1,1,256]{3,2,1,0:T(1,128)S(1)}, s32[1,1,1,256]{3,2,1,0:T(1,128)}, u32[]{:S(2)}) copy-start(s32[1,1,1,256]{3,2,1,0:T(1,128)} %param.18) | copy-start | bytes 3076
  0.0 23.6 %collective-permute-start = (f32[1,1,1,3,256]{4,2,3,1,0:T(1,128)}, f32[1,1,1,3,256]{4,2,3,1,0:T(1,128)S(1)}, u32[]{:S(2)}, u32[]{:S(2)}) collective-permute-start(f32[1,1,1,3,256]{4,2,3,1,0:T(1,128)} %param.16), channel_id=1, source_target_pairs={{0,64},{64,128},{128,192},{192,256},{256,320},{320,384},{384,448},... | collective-permute-start | bytes 9224 | tf_op jit(solution)/shard_map/ppermute | solution.py:17
  5.9 17.7 %collective-permute-start.1 = (f32[1,1,1,3,256]{4,2,3,1,0:T(1,128)}, f32[1,1,1,3,256]{4,2,3,1,0:T(1,128)S(1)}, u32[]{:S(2)}, u32[]{:S(2)}) collective-permute-start(f32[1,1,1,3,256]{4,2,3,1,0:T(1,128)} %param.16), channel_id=1, source_target_pairs={{64,0},{128,64},{192,128},{256,192},{320,256},{384,320},{448,384},... | collective-permute-start | bytes 9224 | tf_op jit(solution)/shard_map/ppermute | solution.py:20
  11.9 9.5 %copy-start.5 = (f32[256,4]{0,1:T(4,128)S(1)}, f32[256,4]{0,1:T(4,128)}, u32[]{:S(2)}) copy-start(f32[256,4]{0,1:T(4,128)} %param.23) | copy-start | bytes 12292
  21.4 2.0 %copy-start.7 = (s32[2]{0:T(128)S(1)}, s32[2]{0:T(128)}, u32[]{:S(2)}) copy-start(s32[2]{0:T(128)} %constant.135) | copy-start | bytes 28
  21.4 2.1 %copy-start.8 = (s32[2]{0:T(128)S(1)}, s32[2]{0:T(128)}, u32[]{:S(2)}) copy-start(s32[2]{0:T(128)} %constant.138) | copy-start | bytes 28
  21.4 2.3 %copy-start.4 = (f32[1,1,1,3,256]{4,2,3,1,0:T(1,128)S(1)}, f32[1,1,1,3,256]{4,2,3,1,0:T(1,128)}, u32[]{:S(2)}) copy-start(f32[1,1,1,3,256]{4,2,3,1,0:T(1,128)} %param.16) | copy-start | bytes 9220
  23.7 16.0 %collective-permute-start.3 = (f32[3,1,1,3,256]{4,2,3,1,0:T(1,128)S(1)}, f32[3,1,1,3,256]{4,2,3,1,0:T(1,128)S(1)}, u32[]{:S(2)}, u32[]{:S(2)}) collective-permute-start(f32[3,1,1,3,256]{4,2,3,1,0:T(1,128)S(1)} %constant_dynamic-update-slice_fusion), channel_id=1, source_target_pairs={{4,0},{8,4},{12,8},{16,12},{20,16},{24,20},{28,24},{32,28},{36,32}... | collective-permute-start | bytes 27656 | tf_op jit(solution)/shard_map/ppermute | solution.py:20
  38.3 4.3 %collective-permute-start.2 = (f32[3,1,1,3,256]{4,2,3,1,0:T(1,128)S(1)}, f32[3,1,1,3,256]{4,2,3,1,0:T(1,128)S(1)}, u32[]{:S(2)}, u32[]{:S(2)}) collective-permute-start(f32[3,1,1,3,256]{4,2,3,1,0:T(1,128)S(1)} %constant_dynamic-update-slice_fusion), channel_id=1, source_target_pairs={{0,4},{4,8},{8,12},{12,16},{16,20},{20,24},{24,28},{28,32},{32,36}... | collective-permute-start | bytes 27656 | tf_op jit(solution)/shard_map/ppermute | solution.py:17
  42.6 6.8 %collective-permute-start.5 = (f32[3,3,1,3,256]{4,2,3,1,0:T(1,128)S(1)}, f32[3,3,1,3,256]{4,2,3,1,0:T(1,128)S(1)}, u32[]{:S(2)}, u32[]{:S(2)}) collective-permute-start(f32[3,3,1,3,256]{4,2,3,1,0:T(1,128)S(1)} %pad_maximum_fusion.4), channel_id=1, source_target_pairs={{1,0},{2,1},{3,2},{0,3},{5,4},{6,5},{7,6},{4,7},{9,8},{10,9},{11,1... | collective-permute-start | bytes 82952 | tf_op jit(solution)/shard_map/ppermute | solution.py:20
  45.7 7.6 %collective-permute-start.4 = (f32[3,3,1,3,256]{4,2,3,1,0:T(1,128)S(1)}, f32[3,3,1,3,256]{4,2,3,1,0:T(1,128)S(1)}, u32[]{:S(2)}, u32[]{:S(2)}) collective-permute-start(f32[3,3,1,3,256]{4,2,3,1,0:T(1,128)S(1)} %pad_maximum_fusion.4), channel_id=1, source_target_pairs={{0,1},{1,2},{2,3},{3,0},{4,5},{5,6},{6,7},{7,4},{8,9},{9,10},{10,1... | collective-permute-start | bytes 82952 | tf_op jit(solution)/shard_map/ppermute | solution.py:17
  71.6 15.9 %copy-start.10 = (f32[256,8]{0,1:T(8,128)S(1)}, f32[256,8]{0,1:T(8,128)}, u32[]{:S(2)}) copy-start(f32[256,8]{0,1:T(8,128)} %param.22) | copy-start | bytes 24580
  87.5 3.4 %copy-start.2 = (f32[2,32,256]{2,1,0:T(8,128)S(1)}, f32[2,32,256]{2,1,0:T(8,128)}, u32[]{:S(2)}) copy-start(f32[2,32,256]{2,1,0:T(8,128)} %param.26) | copy-start | bytes 196612
  90.9 3.4 %copy-start.3 = (f32[32,8]{0,1:T(8,128)S(1)}, f32[32,8]{0,1:T(8,128)}, u32[]{:S(2)}) copy-start(f32[32,8]{0,1:T(8,128)} %param.25) | copy-start | bytes 3076
  92.0 2.9 %copy-start.9 = (f32[2,256,288]{1,2,0:T(8,128)S(1)}, f32[2,256,288]{1,2,0:T(8,128)}, u32[]{:S(2)}) copy-start(f32[2,256,288]{1,2,0:T(8,128)} %param.28) | copy-start | bytes 1769476
  103.0 0.7 copy-start.11
  143.8 24.5 %copy-start.12 = (s32[1,1,1,2]{3,2,1,0:T(1,128)S(1)}, s32[1,1,1,2]{3,2,1,0:T(1,128)}, u32[]{:S(2)}) copy-start(s32[1,1,1,2]{3,2,1,0:T(1,128)} %param.21) | copy-start | bytes 28
  146.6 11.1 %collective-permute-start.6 = (f32[1,3,3,3,256]{4,0,3,2,1:T(1,128)S(1)}, f32[1,3,3,3,256]{4,0,3,2,1:T(1,128)S(1)}, u32[]{:S(2)}, u32[]{:S(2)}) collective-permute-start(f32[1,3,3,3,256]{4,0,3,2,1:T(1,128)S(1)} %copy.150), channel_id=1, source_target_pairs={{0,64},{64,128},{128,192},{192,256},{256,320},{320,384},{384,448},... | collective-permute-start | bytes 82952 | tf_op jit(solution)/shard_map/ppermute | solution.py:17
  155.8 11.8 %collective-permute-start.7 = (f32[1,3,3,3,256]{4,0,3,2,1:T(1,128)S(1)}, f32[1,3,3,3,256]{4,0,3,2,1:T(1,128)S(1)}, u32[]{:S(2)}, u32[]{:S(2)}) collective-permute-start(f32[1,3,3,3,256]{4,0,3,2,1:T(1,128)S(1)} %copy.151), channel_id=1, source_target_pairs={{64,0},{128,64},{192,128},{256,192},{320,256},{384,320},{448,384},... | collective-permute-start | bytes 82952 | tf_op jit(solution)/shard_map/ppermute | solution.py:20
  167.7 4.6 %collective-permute-start.9 = (f32[5,1,3,3,256]{4,1,3,2,0:T(1,128)S(1)}, f32[5,1,3,3,256]{4,1,3,2,0:T(1,128)S(1)}, u32[]{:S(2)}, u32[]{:S(2)}) collective-permute-start(f32[5,1,3,3,256]{4,1,3,2,0:T(1,128)S(1)} %copy.136), channel_id=1, source_target_pairs={{4,0},{8,4},{12,8},{16,12},{20,16},{24,20},{28,24},{32,28},{36,32}... | collective-permute-start | bytes 138248 | tf_op jit(solution)/shard_map/ppermute | solution.py:20
  167.8 4.7 %collective-permute-start.8 = (f32[5,1,3,3,256]{4,1,3,2,0:T(1,128)S(1)}, f32[5,1,3,3,256]{4,1,3,2,0:T(1,128)S(1)}, u32[]{:S(2)}, u32[]{:S(2)}) collective-permute-start(f32[5,1,3,3,256]{4,1,3,2,0:T(1,128)S(1)} %copy.135), channel_id=1, source_target_pairs={{0,4},{4,8},{8,12},{12,16},{16,20},{20,24},{24,28},{28,32},{32,36}... | collective-permute-start | bytes 138248 | tf_op jit(solution)/shard_map/ppermute | solution.py:17
  169.0 11.2 %all-to-all-start.1 = ((f32[4,1,1]{2,1,0:T(1,128)}), f32[4,1,1]{2,1,0:T(1,128)S(1)}, u32[]{:S(2)}, u32[]{:S(2)}) async-start(f32[4,1,1]{2,1,0:T(1,128)} %copy.147), calls=%async_computation.1 | async-start | bytes 4096 | tf_op jit(solution)/shard_map/all_to_all | solution.py:148
  172.5 14.1 %copy-start.6 = (f32[1,1,1,3,256]{4,2,3,1,0:T(1,128)S(1)}, f32[1,1,1,3,256]{4,2,3,1,0:T(1,128)}, u32[]{:S(2)}) copy-start(f32[1,1,1,3,256]{4,2,3,1,0:T(1,128)} %param.17) | copy-start | bytes 9220
  172.8 7.7 %collective-permute-start.11 = (f32[5,5,1,3,256]{4,2,3,1,0:T(1,128)S(1)}, f32[5,5,1,3,256]{4,2,3,1,0:T(1,128)S(1)}, u32[]{:S(2)}, u32[]{:S(2)}) collective-permute-start(f32[5,5,1,3,256]{4,2,3,1,0:T(1,128)S(1)} %copy.140), channel_id=1, source_target_pairs={{1,0},{2,1},{3,2},{0,3},{5,4},{6,5},{7,6},{4,7},{9,8},{10,9},{11,1... | collective-permute-start | bytes 230408 | tf_op jit(solution)/shard_map/ppermute | solution.py:20
  178.3 8.1 %collective-permute-start.10 = (f32[5,5,1,3,256]{4,2,3,1,0:T(1,128)S(1)}, f32[5,5,1,3,256]{4,2,3,1,0:T(1,128)S(1)}, u32[]{:S(2)}, u32[]{:S(2)}) collective-permute-start(f32[5,5,1,3,256]{4,2,3,1,0:T(1,128)S(1)} %copy.139), channel_id=1, source_target_pairs={{0,1},{1,2},{2,3},{3,0},{4,5},{5,6},{6,7},{7,4},{8,9},{9,10},{10,1... | collective-permute-start | bytes 230408 | tf_op jit(solution)/shard_map/ppermute | solution.py:17
  187.5 8.9 %all-to-all-start = ((f32[4,9,128]{2,1,0:T(8,128)}), f32[4,9,128]{2,1,0:T(8,128)S(1)}, u32[]{:S(2)}, u32[]{:S(2)}) async-start(f32[4,9,128]{2,1,0:T(8,128)} %copy.146), calls=%async_computation | async-start | bytes 65536 | tf_op jit(solution)/shard_map/all_to_all | solution.py:147
where the time goes:
time: 201 us; the launch traced here: 197 us
  starting transfers between devices  54 us (27%)
  local copies, waits for them, and re-layouts  50.7 us (25%)
  matrix products  38.4 us (19%)
  waiting for transfers between devices  29.6 us (15%)
  other arithmetic  23 us (11%)
    dot_general x20, matrix products, matmul(): return jnp.dot(left, right, precision=lax.Precision.HIGHEST)  33.1 us
    ppermute x6, starting transfers between devices, extended_2(): lax.ppermute(lax.slice_in_dim(block, 0, width, axis=dim), axis, backward)  27.1 us
    ppermute x6, starting transfers between devices, extended_2(): lax.ppermute(lax.slice_in_dim(block, block.shape[dim] - width, None, axis...  20.5 us
    unnamed x4, other arithmetic  19.3 us
    gather x2, local copies, waits for them, and re-layouts, pair_energy(): near_end = extended[13, :, centres].T  15.8 us
    gather x2, local copies, waits for them, and re-layouts, pair_energy(): far_end = extended[slot_index, :, atom_index].T  15.8 us
    ppermute x6, waiting for transfers between devices, extended_2(): lax.ppermute(lax.slice_in_dim(block, block.shape[dim] - width, None, axis...  12.8 us
    ppermute x6, waiting for transfers between devices, extended_2(): lax.ppermute(lax.slice_in_dim(block, 0, width, axis=dim), axis, backward)  11.2 us
  transfers between devices with their start and end apart: 14, of which 7 were waited for; matrix products, arithmetic and copies ran while one was open for 9% of the time, Pallas kernels for 0%

commit v1 on v0

--- a/solution.py
+++ b/solution.py
@@ -8,12 +8,16 @@
 TIME_STEP = 0.2
 
 
+def ring_pairs(axis):
+    count = lax.axis_size(axis)
+    forward = [(i, (i + 1) % count) for i in range(count)]
+    backward = [(target, source) for source, target in forward]
+    return forward, backward
+
+
 def extended_2(block, sides, width):
     for axis, dim in sides:
-        count = lax.axis_size(axis)
-        forward = [(i, i + 1) for i in range(count - 1)]
-        forward.append((count - 1, 0))
-        backward = [(target, source) for source, target in forward]
+        forward, backward = ring_pairs(axis)
         low = lax.ppermute(
             lax.slice_in_dim(block, block.shape[dim] - width, None, axis=dim), axis, forward
         )
@@ -22,8 +26,23 @@
     return block
 
 
+def fold_halo(grad, axes):
+    for axis in axes:
+        forward, backward = ring_pairs(axis)
+        from_low = lax.ppermute(grad[2], axis, forward)
+        from_high = lax.ppermute(grad[0], axis, backward)
+        grad = grad[1] + from_low + from_high
+    return grad
+
+
 def matmul(left, right):
     return jnp.dot(left, right, precision=lax.Precision.HIGHEST)
+
+
+def matmul_t(left, right):
+    return lax.dot_general(
+        left, right, (((1,), (1,)), ((), ())), precision=lax.Precision.HIGHEST
+    )
 
 
 def pair_energy(
@@ -40,7 +59,7 @@
     latent_weight,
     energy_weight,
 ):
-    atoms_here = own_species.shape[0]
+    slots, _, atoms_here = extended.shape
     pair_count = pair_rows.shape[1]
     depth = atoms_here // 64
     centres = pair_rows[0]
@@ -52,8 +71,13 @@
     offset_y = (slot_index // 3 % 3 - 1).astype(jnp.float32) * 8.0
     offset_z = (slot_index % 3 - 1).astype(jnp.float32) * float(depth)
     shifts = jnp.stack([offset_x, offset_y, offset_z])
-    far_end = extended[slot_index, :, atom_index].T
-    near_end = extended[13, :, centres].T
+    atoms = jnp.arange(atoms_here)
+    atom_hot = (atoms[:, None] == atom_index[None]).astype(jnp.float32)
+    slot_hot = (jnp.arange(slots)[:, None] == slot_index[None]).astype(jnp.float32)
+    member = (centres[:, None] == atoms[None]).astype(jnp.float32)
+    by_atom = matmul(extended.reshape(slots * 3, atoms_here), atom_hot)
+    far_end = jnp.sum(by_atom.reshape(slots, 3, pair_count) * slot_hot[:, None, :], axis=0)
+    near_end = matmul_t(extended[13], member)
     displace = far_end + shifts - near_end
     distance = jnp.sqrt(jnp.sum(displace * displace, axis=0))
     unit = displace / distance
@@ -67,7 +91,8 @@
     in_use = (jnp.arange(pair_count) < live_count * 128).astype(jnp.float32)
     envelope = (1.0 - ratio * ratio) ** 2 * in_use
     kinds = jnp.arange(center_embed.shape[1])[:, None]
-    centre_hot = (kinds == own_species[centres][None]).astype(jnp.float32)
+    species_hot = (kinds == own_species[None]).astype(jnp.float32)
+    centre_hot = matmul_t(species_hot, member)
     other_hot = (kinds == other_species[None]).astype(jnp.float32)
     latent = envelope[None] * jax.nn.silu(
         matmul(radial_weight, basis)
@@ -76,15 +101,12 @@
     )
     channels = vector_weight.shape[0]
     vectors = envelope[None, None] * matmul(vector_weight, basis)[None] * unit[:, None, :]
-    member = (centres[:, None] == jnp.arange(atoms_here)[None]).astype(jnp.float32)
     n_layers = env_weight.shape[0]
     for layer in range(n_layers):
         env_pairs = matmul(env_weight[layer], latent)
         spread = (unit[:, None, :] * env_pairs[None]).reshape(3 * channels, pair_count)
         environment = ENV_SCALE * matmul(spread, member)
-        at_pairs = lax.dot_general(
-            environment, member, (((1,), (1,)), ((), ())), precision=lax.Precision.HIGHEST
-        )
+        at_pairs = matmul_t(environment, member)
         at_pairs = at_pairs.reshape(3, channels, pair_count)
         scalars = jnp.sum(vectors * at_pairs, axis=0)
         update = matmul(latent_weight[layer], jnp.concatenate([latent, scalars], axis=0))
@@ -131,9 +153,7 @@
         energy_weight,
     )
     grad = grad.reshape(3, 3, 3, 3, atoms_here)
-    rim = extended_2(grad, (("gx", 0), ("gy", 1), ("gz", 2)), 1)
-    total = jnp.sum(rim[0::2, 0::2, 0::2], axis=(0, 1, 2))
-    forces = -total
+    forces = -fold_halo(grad, ("gx", "gy", "gz"))
     inverse_mass = 1.0 / (1.0 + own_species.astype(jnp.float32))
     new_vel = velocities[0, 0, 0] + TIME_STEP * forces * inverse_mass[None]
     new_pos = positions[0, 0, 0] + TIME_STEP * new_vel
@@ -142,15 +162,12 @@
     blocks = state.reshape(9, blocks_count, 128).transpose(1, 0, 2)
     hits = (owners[0, 0, 0][:, None] == jnp.arange(zcount)[None]).astype(jnp.float32)
     outgoing = jnp.einsum("bd,bcq->dcq", hits, blocks, precision=lax.Precision.HIGHEST)
-    flags = jnp.sum(hits, axis=0)[:, None]
-    arrived, arrived_flags = (
-        lax.all_to_all(outgoing, "gz", split_axis=0, concat_axis=0, tiled=True),
-        lax.all_to_all(flags, "gz", split_axis=0, concat_axis=0, tiled=True),
-    )
+    sent = jnp.sum(hits, axis=0)
     myself = lax.axis_index("gz")
-    source = jnp.arange(zcount, dtype=jnp.int32)
-    rise = arrived_flags[:, 0] * (source - myself).astype(jnp.float32) * float(depth)
-    arrived = arrived.at[:, 2, :].add(rise[:, None])
+    target = jnp.arange(zcount, dtype=jnp.int32)
+    rise = sent * (myself - target).astype(jnp.float32) * float(depth)
+    outgoing = outgoing.at[:, 2, :].add(rise[:, None])
+    arrived = lax.all_to_all(outgoing, "gz", split_axis=0, concat_axis=0, tiled=True)
     return arrived[None, None, None]
 
 

time: 201 us -> 124 us (0.62); the launches traced: 197 us -> 124 us
  local copies, waits for them, and re-layouts: 50.7 us -> 2.11 us
  other arithmetic: 23 us -> 2.56 us
  blocking collectives: 0 us -> 10.8 us
  waiting for transfers between devices: 29.6 us -> 21.2 us
  starting transfers between devices: 54 us -> 45.8 us
    gather x5 -> x0, local copies, waits for them, and re-layouts: 41 us -> none  [the longest x2 15.8 us: pair_energy(): near_end = extended[13, :, centres].T]
    unnamed x4 -> x0, other arithmetic: 19.3 us -> none
    ppermute x0 -> x6, starting transfers between devices: none -> 16.8 us  [the longest x3 10.6 us: fold_halo(): from_high = lax.ppermute(grad[0], axis, backward)]
    ppermute x0 -> x6, waiting for transfers between devices: none -> 12.8 us  [the longest x3 11.5 us: fold_halo(): from_high = lax.ppermute(grad[0], axis, backward)]
    ppermute x6 -> x3, starting transfers between devices: 20.5 us -> 8.43 us  [extended_2(): lax.ppermute(lax.slice_in_dim(block, block.shape[dim] - width, None, axis...]
    ppermute x6 -> x3, waiting for transfers between devices: 12.8 us -> 0.93 us  [extended_2(): lax.ppermute(lax.slice_in_dim(block, block.shape[dim] - width, None, axis...]
    all_to_all x0 -> x1, blocking collectives: none -> 10.8 us  [per_device(): lax.all_to_all(outgoing, 'gz', split_axis=0, concat_axis=0, tiled=True)]
    ppermute x6 -> x3, starting transfers between devices: 27.1 us -> 20.5 us  [extended_2(): lax.ppermute(lax.slice_in_dim(block, 0, width, axis=dim), axis, backward)]
  transfers between devices with their start and end apart: 14 -> 12, of which waited for: 7 -> 6; matrix products, arithmetic and copies ran while one was open for 9% -> 3% of each run, Pallas kernels for 0% -> 0%
where the time goes in v1:
time: 124 us
  starting transfers between devices  45.8 us (37%)
  matrix products  39.9 us (32%)
  waiting for transfers between devices  21.2 us (17%)
  blocking collectives  10.8 us (9%)
  other arithmetic  2.56 us (2%)
  local copies, waits for them, and re-layouts  2.11 us (2%)
  between operations  1.3 us (1%)
    dot_general x22, matrix products, matmul(): return jnp.dot(left, right, precision=lax.Precision.HIGHEST)  32.8 us
    ppermute x3, starting transfers between devices, extended_2(): lax.ppermute(lax.slice_in_dim(block, 0, width, axis=dim), axis, backward)  20.5 us
    ppermute x3, waiting for transfers between devices, fold_halo(): from_high = lax.ppermute(grad[0], axis, backward)  11.5 us
    all_to_all x1, blocking collectives, per_device(): lax.all_to_all(outgoing, 'gz', split_axis=0, concat_axis=0, tiled=True)  10.8 us
    ppermute x3, starting transfers between devices, fold_halo(): from_high = lax.ppermute(grad[0], axis, backward)  10.6 us
    ppermute x3, starting transfers between devices, extended_2(): lax.ppermute(lax.slice_in_dim(block, block.shape[dim] - width, None, axis...  8.43 us
    ppermute x3, waiting for transfers between devices, extended_2(): lax.ppermute(lax.slice_in_dim(block, 0, width, axis=dim), axis, backward)  7.42 us
    dot_general x7, matrix products, matmul_t(): lax.dot_general(left, right, (((1,), (1,)), ((), ())), precision=lax.Prec...  6.79 us
  transfers between devices with their start and end apart: 12, of which 6 were waited for; matrix products, arithmetic and copies ran while one was open for 3% of the time, Pallas kernels for 0%

profile of v1, /device:TPU:112, one launch (start us, length us, event | category | flops | bytes accessed | tf_op | source)
XLA Modules:
  0.0 123.6 jit_solution(1002559258797208673)
XLA Ops:
  0.0 5.9 %collective-permute-start = (f32[1,1,1,3,256]{4,2,3,1,0:T(1,128)}, f32[1,1,1,3,256]{4,2,3,1,0:T(1,128)S(1)}, u32[]{:S(2)}, u32[]{:S(2)}) collective-permute-start(f32[1,1,1,3,256]{4,2,3,1,0:T(1,128)} %param.16), channel_id=1, source_target_pairs={{0,64},{64,128},{128,192},{192,256},{256,320},{320,384},{384,448},... | collective-permute-start | bytes 9224 | tf_op jit(solution)/shard_map/ppermute | solution.py:21
  5.9 1.9 %collective-permute-start.1 = (f32[1,1,1,3,256]{4,2,3,1,0:T(1,128)}, f32[1,1,1,3,256]{4,2,3,1,0:T(1,128)S(1)}, u32[]{:S(2)}, u32[]{:S(2)}) collective-permute-start(f32[1,1,1,3,256]{4,2,3,1,0:T(1,128)} %param.16), channel_id=1, source_target_pairs={{64,0},{128,64},{192,128},{256,192},{320,256},{384,320},{448,384},... | collective-permute-start | bytes 9224 | tf_op jit(solution)/shard_map/ppermute | solution.py:24
  9.6 1.5 %fusion.113 = f32[1536,256]{0,1:T(8,128)S(1)} fusion(f32[256,4]{0,1:T(4,128)} %param.24, s32[1536]{0:T(1024)S(1)} %get-tuple-element.26), kind=kOutput, calls=%fused_computation.169 | convolution fusion | flops 18880512 | bytes 1583104 | tf_op jit(solution)/shard_map/jvp()/dot_general | solution.py:39
  11.1 6.5 %collective-permute-done.1 = f32[1,1,1,3,256]{4,2,3,1,0:T(1,128)S(1)} collective-permute-done((f32[1,1,1,3,256]{4,2,3,1,0:T(1,128)}, f32[1,1,1,3,256]{4,2,3,1,0:T(1,128)S(1)}, u32[]{:S(2)}, u32[]{:S(2)}) %collective-permute-start.1) | collective-permute-done | bytes 3104 | tf_op jit(solution)/shard_map/ppermute | solution.py:24
  17.7 13.4 %collective-permute-start.3 = (f32[3,1,1,3,256]{4,2,3,1,0:T(1,128)S(1)}, f32[3,1,1,3,256]{4,2,3,1,0:T(1,128)S(1)}, u32[]{:S(2)}, u32[]{:S(2)}) collective-permute-start(f32[3,1,1,3,256]{4,2,3,1,0:T(1,128)S(1)} %constant_dynamic-update-slice_fusion), channel_id=1, source_target_pairs={{4,0},{8,4},{12,8},{16,12},{20,16},{24,20},{28,24},{32,28},{36,32}... | collective-permute-start | bytes 27656 | tf_op jit(solution)/shard_map/ppermute | solution.py:24
  32.5 2.5 %collective-permute-start.4 = (f32[3,3,1,3,256]{4,2,3,1,0:T(1,128)S(1)}, f32[3,3,1,3,256]{4,2,3,1,0:T(1,128)S(1)}, u32[]{:S(2)}, u32[]{:S(2)}) collective-permute-start(f32[3,3,1,3,256]{4,2,3,1,0:T(1,128)S(1)} %pad_maximum_fusion.1), channel_id=1, source_target_pairs={{0,1},{1,2},{2,3},{3,0},{4,5},{5,6},{6,7},{7,4},{8,9},{9,10},{10,1... | collective-permute-start | bytes 82952 | tf_op jit(solution)/shard_map/ppermute | solution.py:21
  35.0 5.1 %collective-permute-start.5 = (f32[3,3,1,3,256]{4,2,3,1,0:T(1,128)S(1)}, f32[3,3,1,3,256]{4,2,3,1,0:T(1,128)S(1)}, u32[]{:S(2)}, u32[]{:S(2)}) collective-permute-start(f32[3,3,1,3,256]{4,2,3,1,0:T(1,128)S(1)} %pad_maximum_fusion.1), channel_id=1, source_target_pairs={{1,0},{2,1},{3,2},{0,3},{5,4},{6,5},{7,6},{4,7},{9,8},{10,9},{11,1... | collective-permute-start | bytes 82952 | tf_op jit(solution)/shard_map/ppermute | solution.py:24
  43.5 1.5 %fusion.93 = f32[1536,256]{0,1:T(8,128)S(1)} fusion(f32[256,8]{0,1:T(8,128)S(1)} %copy-done.4, f32[1536]{0:T(1024)S(1)} %get-tuple-element.48, f32[8]{0:T(128)S(1)} %get-tuple-element.68), kind=kOutput, calls=%fused_computation.145 | convolution fusion | flops 37797888 | bytes 1587232 | tf_op jit(solution)/shard_map/jvp()/dot_general | solution.py:39
  45.1 1.9 %broadcast_multiply_fusion = (f32[256,1536]{1,0:T(8,128)S(1)}, f32[256,1536]{1,0:T(8,128)S(1)}) fusion(f32[1536]{0:T(1024)S(1)} %get-tuple-element.47, f32[1536,256]{0,1:T(8,128)S(1)} %fusion.113, f32[1536,256]{0,1:T(8,128)S(1)} %fusion.93, f32[4,1536]{1,0:T(4,128)S(1)} %fusion.39, f32[256,4]{0,1:T(4,128)S(1)} %copy-done.8), kind=kOutput, calls=%fused_computation.85 | convolution fusion | flops 21626880 | bytes 6326272 | tf_op jit(solution)/shard_map/jvp()/dot_general | solution.py:39
  47.0 1.0 convolution_bitcast_fusion.9
  48.8 1.7 %fusion.37 = f32[96,1536]{1,0:T(8,128)S(1)} fusion(f32[96,256]{1,0:T(8,128)S(1)} %fusion.47, s32[1536]{0:T(1024)S(1)} %get-tuple-element.28), kind=kOutput, calls=%fused_computation.62 | convolution fusion | flops 453378048 | bytes 694272 | tf_op jit(solution)/shard_map/jvp()/dot_general | solution.py:43
  51.2 3.1 %multiply_add_fusion = (f32[256,1536]{1,0:T(8,128)S(1)}, f32[256,1536]{1,0:T(8,128)S(1)}) fusion(f32[256,1536]{1,0:T(8,128)S(1)} %get-tuple-element.55, f32[1536]{0:T(1024)S(1)} %get-tuple-element.47, f32[2,256,288]{1,2,0:T(8,128)S(1)} %copy-done.7, f32[32,1536]{1,0:T(8,128)S(1)} %multiply_reduce_fusion.11), kind=kOutput, calls=%fused_computation.49 | convolution fusion | flops 1361756160 | bytes 6791168 | tf_op jit(solution)/shard_map/jvp()/dot_general | solution.py:39
  56.1 1.7 %fusion.35 = f32[96,1536]{1,0:T(8,128)S(1)} fusion(f32[96,256]{1,0:T(8,128)S(1)} %fusion.48, s32[1536]{0:T(1024)S(1)} %get-tuple-element.28), kind=kOutput, calls=%fused_computation.60 | convolution fusion | flops 453378048 | bytes 694272 | tf_op jit(solution)/shard_map/jvp()/dot_general | solution.py:43
  57.8 1.0 convolution_bitcast_fusion.8
  59.6 3.1 %multiply_reduce_fusion.2 = (f32[1536]{0:T(1024)S(1)}, f32[256,1536]{1,0:T(8,128)S(1)}) fusion(f32[256]{0:T(256)S(1)} %copy-done.9, f32[2,256,288]{1,2,0:T(8,128)S(1)} %copy-done.7, f32[32,1536]{1,0:T(8,128)S(1)} %get-tuple-element.34, f32[256,1536]{1,0:T(8,128)S(1)} %get-tuple-element.59), kind=kOutput, calls=%fused_computation.44 | convolution fusion | flops 1361754624 | bytes 3644416 | tf_op jit(solution)/shard_map/jvp()/dot_general | solution.py:39
  62.6 2.3 %convolution_bitcast_fusion.1 = f32[288,1536]{1,0:T(8,128)S(1)} fusion(f32[256,1536]{1,0:T(8,128)S(1)} %get-tuple-element.64, f32[256]{0:T(256)S(1)} %copy-done.9, f32[1536]{0:T(1024)S(1)} %get-tuple-element.47, f32[2,256,288]{1,2,0:T(8,128)S(1)} %copy-done.7), kind=kOutput, calls=%fused_computation.3 | convolution fusion | flops 1362886656 | bytes 3646464 | tf_op jit(solution)/shard_map/transpose(jvp())/dot_general | solution.py:39
  65.8 1.7 %fusion.33 = f32[96,1536]{1,0:T(8,128)S(1)} fusion(f32[96,256]{1,0:T(8,128)S(1)} %fusion.49, s32[1536]{0:T(1024)S(1)} %get-tuple-element.28), kind=kOutput, calls=%fused_computation.58 | convolution fusion | flops 453378048 | bytes 694272 | tf_op jit(solution)/shard_map/transpose(jvp())/dot_general | solution.py:39
  67.7 1.9 %multiply_reduce_fusion.1 = (f32[1536]{0:T(1024)S(1)}, f32[256,1536]{1,0:T(8,128)S(1)}) fusion(f32[256,1536]{1,0:T(8,128)S(1)} %get-tuple-element.60, f32[32,1536]{1,0:T(8,128)S(1)} %get-tuple-element.23, f32[2,32,256]{2,1,0:T(8,128)S(1)} %copy-done.1, f32[288,1536]{1,0:T(8,128)S(1)} %convolution_bitcast_fusion.1, f32[256]{0:T(256)S(1)} %copy-done.9), kind=kOutput, calls=%fused_computation.43 | convolution fusion | flops 154139136 | bytes 4955136 | tf_op jit(solution)/shard_map/transpose(jvp())/dot_general | solution.py:39
  69.6 2.3 %convolution_bitcast_fusion = f32[288,1536]{1,0:T(8,128)S(1)} fusion(f32[256,1536]{1,0:T(8,128)S(1)} %get-tuple-element.60, f32[256,1536]{1,0:T(8,128)S(1)} %get-tuple-element.66, f32[1536]{0:T(1024)S(1)} %get-tuple-element.47, f32[2,256,288]{1,2,0:T(8,128)S(1)} %copy-done.7), kind=kOutput, calls=%fused_computation.2 | convolution fusion | flops 1362886656 | bytes 5218304 | tf_op jit(solution)/shard_map/transpose(jvp())/dot_general | solution.py:39
  72.8 1.5 %fusion.31 = f32[96,1536]{1,0:T(8,128)S(1)} fusion(f32[96,256]{1,0:T(8,128)S(1)} %fusion.50, s32[1536]{0:T(1024)S(1)} %get-tuple-element.28), kind=kOutput, calls=%fused_computation.56 | convolution fusion | flops 453378048 | bytes 694272 | tf_op jit(solution)/shard_map/transpose(jvp())/dot_general | solution.py:39
  74.8 1.6 %fusion.4 = f32[256,1536]{1,0:T(8,128)S(1)} fusion(f32[256,1536]{1,0:T(8,128)S(1)} %get-tuple-element.66, f32[32,1536]{1,0:T(8,128)S(1)} %get-tuple-element.41, f32[32,256]{1,0:T(8,128)S(1)} %copy-done, f32[288,1536]{1,0:T(8,128)S(1)} %convolution_bitcast_fusion), kind=kOutput, calls=%fused_computation.9 | convolution fusion | flops 151781376 | bytes 4947968 | tf_op jit(solution)/shard_map/transpose(jvp())/dot_general | solution.py:39
  76.6 1.8 %multiply_reduce_fusion = (f32[1536]{0:T(1024)S(1)}, f32[256,1536]{1,0:T(8,128)S(1)}) fusion(f32[256,1536]{1,0:T(8,128)S(1)} %get-tuple-element.56, f32[256,1536]{1,0:T(8,128)S(1)} %fusion.4, f32[32,1536]{1,0:T(8,128)S(1)} %get-tuple-element.21, f32[2,32,256]{2,1,0:T(8,128)S(1)} %copy-done.1), kind=kOutput, calls=%fused_computation.42 | convolution fusion | flops 153745920 | bytes 4954112 | tf_op jit(solution)/shard_map/transpose(jvp())/dot_general | solution.py:39
  78.5 1.6 %fusion.91 = (f32[1536]{0:T(1024)S(1)}, f32[1536]{0:T(1024)S(1)}) fusion(f32[1536]{0:T(1024)S(1)} %get-tuple-element.46, f32[1536]{0:T(1024)S(1)} %get-tuple-element.48, f32[8]{0:T(128)S(1)} %get-tuple-element.68, f32[8]{0:T(128)S(1)} %get-tuple-element.67, f32[1536,8]{0,1:T(8,128)S(1)} %fusion.85, f32[256,8]{0,1:T(8,128)S(1)} %copy-done.4, ...), kind=kOutput, calls=%fused_computation.139 | convolution fusion | flops 41825280 | bytes 3233856 | tf_op jit(solution)/shard_map/transpose(jvp())/dot_general | solution.py:39
  81.9 4.3 %collective-permute-start.6 = (f32[3,3,3,256]{3,2,1,0:T(4,128)S(1)}, f32[3,3,3,256]{3,2,1,0:T(4,128)S(1)}, u32[]{:S(2)}, u32[]{:S(2)}) collective-permute-start(f32[3,3,3,256]{3,2,1,0:T(4,128)S(1)} %bitcast.198), channel_id=1, source_target_pairs={{0,64},{64,128},{128,192},{192,256},{256,320},{320,384},{384,448},... | collective-permute-start | bytes 82952 | tf_op jit(solution)/shard_map/ppermute | solution.py:32
  86.2 1.9 %collective-permute-start.7 = (f32[3,3,3,256]{3,2,1,0:T(4,128)S(1)}, f32[3,3,3,256]{3,2,1,0:T(4,128)S(1)}, u32[]{:S(2)}, u32[]{:S(2)}) collective-permute-start(f32[3,3,3,256]{3,2,1,0:T(4,128)S(1)} %bitcast.197), channel_id=1, source_target_pairs={{64,0},{128,64},{192,128},{256,192},{320,256},{384,320},{448,384},... | collective-permute-start | bytes 82952 | tf_op jit(solution)/shard_map/ppermute | solution.py:33
  88.2 10.2 %collective-permute-done.7 = f32[3,3,3,256]{3,2,1,0:T(4,128)S(1)} collective-permute-done((f32[3,3,3,256]{3,2,1,0:T(4,128)S(1)}, f32[3,3,3,256]{3,2,1,0:T(4,128)S(1)}, u32[]{:S(2)}, u32[]{:S(2)}) %collective-permute-start.7) | collective-permute-done | bytes 27680 | tf_op jit(solution)/shard_map/ppermute | solution.py:33
  98.4 2.9 %collective-permute-start.9 = (f32[3,3,256]{2,1,0:T(4,128)S(1)}, f32[3,3,256]{2,1,0:T(4,128)S(1)}, u32[]{:S(2)}, u32[]{:S(2)}) collective-permute-start(f32[3,3,256]{2,1,0:T(4,128)S(1)} %get-tuple-element.40), channel_id=1, source_target_pairs={{4,0},{8,4},{12,8},{16,12},{20,16},{24,20},{28,24},{32,28},{36,32}... | collective-permute-start | bytes 27656 | tf_op jit(solution)/shard_map/ppermute | solution.py:33
  101.5 1.3 %collective-permute-done.8 = f32[3,3,256]{2,1,0:T(4,128)S(1)} collective-permute-done((f32[3,3,256]{2,1,0:T(4,128)S(1)}, f32[3,3,256]{2,1,0:T(4,128)S(1)}, u32[]{:S(2)}, u32[]{:S(2)}) %collective-permute-start.8) | collective-permute-done | bytes 9248 | tf_op jit(solution)/shard_map/ppermute | solution.py:32
  102.8 1.9 %collective-permute-start.10 = (f32[3,256]{1,0:T(4,128)S(1)}, f32[3,256]{1,0:T(4,128)S(1)}, u32[]{:S(2)}, u32[]{:S(2)}) collective-permute-start(f32[3,256]{1,0:T(4,128)S(1)} %get-tuple-element.44), channel_id=1, source_target_pairs={{0,1},{1,2},{2,3},{3,0},{4,5},{5,6},{6,7},{7,4},{8,9},{9,10},{10,1... | collective-permute-start | bytes 9224 | tf_op jit(solution)/shard_map/ppermute | solution.py:32
  104.7 5.7 %collective-permute-start.11 = (f32[3,256]{1,0:T(4,128)S(1)}, f32[3,256]{1,0:T(4,128)S(1)}, u32[]{:S(2)}, u32[]{:S(2)}) collective-permute-start(f32[3,256]{1,0:T(4,128)S(1)} %get-tuple-element.45), channel_id=1, source_target_pairs={{1,0},{2,1},{3,2},{0,3},{5,4},{6,5},{7,6},{4,7},{9,8},{10,9},{11,1... | collective-permute-start | bytes 9224 | tf_op jit(solution)/shard_map/ppermute | solution.py:33
  110.5 1.3 %collective-permute-done.11 = f32[3,256]{1,0:T(4,128)S(1)} collective-permute-done((f32[3,256]{1,0:T(4,128)S(1)}, f32[3,256]{1,0:T(4,128)S(1)}, u32[]{:S(2)}, u32[]{:S(2)}) %collective-permute-start.11) | collective-permute-done | bytes 3104 | tf_op jit(solution)/shard_map/ppermute | solution.py:33
  112.2 10.8 %all_to_all.5 = f32[4,9,128]{2,1,0:T(8,128)S(1)} all-to-all(f32[4,9,128]{2,1,0:T(8,128)S(1)} %copy.19), channel_id=1, replica_groups=mesh['gx'=16,'gy'=16,'gz'=4] {'gz'}, dimensions={0} | all-to-all | bytes 36864 | tf_op jit(solution)/shard_map/all_to_all | solution.py:170
  (90 shorter events, 15.3 us)
Async XLA Ops:
  0.0 57.8 %copy-start = (f32[32,256]{1,0:T(8,128)S(1)}, f32[32,256]{1,0:T(8,128)}, u32[]{:S(2)}) copy-start(f32[32,256]{1,0:T(8,128)} %param.27) | copy-start | bytes 98308
  0.0 11.1 %copy-start.3 = (f32[1,1,1,3,256]{4,2,3,1,0:T(1,128)S(1)}, f32[1,1,1,3,256]{4,2,3,1,0:T(1,128)}, u32[]{:S(2)}) copy-start(f32[1,1,1,3,256]{4,2,3,1,0:T(1,128)} %param.16) | copy-start | bytes 9220
  0.0 31.1 %copy-start.6 = (s32[1,1,1,256]{3,2,1,0:T(1,128)S(1)}, s32[1,1,1,256]{3,2,1,0:T(1,128)}, u32[]{:S(2)}) copy-start(s32[1,1,1,256]{3,2,1,0:T(1,128)} %param.18) | copy-start | bytes 3076
  0.0 11.1 %collective-permute-start = (f32[1,1,1,3,256]{4,2,3,1,0:T(1,128)}, f32[1,1,1,3,256]{4,2,3,1,0:T(1,128)S(1)}, u32[]{:S(2)}, u32[]{:S(2)}) collective-permute-start(f32[1,1,1,3,256]{4,2,3,1,0:T(1,128)} %param.16), channel_id=1, source_target_pairs={{0,64},{64,128},{128,192},{192,256},{256,320},{320,384},{384,448},... | collective-permute-start | bytes 9224 | tf_op jit(solution)/shard_map/ppermute | solution.py:21
  5.9 11.7 %collective-permute-start.1 = (f32[1,1,1,3,256]{4,2,3,1,0:T(1,128)}, f32[1,1,1,3,256]{4,2,3,1,0:T(1,128)S(1)}, u32[]{:S(2)}, u32[]{:S(2)}) collective-permute-start(f32[1,1,1,3,256]{4,2,3,1,0:T(1,128)} %param.16), channel_id=1, source_target_pairs={{64,0},{128,64},{192,128},{256,192},{320,256},{384,320},{448,384},... | collective-permute-start | bytes 9224 | tf_op jit(solution)/shard_map/ppermute | solution.py:24
  11.1 32.4 %copy-start.4 = (f32[256,8]{0,1:T(8,128)S(1)}, f32[256,8]{0,1:T(8,128)}, u32[]{:S(2)}) copy-start(f32[256,8]{0,1:T(8,128)} %param.22) | copy-start | bytes 24580
  17.7 14.8 %collective-permute-start.2 = (f32[3,1,1,3,256]{4,2,3,1,0:T(1,128)S(1)}, f32[3,1,1,3,256]{4,2,3,1,0:T(1,128)S(1)}, u32[]{:S(2)}, u32[]{:S(2)}) collective-permute-start(f32[3,1,1,3,256]{4,2,3,1,0:T(1,128)S(1)} %constant_dynamic-update-slice_fusion), channel_id=1, source_target_pairs={{0,4},{4,8},{8,12},{12,16},{16,20},{20,24},{24,28},{28,32},{32,36}... | collective-permute-start | bytes 27656 | tf_op jit(solution)/shard_map/ppermute | solution.py:21
  17.7 14.8 %collective-permute-start.3 = (f32[3,1,1,3,256]{4,2,3,1,0:T(1,128)S(1)}, f32[3,1,1,3,256]{4,2,3,1,0:T(1,128)S(1)}, u32[]{:S(2)}, u32[]{:S(2)}) collective-permute-start(f32[3,1,1,3,256]{4,2,3,1,0:T(1,128)S(1)} %constant_dynamic-update-slice_fusion), channel_id=1, source_target_pairs={{4,0},{8,4},{12,8},{16,12},{20,16},{24,20},{28,24},{32,28},{36,32}... | collective-permute-start | bytes 27656 | tf_op jit(solution)/shard_map/ppermute | solution.py:24
  32.5 8.3 %collective-permute-start.4 = (f32[3,3,1,3,256]{4,2,3,1,0:T(1,128)S(1)}, f32[3,3,1,3,256]{4,2,3,1,0:T(1,128)S(1)}, u32[]{:S(2)}, u32[]{:S(2)}) collective-permute-start(f32[3,3,1,3,256]{4,2,3,1,0:T(1,128)S(1)} %pad_maximum_fusion.1), channel_id=1, source_target_pairs={{0,1},{1,2},{2,3},{3,0},{4,5},{5,6},{6,7},{7,4},{8,9},{9,10},{10,1... | collective-permute-start | bytes 82952 | tf_op jit(solution)/shard_map/ppermute | solution.py:21
  35.0 6.7 %collective-permute-start.5 = (f32[3,3,1,3,256]{4,2,3,1,0:T(1,128)S(1)}, f32[3,3,1,3,256]{4,2,3,1,0:T(1,128)S(1)}, u32[]{:S(2)}, u32[]{:S(2)}) collective-permute-start(f32[3,3,1,3,256]{4,2,3,1,0:T(1,128)S(1)} %pad_maximum_fusion.1), channel_id=1, source_target_pairs={{1,0},{2,1},{3,2},{0,3},{5,4},{6,5},{7,6},{4,7},{9,8},{10,9},{11,1... | collective-permute-start | bytes 82952 | tf_op jit(solution)/shard_map/ppermute | solution.py:24
  41.8 3.3 %copy-start.8 = (f32[256,4]{0,1:T(4,128)S(1)}, f32[256,4]{0,1:T(4,128)}, u32[]{:S(2)}) copy-start(f32[256,4]{0,1:T(4,128)} %param.23) | copy-start | bytes 12292
  45.1 1.9 %copy-start.1 = (f32[2,32,256]{2,1,0:T(8,128)S(1)}, f32[2,32,256]{2,1,0:T(8,128)}, u32[]{:S(2)}) copy-start(f32[2,32,256]{2,1,0:T(8,128)} %param.26) | copy-start | bytes 196612
  46.9 3.6 %copy-start.2 = (f32[32,8]{0,1:T(8,128)S(1)}, f32[32,8]{0,1:T(8,128)}, u32[]{:S(2)}) copy-start(f32[32,8]{0,1:T(8,128)} %param.25) | copy-start | bytes 3076
  48.1 3.1 %copy-start.7 = (f32[2,256,288]{1,2,0:T(8,128)S(1)}, f32[2,256,288]{1,2,0:T(8,128)}, u32[]{:S(2)}) copy-start(f32[2,256,288]{1,2,0:T(8,128)} %param.28) | copy-start | bytes 1769476
  58.9 0.7 copy-start.9
  80.1 21.3 %copy-start.10 = (s32[1,1,1,2]{3,2,1,0:T(1,128)S(1)}, s32[1,1,1,2]{3,2,1,0:T(1,128)}, u32[]{:S(2)}) copy-start(s32[1,1,1,2]{3,2,1,0:T(1,128)} %param.21) | copy-start | bytes 28
  80.1 31.7 %copy-start.5 = (f32[1,1,1,3,256]{4,2,3,1,0:T(1,128)S(1)}, f32[1,1,1,3,256]{4,2,3,1,0:T(1,128)}, u32[]{:S(2)}) copy-start(f32[1,1,1,3,256]{4,2,3,1,0:T(1,128)} %param.17) | copy-start | bytes 9220
  81.9 6.3 %collective-permute-start.6 = (f32[3,3,3,256]{3,2,1,0:T(4,128)S(1)}, f32[3,3,3,256]{3,2,1,0:T(4,128)S(1)}, u32[]{:S(2)}, u32[]{:S(2)}) collective-permute-start(f32[3,3,3,256]{3,2,1,0:T(4,128)S(1)} %bitcast.198), channel_id=1, source_target_pairs={{0,64},{64,128},{128,192},{192,256},{256,320},{320,384},{384,448},... | collective-permute-start | bytes 82952 | tf_op jit(solution)/shard_map/ppermute | solution.py:32
  86.2 12.2 %collective-permute-start.7 = (f32[3,3,3,256]{3,2,1,0:T(4,128)S(1)}, f32[3,3,3,256]{3,2,1,0:T(4,128)S(1)}, u32[]{:S(2)}, u32[]{:S(2)}) collective-permute-start(f32[3,3,3,256]{3,2,1,0:T(4,128)S(1)} %bitcast.197), channel_id=1, source_target_pairs={{64,0},{128,64},{192,128},{256,192},{320,256},{384,320},{448,384},... | collective-permute-start | bytes 82952 | tf_op jit(solution)/shard_map/ppermute | solution.py:33
  98.4 4.3 %collective-permute-start.8 = (f32[3,3,256]{2,1,0:T(4,128)S(1)}, f32[3,3,256]{2,1,0:T(4,128)S(1)}, u32[]{:S(2)}, u32[]{:S(2)}) collective-permute-start(f32[3,3,256]{2,1,0:T(4,128)S(1)} %get-tuple-element.39), channel_id=1, source_target_pairs={{0,4},{4,8},{8,12},{12,16},{16,20},{20,24},{24,28},{28,32},{32,36}... | collective-permute-start | bytes 27656 | tf_op jit(solution)/shard_map/ppermute | solution.py:32
  98.4 4.3 %collective-permute-start.9 = (f32[3,3,256]{2,1,0:T(4,128)S(1)}, f32[3,3,256]{2,1,0:T(4,128)S(1)}, u32[]{:S(2)}, u32[]{:S(2)}) collective-permute-start(f32[3,3,256]{2,1,0:T(4,128)S(1)} %get-tuple-element.40), channel_id=1, source_target_pairs={{4,0},{8,4},{12,8},{16,12},{20,16},{24,20},{28,24},{32,28},{36,32}... | collective-permute-start | bytes 27656 | tf_op jit(solution)/shard_map/ppermute | solution.py:33
  102.8 7.7 %collective-permute-start.10 = (f32[3,256]{1,0:T(4,128)S(1)}, f32[3,256]{1,0:T(4,128)S(1)}, u32[]{:S(2)}, u32[]{:S(2)}) collective-permute-start(f32[3,256]{1,0:T(4,128)S(1)} %get-tuple-element.44), channel_id=1, source_target_pairs={{0,1},{1,2},{2,3},{3,0},{4,5},{5,6},{6,7},{7,4},{8,9},{9,10},{10,1... | collective-permute-start | bytes 9224 | tf_op jit(solution)/shard_map/ppermute | solution.py:32
  104.7 7.0 %collective-permute-start.11 = (f32[3,256]{1,0:T(4,128)S(1)}, f32[3,256]{1,0:T(4,128)S(1)}, u32[]{:S(2)}, u32[]{:S(2)}) collective-permute-start(f32[3,256]{1,0:T(4,128)S(1)} %get-tuple-element.45), channel_id=1, source_target_pairs={{1,0},{2,1},{3,2},{0,3},{5,4},{6,5},{7,6},{4,7},{9,8},{10,9},{11,1... | collective-permute-start | bytes 9224 | tf_op jit(solution)/shard_map/ppermute | solution.py:33

commit v2 on v1

--- a/solution.py
+++ b/solution.py
@@ -35,14 +35,12 @@
     return grad
 
 
-def matmul(left, right):
-    return jnp.dot(left, right, precision=lax.Precision.HIGHEST)
+def matmul(left, right, precision=lax.Precision.HIGH):
+    return jnp.dot(left, right, precision=precision)
 
 
-def matmul_t(left, right):
-    return lax.dot_general(
-        left, right, (((1,), (1,)), ((), ())), precision=lax.Precision.HIGHEST
-    )
+def matmul_t(left, right, precision=lax.Precision.HIGH):
+    return lax.dot_general(left, right, (((1,), (1,)), ((), ())), precision=precision)
 
 
 def pair_energy(
@@ -75,9 +73,11 @@
     atom_hot = (atoms[:, None] == atom_index[None]).astype(jnp.float32)
     slot_hot = (jnp.arange(slots)[:, None] == slot_index[None]).astype(jnp.float32)
     member = (centres[:, None] == atoms[None]).astype(jnp.float32)
-    by_atom = matmul(extended.reshape(slots * 3, atoms_here), atom_hot)
+    by_atom = matmul(
+        extended.reshape(slots * 3, atoms_here), atom_hot, lax.Precision.HIGHEST
+    )
     far_end = jnp.sum(by_atom.reshape(slots, 3, pair_count) * slot_hot[:, None, :], axis=0)
-    near_end = matmul_t(extended[13], member)
+    near_end = matmul_t(extended[13], member, lax.Precision.HIGHEST)
     displace = far_end + shifts - near_end
     distance = jnp.sqrt(jnp.sum(displace * displace, axis=0))
     unit = displace / distance

time: 124 us -> 112 us (0.903)
  matrix products: 39.9 us -> 27.8 us
    dot_general x29, matrix products: 39.6 us -> 27.5 us  [the longest x22 22 us: matmul(): return jnp.dot(left, right, precision=precision)]
where the time goes in v2:
time: 112 us; the launch traced here: 111 us
  starting transfers between devices  45.5 us (41%)
  matrix products  27.8 us (25%)
  waiting for transfers between devices  21.4 us (19%)
  blocking collectives  10.8 us (10%)
  other arithmetic  2.58 us (2%)
  local copies, waits for them, and re-layouts  2.12 us (2%)
  between operations  1.27 us (1%)
    dot_general x22, matrix products, matmul(): return jnp.dot(left, right, precision=precision)  22 us
    ppermute x3, starting transfers between devices, extended_2(): lax.ppermute(lax.slice_in_dim(block, 0, width, axis=dim), axis, backward)  20.5 us
    ppermute x3, waiting for transfers between devices, fold_halo(): from_high = lax.ppermute(grad[0], axis, backward)  11.5 us
    all_to_all x1, blocking collectives, per_device(): lax.all_to_all(outgoing, 'gz', split_axis=0, concat_axis=0, tiled=True)  10.8 us
    ppermute x3, starting transfers between devices, fold_halo(): from_high = lax.ppermute(grad[0], axis, backward)  10.6 us
    ppermute x3, starting transfers between devices, extended_2(): lax.ppermute(lax.slice_in_dim(block, block.shape[dim] - width, None, axis...  8.43 us
    ppermute x3, waiting for transfers between devices, extended_2(): lax.ppermute(lax.slice_in_dim(block, 0, width, axis=dim), axis, backward)  7.63 us
    ppermute x3, starting transfers between devices, fold_halo(): from_low = lax.ppermute(grad[2], axis, forward)  6.05 us
  transfers between devices with their start and end apart: 12, of which 6 were waited for; matrix products, arithmetic and copies ran while one was open for 3% of the time, Pallas kernels for 0%

profile of v2, /device:TPU:112, one launch (start us, length us, event | category | flops | bytes accessed | tf_op | source)
XLA Modules:
  0.0 111.5 jit_solution(9216087077763116410)
XLA Ops:
  0.0 5.9 %collective-permute-start = (f32[1,1,1,3,256]{4,2,3,1,0:T(1,128)}, f32[1,1,1,3,256]{4,2,3,1,0:T(1,128)S(1)}, u32[]{:S(2)}, u32[]{:S(2)}) collective-permute-start(f32[1,1,1,3,256]{4,2,3,1,0:T(1,128)} %param.16), channel_id=1, source_target_pairs={{0,64},{64,128},{128,192},{192,256},{256,320},{320,384},{384,448},... | collective-permute-start | bytes 9224 | tf_op jit(solution)/shard_map/ppermute | solution.py:21
  5.9 1.9 %collective-permute-start.1 = (f32[1,1,1,3,256]{4,2,3,1,0:T(1,128)}, f32[1,1,1,3,256]{4,2,3,1,0:T(1,128)S(1)}, u32[]{:S(2)}, u32[]{:S(2)}) collective-permute-start(f32[1,1,1,3,256]{4,2,3,1,0:T(1,128)} %param.16), channel_id=1, source_target_pairs={{64,0},{128,64},{192,128},{256,192},{320,256},{384,320},{448,384},... | collective-permute-start | bytes 9224 | tf_op jit(solution)/shard_map/ppermute | solution.py:24
  9.6 1.3 %fusion.113 = f32[1536,256]{0,1:T(8,128)S(1)} fusion(f32[256,4]{0,1:T(4,128)} %param.24, s32[1536]{0:T(1024)S(1)} %get-tuple-element.26), kind=kOutput, calls=%fused_computation.169 | convolution fusion | flops 9443328 | bytes 1583104 | tf_op jit(solution)/shard_map/jvp()/dot_general | solution.py:39
  10.9 6.7 %collective-permute-done.1 = f32[1,1,1,3,256]{4,2,3,1,0:T(1,128)S(1)} collective-permute-done((f32[1,1,1,3,256]{4,2,3,1,0:T(1,128)}, f32[1,1,1,3,256]{4,2,3,1,0:T(1,128)S(1)}, u32[]{:S(2)}, u32[]{:S(2)}) %collective-permute-start.1) | collective-permute-done | bytes 3104 | tf_op jit(solution)/shard_map/ppermute | solution.py:24
  17.7 13.4 %collective-permute-start.3 = (f32[3,1,1,3,256]{4,2,3,1,0:T(1,128)S(1)}, f32[3,1,1,3,256]{4,2,3,1,0:T(1,128)S(1)}, u32[]{:S(2)}, u32[]{:S(2)}) collective-permute-start(f32[3,1,1,3,256]{4,2,3,1,0:T(1,128)S(1)} %constant_dynamic-update-slice_fusion), channel_id=1, source_target_pairs={{4,0},{8,4},{12,8},{16,12},{20,16},{24,20},{28,24},{32,28},{36,32}... | collective-permute-start | bytes 27656 | tf_op jit(solution)/shard_map/ppermute | solution.py:24
  31.5 0.9 collective-permute-done.2
  32.5 2.5 %collective-permute-start.4 = (f32[3,3,1,3,256]{4,2,3,1,0:T(1,128)S(1)}, f32[3,3,1,3,256]{4,2,3,1,0:T(1,128)S(1)}, u32[]{:S(2)}, u32[]{:S(2)}) collective-permute-start(f32[3,3,1,3,256]{4,2,3,1,0:T(1,128)S(1)} %pad_maximum_fusion.1), channel_id=1, source_target_pairs={{0,1},{1,2},{2,3},{3,0},{4,5},{5,6},{6,7},{7,4},{8,9},{9,10},{10,1... | collective-permute-start | bytes 82952 | tf_op jit(solution)/shard_map/ppermute | solution.py:21
  35.0 5.1 %collective-permute-start.5 = (f32[3,3,1,3,256]{4,2,3,1,0:T(1,128)S(1)}, f32[3,3,1,3,256]{4,2,3,1,0:T(1,128)S(1)}, u32[]{:S(2)}, u32[]{:S(2)}) collective-permute-start(f32[3,3,1,3,256]{4,2,3,1,0:T(1,128)S(1)} %pad_maximum_fusion.1), channel_id=1, source_target_pairs={{1,0},{2,1},{3,2},{0,3},{5,4},{6,5},{7,6},{4,7},{9,8},{10,9},{11,1... | collective-permute-start | bytes 82952 | tf_op jit(solution)/shard_map/ppermute | solution.py:24
  43.5 0.9 fusion.93
  44.5 1.2 %broadcast_multiply_fusion = (f32[256,1536]{1,0:T(8,128)S(1)}, f32[256,1536]{1,0:T(8,128)S(1)}) fusion(f32[1536]{0:T(1024)S(1)} %get-tuple-element.47, f32[1536,256]{0,1:T(8,128)S(1)} %fusion.113, f32[1536,256]{0,1:T(8,128)S(1)} %fusion.93, f32[4,1536]{1,0:T(4,128)S(1)} %fusion.39, f32[256,4]{0,1:T(4,128)S(1)} %copy-done.8), kind=kOutput, calls=%fused_computation.85 | convolution fusion | flops 12189696 | bytes 6326272 | tf_op jit(solution)/shard_map/jvp()/dot_general | solution.py:39
  46.9 1.4 %fusion.37 = f32[96,1536]{1,0:T(8,128)S(1)} fusion(f32[96,256]{1,0:T(8,128)S(1)} %fusion.47, s32[1536]{0:T(1024)S(1)} %get-tuple-element.28), kind=kOutput, calls=%fused_computation.62 | convolution fusion | flops 226885632 | bytes 694272 | tf_op jit(solution)/shard_map/jvp()/dot_general | solution.py:43
  48.8 1.8 %multiply_add_fusion = (f32[256,1536]{1,0:T(8,128)S(1)}, f32[256,1536]{1,0:T(8,128)S(1)}) fusion(f32[256,1536]{1,0:T(8,128)S(1)} %get-tuple-element.55, f32[1536]{0:T(1024)S(1)} %get-tuple-element.47, f32[2,256,288]{1,2,0:T(8,128)S(1)} %copy-done.7, f32[32,1536]{1,0:T(8,128)S(1)} %multiply_reduce_fusion.11), kind=kOutput, calls=%fused_computation.49 | convolution fusion | flops 682278912 | bytes 6791168 | tf_op jit(solution)/shard_map/jvp()/dot_general | solution.py:39
  51.7 1.2 %fusion.35 = f32[96,1536]{1,0:T(8,128)S(1)} fusion(f32[96,256]{1,0:T(8,128)S(1)} %fusion.48, s32[1536]{0:T(1024)S(1)} %get-tuple-element.28), kind=kOutput, calls=%fused_computation.60 | convolution fusion | flops 226885632 | bytes 694272 | tf_op jit(solution)/shard_map/jvp()/dot_general | solution.py:43
  54.2 1.7 %multiply_reduce_fusion.2 = (f32[1536]{0:T(1024)S(1)}, f32[256,1536]{1,0:T(8,128)S(1)}) fusion(f32[256]{0:T(256)S(1)} %copy-done.9, f32[2,256,288]{1,2,0:T(8,128)S(1)} %copy-done.7, f32[32,1536]{1,0:T(8,128)S(1)} %get-tuple-element.34, f32[256,1536]{1,0:T(8,128)S(1)} %get-tuple-element.59), kind=kOutput, calls=%fused_computation.44 | convolution fusion | flops 682277376 | bytes 3644416 | tf_op jit(solution)/shard_map/jvp()/dot_general | solution.py:39
  55.9 1.4 %convolution_bitcast_fusion.1 = f32[288,1536]{1,0:T(8,128)S(1)} fusion(f32[256,1536]{1,0:T(8,128)S(1)} %get-tuple-element.64, f32[256]{0:T(256)S(1)} %copy-done.9, f32[1536]{0:T(1024)S(1)} %get-tuple-element.47, f32[2,256,288]{1,2,0:T(8,128)S(1)} %copy-done.7), kind=kOutput, calls=%fused_computation.3 | convolution fusion | flops 683409408 | bytes 3646464 | tf_op jit(solution)/shard_map/transpose(jvp())/dot_general | solution.py:39
  58.0 1.2 %fusion.33 = f32[96,1536]{1,0:T(8,128)S(1)} fusion(f32[96,256]{1,0:T(8,128)S(1)} %fusion.49, s32[1536]{0:T(1024)S(1)} %get-tuple-element.28), kind=kOutput, calls=%fused_computation.58 | convolution fusion | flops 226885632 | bytes 694272 | tf_op jit(solution)/shard_map/transpose(jvp())/dot_general | solution.py:39
  59.4 1.2 %multiply_reduce_fusion.1 = (f32[1536]{0:T(1024)S(1)}, f32[256,1536]{1,0:T(8,128)S(1)}) fusion(f32[256,1536]{1,0:T(8,128)S(1)} %get-tuple-element.60, f32[32,1536]{1,0:T(8,128)S(1)} %get-tuple-element.23, f32[2,32,256]{2,1,0:T(8,128)S(1)} %copy-done.1, f32[288,1536]{1,0:T(8,128)S(1)} %convolution_bitcast_fusion.1, f32[256]{0:T(256)S(1)} %copy-done.9), kind=kOutput, calls=%fused_computation.43 | convolution fusion | flops 78641664 | bytes 4955136 | tf_op jit(solution)/shard_map/transpose(jvp())/dot_general | solution.py:39
  60.6 1.4 %convolution_bitcast_fusion = f32[288,1536]{1,0:T(8,128)S(1)} fusion(f32[256,1536]{1,0:T(8,128)S(1)} %get-tuple-element.60, f32[256,1536]{1,0:T(8,128)S(1)} %get-tuple-element.66, f32[1536]{0:T(1024)S(1)} %get-tuple-element.47, f32[2,256,288]{1,2,0:T(8,128)S(1)} %copy-done.7), kind=kOutput, calls=%fused_computation.2 | convolution fusion | flops 683409408 | bytes 5218304 | tf_op jit(solution)/shard_map/transpose(jvp())/dot_general | solution.py:39
  62.7 1.4 %fusion.31 = f32[96,1536]{1,0:T(8,128)S(1)} fusion(f32[96,256]{1,0:T(8,128)S(1)} %fusion.50, s32[1536]{0:T(1024)S(1)} %get-tuple-element.28), kind=kOutput, calls=%fused_computation.56 | convolution fusion | flops 226885632 | bytes 694272 | tf_op jit(solution)/shard_map/transpose(jvp())/dot_general | solution.py:39
  64.6 1.0 fusion.4
  65.8 1.2 %multiply_reduce_fusion = (f32[1536]{0:T(1024)S(1)}, f32[256,1536]{1,0:T(8,128)S(1)}) fusion(f32[256,1536]{1,0:T(8,128)S(1)} %get-tuple-element.56, f32[256,1536]{1,0:T(8,128)S(1)} %fusion.4, f32[32,1536]{1,0:T(8,128)S(1)} %get-tuple-element.21, f32[2,32,256]{2,1,0:T(8,128)S(1)} %copy-done.1), kind=kOutput, calls=%fused_computation.42 | convolution fusion | flops 78248448 | bytes 4954112 | tf_op jit(solution)/shard_map/transpose(jvp())/dot_general | solution.py:39
  67.1 1.1 fusion.91
  68.2 1.0 fusion.41
  70.0 4.1 %collective-permute-start.6 = (f32[3,3,3,256]{3,2,1,0:T(4,128)S(1)}, f32[3,3,3,256]{3,2,1,0:T(4,128)S(1)}, u32[]{:S(2)}, u32[]{:S(2)}) collective-permute-start(f32[3,3,3,256]{3,2,1,0:T(4,128)S(1)} %bitcast.198), channel_id=1, source_target_pairs={{0,64},{64,128},{128,192},{192,256},{256,320},{320,384},{384,448},... | collective-permute-start | bytes 82952 | tf_op jit(solution)/shard_map/ppermute | solution.py:32
  74.1 1.9 %collective-permute-start.7 = (f32[3,3,3,256]{3,2,1,0:T(4,128)S(1)}, f32[3,3,3,256]{3,2,1,0:T(4,128)S(1)}, u32[]{:S(2)}, u32[]{:S(2)}) collective-permute-start(f32[3,3,3,256]{3,2,1,0:T(4,128)S(1)} %bitcast.197), channel_id=1, source_target_pairs={{64,0},{128,64},{192,128},{256,192},{320,256},{384,320},{448,384},... | collective-permute-start | bytes 82952 | tf_op jit(solution)/shard_map/ppermute | solution.py:33
  76.0 10.2 %collective-permute-done.7 = f32[3,3,3,256]{3,2,1,0:T(4,128)S(1)} collective-permute-done((f32[3,3,3,256]{3,2,1,0:T(4,128)S(1)}, f32[3,3,3,256]{3,2,1,0:T(4,128)S(1)}, u32[]{:S(2)}, u32[]{:S(2)}) %collective-permute-start.7) | collective-permute-done | bytes 27680 | tf_op jit(solution)/shard_map/ppermute | solution.py:33
  86.3 2.9 %collective-permute-start.9 = (f32[3,3,256]{2,1,0:T(4,128)S(1)}, f32[3,3,256]{2,1,0:T(4,128)S(1)}, u32[]{:S(2)}, u32[]{:S(2)}) collective-permute-start(f32[3,3,256]{2,1,0:T(4,128)S(1)} %get-tuple-element.40), channel_id=1, source_target_pairs={{4,0},{8,4},{12,8},{16,12},{20,16},{24,20},{28,24},{32,28},{36,32}... | collective-permute-start | bytes 27656 | tf_op jit(solution)/shard_map/ppermute | solution.py:33
  89.4 1.3 %collective-permute-done.8 = f32[3,3,256]{2,1,0:T(4,128)S(1)} collective-permute-done((f32[3,3,256]{2,1,0:T(4,128)S(1)}, f32[3,3,256]{2,1,0:T(4,128)S(1)}, u32[]{:S(2)}, u32[]{:S(2)}) %collective-permute-start.8) | collective-permute-done | bytes 9248 | tf_op jit(solution)/shard_map/ppermute | solution.py:32
  90.7 1.9 %collective-permute-start.10 = (f32[3,256]{1,0:T(4,128)S(1)}, f32[3,256]{1,0:T(4,128)S(1)}, u32[]{:S(2)}, u32[]{:S(2)}) collective-permute-start(f32[3,256]{1,0:T(4,128)S(1)} %get-tuple-element.44), channel_id=1, source_target_pairs={{0,1},{1,2},{2,3},{3,0},{4,5},{5,6},{6,7},{7,4},{8,9},{9,10},{10,1... | collective-permute-start | bytes 9224 | tf_op jit(solution)/shard_map/ppermute | solution.py:32
  92.6 5.7 %collective-permute-start.11 = (f32[3,256]{1,0:T(4,128)S(1)}, f32[3,256]{1,0:T(4,128)S(1)}, u32[]{:S(2)}, u32[]{:S(2)}) collective-permute-start(f32[3,256]{1,0:T(4,128)S(1)} %get-tuple-element.45), channel_id=1, source_target_pairs={{1,0},{2,1},{3,2},{0,3},{5,4},{6,5},{7,6},{4,7},{9,8},{10,9},{11,1... | collective-permute-start | bytes 9224 | tf_op jit(solution)/shard_map/ppermute | solution.py:33
  98.4 1.3 %collective-permute-done.11 = f32[3,256]{1,0:T(4,128)S(1)} collective-permute-done((f32[3,256]{1,0:T(4,128)S(1)}, f32[3,256]{1,0:T(4,128)S(1)}, u32[]{:S(2)}, u32[]{:S(2)}) %collective-permute-start.11) | collective-permute-done | bytes 3104 | tf_op jit(solution)/shard_map/ppermute | solution.py:33
  100.1 10.8 %all_to_all.5 = f32[4,9,128]{2,1,0:T(8,128)S(1)} all-to-all(f32[4,9,128]{2,1,0:T(8,128)S(1)} %copy.19), channel_id=1, replica_groups=mesh['gx'=16,'gy'=16,'gz'=4] {'gz'}, dimensions={0} | all-to-all | bytes 36864 | tf_op jit(solution)/shard_map/all_to_all | solution.py:170
  (90 shorter events, 12.7 us)
Async XLA Ops:
  0.0 52.9 %copy-start = (f32[32,256]{1,0:T(8,128)S(1)}, f32[32,256]{1,0:T(8,128)}, u32[]{:S(2)}) copy-start(f32[32,256]{1,0:T(8,128)} %param.27) | copy-start | bytes 98308
  0.0 10.9 %copy-start.3 = (f32[1,1,1,3,256]{4,2,3,1,0:T(1,128)S(1)}, f32[1,1,1,3,256]{4,2,3,1,0:T(1,128)}, u32[]{:S(2)}) copy-start(f32[1,1,1,3,256]{4,2,3,1,0:T(1,128)} %param.16) | copy-start | bytes 9220
  0.0 31.1 %copy-start.6 = (s32[1,1,1,256]{3,2,1,0:T(1,128)S(1)}, s32[1,1,1,256]{3,2,1,0:T(1,128)}, u32[]{:S(2)}) copy-start(s32[1,1,1,256]{3,2,1,0:T(1,128)} %param.18) | copy-start | bytes 3076
  0.0 10.9 %collective-permute-start = (f32[1,1,1,3,256]{4,2,3,1,0:T(1,128)}, f32[1,1,1,3,256]{4,2,3,1,0:T(1,128)S(1)}, u32[]{:S(2)}, u32[]{:S(2)}) collective-permute-start(f32[1,1,1,3,256]{4,2,3,1,0:T(1,128)} %param.16), channel_id=1, source_target_pairs={{0,64},{64,128},{128,192},{192,256},{256,320},{320,384},{384,448},... | collective-permute-start | bytes 9224 | tf_op jit(solution)/shard_map/ppermute | solution.py:21
  5.9 11.7 %collective-permute-start.1 = (f32[1,1,1,3,256]{4,2,3,1,0:T(1,128)}, f32[1,1,1,3,256]{4,2,3,1,0:T(1,128)S(1)}, u32[]{:S(2)}, u32[]{:S(2)}) collective-permute-start(f32[1,1,1,3,256]{4,2,3,1,0:T(1,128)} %param.16), channel_id=1, source_target_pairs={{64,0},{128,64},{192,128},{256,192},{320,256},{384,320},{448,384},... | collective-permute-start | bytes 9224 | tf_op jit(solution)/shard_map/ppermute | solution.py:24
  10.9 32.6 %copy-start.4 = (f32[256,8]{0,1:T(8,128)S(1)}, f32[256,8]{0,1:T(8,128)}, u32[]{:S(2)}) copy-start(f32[256,8]{0,1:T(8,128)} %param.22) | copy-start | bytes 24580
  17.7 14.8 %collective-permute-start.2 = (f32[3,1,1,3,256]{4,2,3,1,0:T(1,128)S(1)}, f32[3,1,1,3,256]{4,2,3,1,0:T(1,128)S(1)}, u32[]{:S(2)}, u32[]{:S(2)}) collective-permute-start(f32[3,1,1,3,256]{4,2,3,1,0:T(1,128)S(1)} %constant_dynamic-update-slice_fusion), channel_id=1, source_target_pairs={{0,4},{4,8},{8,12},{12,16},{16,20},{20,24},{24,28},{28,32},{32,36}... | collective-permute-start | bytes 27656 | tf_op jit(solution)/shard_map/ppermute | solution.py:21
  17.7 14.8 %collective-permute-start.3 = (f32[3,1,1,3,256]{4,2,3,1,0:T(1,128)S(1)}, f32[3,1,1,3,256]{4,2,3,1,0:T(1,128)S(1)}, u32[]{:S(2)}, u32[]{:S(2)}) collective-permute-start(f32[3,1,1,3,256]{4,2,3,1,0:T(1,128)S(1)} %constant_dynamic-update-slice_fusion), channel_id=1, source_target_pairs={{4,0},{8,4},{12,8},{16,12},{20,16},{24,20},{28,24},{32,28},{36,32}... | collective-permute-start | bytes 27656 | tf_op jit(solution)/shard_map/ppermute | solution.py:24
  32.5 8.3 %collective-permute-start.4 = (f32[3,3,1,3,256]{4,2,3,1,0:T(1,128)S(1)}, f32[3,3,1,3,256]{4,2,3,1,0:T(1,128)S(1)}, u32[]{:S(2)}, u32[]{:S(2)}) collective-permute-start(f32[3,3,1,3,256]{4,2,3,1,0:T(1,128)S(1)} %pad_maximum_fusion.1), channel_id=1, source_target_pairs={{0,1},{1,2},{2,3},{3,0},{4,5},{5,6},{6,7},{7,4},{8,9},{9,10},{10,1... | collective-permute-start | bytes 82952 | tf_op jit(solution)/shard_map/ppermute | solution.py:21
  35.0 6.7 %collective-permute-start.5 = (f32[3,3,1,3,256]{4,2,3,1,0:T(1,128)S(1)}, f32[3,3,1,3,256]{4,2,3,1,0:T(1,128)S(1)}, u32[]{:S(2)}, u32[]{:S(2)}) collective-permute-start(f32[3,3,1,3,256]{4,2,3,1,0:T(1,128)S(1)} %pad_maximum_fusion.1), channel_id=1, source_target_pairs={{1,0},{2,1},{3,2},{0,3},{5,4},{6,5},{7,6},{4,7},{9,8},{10,9},{11,1... | collective-permute-start | bytes 82952 | tf_op jit(solution)/shard_map/ppermute | solution.py:24
  41.8 2.7 %copy-start.8 = (f32[256,4]{0,1:T(4,128)S(1)}, f32[256,4]{0,1:T(4,128)}, u32[]{:S(2)}) copy-start(f32[256,4]{0,1:T(4,128)} %param.23) | copy-start | bytes 12292
  44.5 1.3 %copy-start.1 = (f32[2,32,256]{2,1,0:T(8,128)S(1)}, f32[2,32,256]{2,1,0:T(8,128)}, u32[]{:S(2)}) copy-start(f32[2,32,256]{2,1,0:T(8,128)} %param.26) | copy-start | bytes 196612
  45.7 2.5 %copy-start.2 = (f32[32,8]{0,1:T(8,128)S(1)}, f32[32,8]{0,1:T(8,128)}, u32[]{:S(2)}) copy-start(f32[32,8]{0,1:T(8,128)} %param.25) | copy-start | bytes 3076
  46.4 2.5 %copy-start.7 = (f32[2,256,288]{1,2,0:T(8,128)S(1)}, f32[2,256,288]{1,2,0:T(8,128)}, u32[]{:S(2)}) copy-start(f32[2,256,288]{1,2,0:T(8,128)} %param.28) | copy-start | bytes 1769476
  53.5 0.7 copy-start.9
  68.2 21.1 %copy-start.10 = (s32[1,1,1,2]{3,2,1,0:T(1,128)S(1)}, s32[1,1,1,2]{3,2,1,0:T(1,128)}, u32[]{:S(2)}) copy-start(s32[1,1,1,2]{3,2,1,0:T(1,128)} %param.21) | copy-start | bytes 28
  68.2 31.5 %copy-start.5 = (f32[1,1,1,3,256]{4,2,3,1,0:T(1,128)S(1)}, f32[1,1,1,3,256]{4,2,3,1,0:T(1,128)}, u32[]{:S(2)}) copy-start(f32[1,1,1,3,256]{4,2,3,1,0:T(1,128)} %param.17) | copy-start | bytes 9220
  70.0 6.1 %collective-permute-start.6 = (f32[3,3,3,256]{3,2,1,0:T(4,128)S(1)}, f32[3,3,3,256]{3,2,1,0:T(4,128)S(1)}, u32[]{:S(2)}, u32[]{:S(2)}) collective-permute-start(f32[3,3,3,256]{3,2,1,0:T(4,128)S(1)} %bitcast.198), channel_id=1, source_target_pairs={{0,64},{64,128},{128,192},{192,256},{256,320},{320,384},{384,448},... | collective-permute-start | bytes 82952 | tf_op jit(solution)/shard_map/ppermute | solution.py:32
  74.1 12.2 %collective-permute-start.7 = (f32[3,3,3,256]{3,2,1,0:T(4,128)S(1)}, f32[3,3,3,256]{3,2,1,0:T(4,128)S(1)}, u32[]{:S(2)}, u32[]{:S(2)}) collective-permute-start(f32[3,3,3,256]{3,2,1,0:T(4,128)S(1)} %bitcast.197), channel_id=1, source_target_pairs={{64,0},{128,64},{192,128},{256,192},{320,256},{384,320},{448,384},... | collective-permute-start | bytes 82952 | tf_op jit(solution)/shard_map/ppermute | solution.py:33
  86.3 4.3 %collective-permute-start.8 = (f32[3,3,256]{2,1,0:T(4,128)S(1)}, f32[3,3,256]{2,1,0:T(4,128)S(1)}, u32[]{:S(2)}, u32[]{:S(2)}) collective-permute-start(f32[3,3,256]{2,1,0:T(4,128)S(1)} %get-tuple-element.39), channel_id=1, source_target_pairs={{0,4},{4,8},{8,12},{12,16},{16,20},{20,24},{24,28},{28,32},{32,36}... | collective-permute-start | bytes 27656 | tf_op jit(solution)/shard_map/ppermute | solution.py:32
  86.3 4.3 %collective-permute-start.9 = (f32[3,3,256]{2,1,0:T(4,128)S(1)}, f32[3,3,256]{2,1,0:T(4,128)S(1)}, u32[]{:S(2)}, u32[]{:S(2)}) collective-permute-start(f32[3,3,256]{2,1,0:T(4,128)S(1)} %get-tuple-element.40), channel_id=1, source_target_pairs={{4,0},{8,4},{12,8},{16,12},{20,16},{24,20},{28,24},{32,28},{36,32}... | collective-permute-start | bytes 27656 | tf_op jit(solution)/shard_map/ppermute | solution.py:33
  90.7 7.7 %collective-permute-start.10 = (f32[3,256]{1,0:T(4,128)S(1)}, f32[3,256]{1,0:T(4,128)S(1)}, u32[]{:S(2)}, u32[]{:S(2)}) collective-permute-start(f32[3,256]{1,0:T(4,128)S(1)} %get-tuple-element.44), channel_id=1, source_target_pairs={{0,1},{1,2},{2,3},{3,0},{4,5},{5,6},{6,7},{7,4},{8,9},{9,10},{10,1... | collective-permute-start | bytes 9224 | tf_op jit(solution)/shard_map/ppermute | solution.py:32
  92.6 7.0 %collective-permute-start.11 = (f32[3,256]{1,0:T(4,128)S(1)}, f32[3,256]{1,0:T(4,128)S(1)}, u32[]{:S(2)}, u32[]{:S(2)}) collective-permute-start(f32[3,256]{1,0:T(4,128)S(1)} %get-tuple-element.45), channel_id=1, source_target_pairs={{1,0},{2,1},{3,2},{0,3},{5,4},{6,5},{7,6},{4,7},{9,8},{10,9},{11,1... | collective-permute-start | bytes 9224 | tf_op jit(solution)/shard_map/ppermute | solution.py:33

commit v3 on v2

--- a/solution.py
+++ b/solution.py
@@ -135,8 +135,13 @@
     atoms_here = positions.shape[4]
     depth = atoms_here // 64
     zcount = lax.axis_size("gz")
-    beside_all = extended_2(positions, (("gx", 0), ("gy", 1), ("gz", 2)), 1)
-    extended = beside_all.reshape(27, 3, atoms_here)
+    blocks_count = atoms_here // 128
+    own_owners = owners[0, 0, 0]
+    owner_row = jnp.repeat(own_owners.astype(jnp.float32), 128)
+    carried = jnp.concatenate([positions, owner_row.reshape(1, 1, 1, 1, atoms_here)], axis=3)
+    beside_all = extended_2(carried, (("gx", 0), ("gy", 1), ("gz", 2)), 1)
+    extended = beside_all[:, :, :, :3].reshape(27, 3, atoms_here)
+    beside_owners = beside_all[1, 1, :, 3]
     own_species = species[0, 0, 0]
     grad = jax.grad(pair_energy)(
         extended,
@@ -153,21 +158,40 @@
         energy_weight,
     )
     grad = grad.reshape(3, 3, 3, 3, atoms_here)
-    forces = -fold_halo(grad, ("gx", "gy", "gz"))
+    partial = fold_halo(grad, ("gx", "gy"))
+    myself = lax.axis_index("gz")
+    receivers = jnp.arange(zcount)
+    sources = jnp.arange(zcount)
+    beside_hits = (
+        beside_owners.reshape(3, blocks_count, 128)[:, :, 0, None] == receivers.astype(jnp.float32)
+    ).astype(jnp.float32)
+    partial_blocks = partial.reshape(3, 3, blocks_count, 128).transpose(0, 2, 1, 3)
+    per_receiver = jnp.sum(beside_hits[:, :, :, None, None] * partial_blocks[:, :, None], axis=1)
+    source_of = (sources[None] == (myself + jnp.arange(3)[:, None] - 1) % zcount).astype(jnp.float32)
+    grad_out = jnp.sum(source_of[:, None, :, None, None] * per_receiver[:, :, None], axis=0)
     inverse_mass = 1.0 / (1.0 + own_species.astype(jnp.float32))
-    new_vel = velocities[0, 0, 0] + TIME_STEP * forces * inverse_mass[None]
-    new_pos = positions[0, 0, 0] + TIME_STEP * new_vel
-    state = jnp.concatenate([new_pos, new_vel, forces], axis=0)
-    blocks_count = atoms_here // 128
-    blocks = state.reshape(9, blocks_count, 128).transpose(1, 0, 2)
-    hits = (owners[0, 0, 0][:, None] == jnp.arange(zcount)[None]).astype(jnp.float32)
-    outgoing = jnp.einsum("bd,bcq->dcq", hits, blocks, precision=lax.Precision.HIGHEST)
-    sent = jnp.sum(hits, axis=0)
-    myself = lax.axis_index("gz")
-    target = jnp.arange(zcount, dtype=jnp.int32)
-    rise = sent * (myself - target).astype(jnp.float32) * float(depth)
-    outgoing = outgoing.at[:, 2, :].add(rise[:, None])
+    own_rows = jnp.concatenate(
+        [positions[0, 0, 0], velocities[0, 0, 0], inverse_mass[None], jnp.ones((1, atoms_here), jnp.float32)],
+        axis=0,
+    )
+    own_blocks = own_rows.reshape(8, blocks_count, 128).transpose(1, 0, 2)
+    hits = (own_owners[:, None] == receivers[None]).astype(jnp.float32)
+    own_out = jnp.sum(hits[:, :, None, None] * own_blocks[:, None], axis=0)
+    at_self = (sources == myself).astype(jnp.float32)
+    own_out = at_self[None, :, None, None] * own_out[:, None]
+    outgoing = jnp.concatenate([grad_out, own_out], axis=2)
     arrived = lax.all_to_all(outgoing, "gz", split_axis=0, concat_axis=0, tiled=True)
+    gathered = jnp.sum(arrived, axis=0)
+    forces = -gathered[:, 0:3]
+    old_pos = gathered[:, 3:6]
+    old_vel = gathered[:, 6:9]
+    arrived_mass = gathered[:, 9:10]
+    flags = gathered[:, 10, 0]
+    new_vel = old_vel + TIME_STEP * forces * arrived_mass
+    new_pos = old_pos + TIME_STEP * new_vel
+    state = jnp.concatenate([new_pos, new_vel, forces], axis=1)
+    rise = flags * (sources - myself).astype(jnp.float32) * float(depth)
+    arrived = state.at[:, 2, :].add(rise[:, None])
     return arrived[None, None, None]
 
 

time: 112 us -> 114 us (1.018)
  the two profiles are of different devices: /device:TPU:112 before, /device:TPU:2 now
where the time goes in v3:
time: 114 us
  starting transfers between devices  44.1 us (39%)
  matrix products  28.2 us (25%)
  waiting for transfers between devices  21.4 us (19%)
  blocking collectives  9.26 us (8%)
  other arithmetic  7.82 us (7%)
  local copies, waits for them, and re-layouts  1.74 us (2%)
  between operations  1.26 us (1%)
    ppermute x3, starting transfers between devices, extended_2(): lax.ppermute(lax.slice_in_dim(block, 0, width, axis=dim), axis, backward)  27 us
    dot_general x22, matrix products, matmul(): return jnp.dot(left, right, precision=precision)  22 us
    ppermute x2, waiting for transfers between devices, fold_halo(): from_low = lax.ppermute(grad[2], axis, forward)  11.4 us
    ppermute x2, starting transfers between devices, fold_halo(): from_high = lax.ppermute(grad[0], axis, backward)  10.8 us
    all_to_all x1, blocking collectives, per_device(): lax.all_to_all(outgoing, 'gz', split_axis=0, concat_axis=0, tiled=True)  9.26 us
    ppermute x3, waiting for transfers between devices, extended_2(): lax.ppermute(lax.slice_in_dim(block, block.shape[dim] - width, None, axis...  8.61 us
    dot_general x7, matrix products, matmul_t(): lax.dot_general(left, right, (((1,), (1,)), ((), ())), precision=precision)  6.19 us
    ppermute x3, starting transfers between devices, extended_2(): lax.ppermute(lax.slice_in_dim(block, block.shape[dim] - width, None, axis...  4.42 us
  transfers between devices with their start and end apart: 10, of which 6 were waited for; matrix products, arithmetic and copies ran while one was open for 6% of the time, Pallas kernels for 0%

profile of v3, /device:TPU:2, one launch (start us, length us, event | category | flops | bytes accessed | tf_op | source)
XLA Modules:
  0.0 113.7 jit_solution(15629110484393910027)
XLA Ops:
  1.4 10.2 %collective-permute-start.1 = (f32[1,1,1,4,256]{4,2,3,1,0:T(1,128)S(1)}, f32[1,1,1,4,256]{4,2,3,1,0:T(1,128)S(1)}, u32[]{:S(2)}, u32[]{:S(2)}) collective-permute-start(f32[1,1,1,4,256]{4,2,3,1,0:T(1,128)S(1)} %pad_maximum_fusion.4), channel_id=1, source_target_pairs={{64,0},{128,64},{192,128},{256,192},{320,256},{384,320},{448,384},... | collective-permute-start | bytes 12296 | tf_op jit(solution)/shard_map/ppermute | solution.py:24
  11.6 1.9 %collective-permute-start = (f32[1,1,1,4,256]{4,2,3,1,0:T(1,128)S(1)}, f32[1,1,1,4,256]{4,2,3,1,0:T(1,128)S(1)}, u32[]{:S(2)}, u32[]{:S(2)}) collective-permute-start(f32[1,1,1,4,256]{4,2,3,1,0:T(1,128)S(1)} %pad_maximum_fusion.4), channel_id=1, source_target_pairs={{0,64},{64,128},{128,192},{192,256},{256,320},{320,384},{384,448},... | collective-permute-start | bytes 12296 | tf_op jit(solution)/shard_map/ppermute | solution.py:21
  17.6 1.1 fusion.39
  18.8 1.3 %fusion.113 = f32[1536,256]{0,1:T(8,128)S(1)} fusion(f32[256,4]{0,1:T(4,128)} %param.24, s32[1536]{0:T(1024)S(1)} %get-tuple-element.26), kind=kOutput, calls=%fused_computation.174 | convolution fusion | flops 9443328 | bytes 1583104 | tf_op jit(solution)/shard_map/jvp()/dot_general | solution.py:39
  20.1 3.0 %collective-permute-done = f32[1,1,1,4,256]{4,2,3,1,0:T(1,128)S(1)} collective-permute-done((f32[1,1,1,4,256]{4,2,3,1,0:T(1,128)S(1)}, f32[1,1,1,4,256]{4,2,3,1,0:T(1,128)S(1)}, u32[]{:S(2)}, u32[]{:S(2)}) %collective-permute-start) | collective-permute-done | bytes 4128 | tf_op jit(solution)/shard_map/ppermute | solution.py:21
  23.2 13.4 %collective-permute-start.3 = (f32[3,1,1,4,256]{4,2,3,1,0:T(1,128)S(1)}, f32[3,1,1,4,256]{4,2,3,1,0:T(1,128)S(1)}, u32[]{:S(2)}, u32[]{:S(2)}) collective-permute-start(f32[3,1,1,4,256]{4,2,3,1,0:T(1,128)S(1)} %pad_maximum_fusion.3), channel_id=1, source_target_pairs={{4,0},{8,4},{12,8},{16,12},{20,16},{24,20},{28,24},{32,28},{36,32}... | collective-permute-start | bytes 36872 | tf_op jit(solution)/shard_map/ppermute | solution.py:24
  36.7 1.3 %collective-permute-done.3 = f32[3,1,1,4,256]{4,2,3,1,0:T(1,128)S(1)} collective-permute-done((f32[3,1,1,4,256]{4,2,3,1,0:T(1,128)S(1)}, f32[3,1,1,4,256]{4,2,3,1,0:T(1,128)S(1)}, u32[]{:S(2)}, u32[]{:S(2)}) %collective-permute-start.3) | collective-permute-done | bytes 12320 | tf_op jit(solution)/shard_map/ppermute | solution.py:24
  38.0 2.9 %collective-permute-done.2 = f32[3,1,1,4,256]{4,2,3,1,0:T(1,128)S(1)} collective-permute-done((f32[3,1,1,4,256]{4,2,3,1,0:T(1,128)S(1)}, f32[3,1,1,4,256]{4,2,3,1,0:T(1,128)S(1)}, u32[]{:S(2)}, u32[]{:S(2)}) %collective-permute-start.2) | collective-permute-done | bytes 12320 | tf_op jit(solution)/shard_map/ppermute | solution.py:21
  41.0 3.3 %collective-permute-start.5 = (f32[3,3,1,4,256]{4,2,3,1,0:T(1,128)S(1)}, f32[3,3,1,4,256]{4,2,3,1,0:T(1,128)S(1)}, u32[]{:S(2)}, u32[]{:S(2)}) collective-permute-start(f32[3,3,1,4,256]{4,2,3,1,0:T(1,128)S(1)} %pad_maximum_fusion.2), channel_id=1, source_target_pairs={{1,0},{2,1},{3,2},{0,3},{5,4},{6,5},{7,6},{4,7},{9,8},{10,9},{11,1... | collective-permute-start | bytes 110600 | tf_op jit(solution)/shard_map/ppermute | solution.py:24
  44.3 2.5 %collective-permute-start.4 = (f32[3,3,1,4,256]{4,2,3,1,0:T(1,128)S(1)}, f32[3,3,1,4,256]{4,2,3,1,0:T(1,128)S(1)}, u32[]{:S(2)}, u32[]{:S(2)}) collective-permute-start(f32[3,3,1,4,256]{4,2,3,1,0:T(1,128)S(1)} %pad_maximum_fusion.2), channel_id=1, source_target_pairs={{0,1},{1,2},{2,3},{3,0},{4,5},{5,6},{6,7},{7,4},{8,9},{9,10},{10,1... | collective-permute-start | bytes 110600 | tf_op jit(solution)/shard_map/ppermute | solution.py:21
  47.5 2.7 %collective-permute-done.4 = f32[3,3,1,4,256]{4,2,3,1,0:T(1,128)S(1)} collective-permute-done((f32[3,3,1,4,256]{4,2,3,1,0:T(1,128)S(1)}, f32[3,3,1,4,256]{4,2,3,1,0:T(1,128)S(1)}, u32[]{:S(2)}, u32[]{:S(2)}) %collective-permute-start.4) | collective-permute-done | bytes 36896 | tf_op jit(solution)/shard_map/ppermute | solution.py:21
  52.1 0.9 fusion.93
  53.5 1.2 %broadcast_multiply_fusion = (f32[256,1536]{1,0:T(8,128)S(1)}, f32[256,1536]{1,0:T(8,128)S(1)}) fusion(f32[1536]{0:T(1024)S(1)} %get-tuple-element.45, f32[1536,256]{0,1:T(8,128)S(1)} %fusion.113, f32[1536,256]{0,1:T(8,128)S(1)} %fusion.93, f32[4,1536]{1,0:T(4,128)S(1)} %fusion.39, f32[256,4]{0,1:T(4,128)S(1)} %copy-done.6), kind=kOutput, calls=%fused_computation.85 | convolution fusion | flops 12189696 | bytes 6326272 | tf_op jit(solution)/shard_map/jvp()/dot_general | solution.py:39
  56.7 1.4 %fusion.37 = f32[96,1536]{1,0:T(8,128)S(1)} fusion(f32[96,256]{1,0:T(8,128)S(1)} %fusion.47, s32[1536]{0:T(1024)S(1)} %get-tuple-element.28), kind=kOutput, calls=%fused_computation.62 | convolution fusion | flops 226885632 | bytes 694272 | tf_op jit(solution)/shard_map/jvp()/dot_general | solution.py:43
  58.2 1.8 %multiply_add_fusion = (f32[256,1536]{1,0:T(8,128)S(1)}, f32[256,1536]{1,0:T(8,128)S(1)}) fusion(f32[256,1536]{1,0:T(8,128)S(1)} %get-tuple-element.53, f32[1536]{0:T(1024)S(1)} %get-tuple-element.45, f32[2,256,288]{1,2,0:T(8,128)S(1)} %copy-done.5, f32[32,1536]{1,0:T(8,128)S(1)} %multiply_reduce_fusion.11), kind=kOutput, calls=%fused_computation.49 | convolution fusion | flops 682278912 | bytes 6791168 | tf_op jit(solution)/shard_map/jvp()/dot_general | solution.py:39
  61.1 1.2 %fusion.35 = f32[96,1536]{1,0:T(8,128)S(1)} fusion(f32[96,256]{1,0:T(8,128)S(1)} %fusion.48, s32[1536]{0:T(1024)S(1)} %get-tuple-element.28), kind=kOutput, calls=%fused_computation.60 | convolution fusion | flops 226885632 | bytes 694272 | tf_op jit(solution)/shard_map/jvp()/dot_general | solution.py:43
  62.5 1.7 %multiply_reduce_fusion.2 = (f32[1536]{0:T(1024)S(1)}, f32[256,1536]{1,0:T(8,128)S(1)}) fusion(f32[256]{0:T(256)S(1)} %copy-done.7, f32[2,256,288]{1,2,0:T(8,128)S(1)} %copy-done.5, f32[32,1536]{1,0:T(8,128)S(1)} %get-tuple-element.33, f32[256,1536]{1,0:T(8,128)S(1)} %get-tuple-element.57), kind=kOutput, calls=%fused_computation.44 | convolution fusion | flops 682277376 | bytes 3644416 | tf_op jit(solution)/shard_map/jvp()/dot_general | solution.py:39
  64.2 1.4 %convolution_bitcast_fusion.1 = f32[288,1536]{1,0:T(8,128)S(1)} fusion(f32[256,1536]{1,0:T(8,128)S(1)} %get-tuple-element.62, f32[256]{0:T(256)S(1)} %copy-done.7, f32[1536]{0:T(1024)S(1)} %get-tuple-element.45, f32[2,256,288]{1,2,0:T(8,128)S(1)} %copy-done.5), kind=kOutput, calls=%fused_computation.3 | convolution fusion | flops 683409408 | bytes 3646464 | tf_op jit(solution)/shard_map/transpose(jvp())/dot_general | solution.py:39
  66.3 1.2 %fusion.33 = f32[96,1536]{1,0:T(8,128)S(1)} fusion(f32[96,256]{1,0:T(8,128)S(1)} %fusion.49, s32[1536]{0:T(1024)S(1)} %get-tuple-element.28), kind=kOutput, calls=%fused_computation.58 | convolution fusion | flops 226885632 | bytes 694272 | tf_op jit(solution)/shard_map/transpose(jvp())/dot_general | solution.py:39
  67.7 1.2 %multiply_reduce_fusion.1 = (f32[1536]{0:T(1024)S(1)}, f32[256,1536]{1,0:T(8,128)S(1)}) fusion(f32[256,1536]{1,0:T(8,128)S(1)} %get-tuple-element.58, f32[32,1536]{1,0:T(8,128)S(1)} %get-tuple-element.23, f32[2,32,256]{2,1,0:T(8,128)S(1)} %copy-done.2, f32[288,1536]{1,0:T(8,128)S(1)} %convolution_bitcast_fusion.1, f32[256]{0:T(256)S(1)} %copy-done.7), kind=kOutput, calls=%fused_computation.43 | convolution fusion | flops 78641664 | bytes 4955136 | tf_op jit(solution)/shard_map/transpose(jvp())/dot_general | solution.py:39
  69.0 1.4 %convolution_bitcast_fusion = f32[288,1536]{1,0:T(8,128)S(1)} fusion(f32[256,1536]{1,0:T(8,128)S(1)} %get-tuple-element.58, f32[256,1536]{1,0:T(8,128)S(1)} %get-tuple-element.64, f32[1536]{0:T(1024)S(1)} %get-tuple-element.45, f32[2,256,288]{1,2,0:T(8,128)S(1)} %copy-done.5), kind=kOutput, calls=%fused_computation.2 | convolution fusion | flops 683409408 | bytes 5218304 | tf_op jit(solution)/shard_map/transpose(jvp())/dot_general | solution.py:39
  71.0 1.4 %fusion.31 = f32[96,1536]{1,0:T(8,128)S(1)} fusion(f32[96,256]{1,0:T(8,128)S(1)} %fusion.50, s32[1536]{0:T(1024)S(1)} %get-tuple-element.28), kind=kOutput, calls=%fused_computation.56 | convolution fusion | flops 226885632 | bytes 694272 | tf_op jit(solution)/shard_map/transpose(jvp())/dot_general | solution.py:39
  73.1 1.0 fusion.4
  74.1 1.2 %multiply_reduce_fusion = (f32[1536]{0:T(1024)S(1)}, f32[256,1536]{1,0:T(8,128)S(1)}) fusion(f32[256,1536]{1,0:T(8,128)S(1)} %get-tuple-element.54, f32[256,1536]{1,0:T(8,128)S(1)} %fusion.4, f32[32,1536]{1,0:T(8,128)S(1)} %get-tuple-element.21, f32[2,32,256]{2,1,0:T(8,128)S(1)} %copy-done.2), kind=kOutput, calls=%fused_computation.42 | convolution fusion | flops 78248448 | bytes 4954112 | tf_op jit(solution)/shard_map/transpose(jvp())/dot_general | solution.py:39
  75.4 1.1 fusion.91
  76.6 1.0 fusion.41
  78.3 7.8 %collective-permute-start.7 = (f32[3,3,3,256]{3,2,1,0:T(4,128)S(1)}, f32[3,3,3,256]{3,2,1,0:T(4,128)S(1)}, u32[]{:S(2)}, u32[]{:S(2)}) collective-permute-start(f32[3,3,3,256]{3,2,1,0:T(4,128)S(1)} %bitcast.199), channel_id=1, source_target_pairs={{64,0},{128,64},{192,128},{256,192},{320,256},{384,320},{448,384},... | collective-permute-start | bytes 82952 | tf_op jit(solution)/shard_map/ppermute | solution.py:33
  86.1 1.9 %collective-permute-start.6 = (f32[3,3,3,256]{3,2,1,0:T(4,128)S(1)}, f32[3,3,3,256]{3,2,1,0:T(4,128)S(1)}, u32[]{:S(2)}, u32[]{:S(2)}) collective-permute-start(f32[3,3,3,256]{3,2,1,0:T(4,128)S(1)} %bitcast.198), channel_id=1, source_target_pairs={{0,64},{64,128},{128,192},{192,256},{256,320},{320,384},{384,448},... | collective-permute-start | bytes 82952 | tf_op jit(solution)/shard_map/ppermute | solution.py:32
  88.3 10.1 %collective-permute-done.6 = f32[3,3,3,256]{3,2,1,0:T(4,128)S(1)} collective-permute-done((f32[3,3,3,256]{3,2,1,0:T(4,128)S(1)}, f32[3,3,3,256]{3,2,1,0:T(4,128)S(1)}, u32[]{:S(2)}, u32[]{:S(2)}) %collective-permute-start.6) | collective-permute-done | bytes 27680 | tf_op jit(solution)/shard_map/ppermute | solution.py:32
  98.4 2.9 %collective-permute-start.9 = (f32[3,3,256]{2,1,0:T(4,128)S(1)}, f32[3,3,256]{2,1,0:T(4,128)S(1)}, u32[]{:S(2)}, u32[]{:S(2)}) collective-permute-start(f32[3,3,256]{2,1,0:T(4,128)S(1)} %get-tuple-element.39), channel_id=1, source_target_pairs={{4,0},{8,4},{12,8},{16,12},{20,16},{24,20},{28,24},{32,28},{36,32}... | collective-permute-start | bytes 27656 | tf_op jit(solution)/shard_map/ppermute | solution.py:33
  101.4 1.3 %collective-permute-done.8 = f32[3,3,256]{2,1,0:T(4,128)S(1)} collective-permute-done((f32[3,3,256]{2,1,0:T(4,128)S(1)}, f32[3,3,256]{2,1,0:T(4,128)S(1)}, u32[]{:S(2)}, u32[]{:S(2)}) %collective-permute-start.8) | collective-permute-done | bytes 9248 | tf_op jit(solution)/shard_map/ppermute | solution.py:32
  103.0 9.3 %all_to_all.5 = f32[4,4,11,128]{3,1,2,0:T(4,128)S(1)} all-to-all(f32[4,4,11,128]{3,1,2,0:T(4,128)S(1)} %pad_maximum_fusion.1), channel_id=1, replica_groups=mesh['gx'=16,'gy'=16,'gz'=4] {'gz'}, dimensions={0} | all-to-all | bytes 180224 | tf_op jit(solution)/shard_map/all_to_all | solution.py:183
  (98 shorter events, 16.0 us)
Async XLA Ops:
  0.0 54.8 %copy-start = (f32[32,256]{1,0:T(8,128)S(1)}, f32[32,256]{1,0:T(8,128)}, u32[]{:S(2)}) copy-start(f32[32,256]{1,0:T(8,128)} %param.27) | copy-start | bytes 98308
  0.0 23.2 %copy-start.1 = (f32[1,1,1,3,256]{4,2,3,1,0:T(1,128)S(1)}, f32[1,1,1,3,256]{4,2,3,1,0:T(1,128)}, u32[]{:S(2)}) copy-start(f32[1,1,1,3,256]{4,2,3,1,0:T(1,128)} %param.16) | copy-start | bytes 9220
  1.4 18.7 %collective-permute-start.1 = (f32[1,1,1,4,256]{4,2,3,1,0:T(1,128)S(1)}, f32[1,1,1,4,256]{4,2,3,1,0:T(1,128)S(1)}, u32[]{:S(2)}, u32[]{:S(2)}) collective-permute-start(f32[1,1,1,4,256]{4,2,3,1,0:T(1,128)S(1)} %pad_maximum_fusion.4), channel_id=1, source_target_pairs={{64,0},{128,64},{192,128},{256,192},{320,256},{384,320},{448,384},... | collective-permute-start | bytes 12296 | tf_op jit(solution)/shard_map/ppermute | solution.py:24
  11.6 11.5 %collective-permute-start = (f32[1,1,1,4,256]{4,2,3,1,0:T(1,128)S(1)}, f32[1,1,1,4,256]{4,2,3,1,0:T(1,128)S(1)}, u32[]{:S(2)}, u32[]{:S(2)}) collective-permute-start(f32[1,1,1,4,256]{4,2,3,1,0:T(1,128)S(1)} %pad_maximum_fusion.4), channel_id=1, source_target_pairs={{0,64},{64,128},{128,192},{192,256},{256,320},{320,384},{384,448},... | collective-permute-start | bytes 12296 | tf_op jit(solution)/shard_map/ppermute | solution.py:21
  20.1 32.0 %copy-start.4 = (f32[256,8]{0,1:T(8,128)S(1)}, f32[256,8]{0,1:T(8,128)}, u32[]{:S(2)}) copy-start(f32[256,8]{0,1:T(8,128)} %param.22) | copy-start | bytes 24580
  23.2 14.8 %collective-permute-start.3 = (f32[3,1,1,4,256]{4,2,3,1,0:T(1,128)S(1)}, f32[3,1,1,4,256]{4,2,3,1,0:T(1,128)S(1)}, u32[]{:S(2)}, u32[]{:S(2)}) collective-permute-start(f32[3,1,1,4,256]{4,2,3,1,0:T(1,128)S(1)} %pad_maximum_fusion.3), channel_id=1, source_target_pairs={{4,0},{8,4},{12,8},{16,12},{20,16},{24,20},{28,24},{32,28},{36,32}... | collective-permute-start | bytes 36872 | tf_op jit(solution)/shard_map/ppermute | solution.py:24
  36.6 4.3 %collective-permute-start.2 = (f32[3,1,1,4,256]{4,2,3,1,0:T(1,128)S(1)}, f32[3,1,1,4,256]{4,2,3,1,0:T(1,128)S(1)}, u32[]{:S(2)}, u32[]{:S(2)}) collective-permute-start(f32[3,1,1,4,256]{4,2,3,1,0:T(1,128)S(1)} %pad_maximum_fusion.3), channel_id=1, source_target_pairs={{0,4},{4,8},{8,12},{12,16},{16,20},{20,24},{24,28},{28,32},{32,36}... | collective-permute-start | bytes 36872 | tf_op jit(solution)/shard_map/ppermute | solution.py:21
  41.0 6.5 %collective-permute-start.5 = (f32[3,3,1,4,256]{4,2,3,1,0:T(1,128)S(1)}, f32[3,3,1,4,256]{4,2,3,1,0:T(1,128)S(1)}, u32[]{:S(2)}, u32[]{:S(2)}) collective-permute-start(f32[3,3,1,4,256]{4,2,3,1,0:T(1,128)S(1)} %pad_maximum_fusion.2), channel_id=1, source_target_pairs={{1,0},{2,1},{3,2},{0,3},{5,4},{6,5},{7,6},{4,7},{9,8},{10,9},{11,1... | collective-permute-start | bytes 110600 | tf_op jit(solution)/shard_map/ppermute | solution.py:24
  44.3 5.9 %collective-permute-start.4 = (f32[3,3,1,4,256]{4,2,3,1,0:T(1,128)S(1)}, f32[3,3,1,4,256]{4,2,3,1,0:T(1,128)S(1)}, u32[]{:S(2)}, u32[]{:S(2)}) collective-permute-start(f32[3,3,1,4,256]{4,2,3,1,0:T(1,128)S(1)} %pad_maximum_fusion.2), channel_id=1, source_target_pairs={{0,1},{1,2},{2,3},{3,0},{4,5},{5,6},{6,7},{7,4},{8,9},{9,10},{10,1... | collective-permute-start | bytes 110600 | tf_op jit(solution)/shard_map/ppermute | solution.py:21
  50.4 2.7 %copy-start.3 = (f32[32,8]{0,1:T(8,128)S(1)}, f32[32,8]{0,1:T(8,128)}, u32[]{:S(2)}) copy-start(f32[32,8]{0,1:T(8,128)} %param.25) | copy-start | bytes 3076
  50.4 3.1 %copy-start.6 = (f32[256,4]{0,1:T(4,128)S(1)}, f32[256,4]{0,1:T(4,128)}, u32[]{:S(2)}) copy-start(f32[256,4]{0,1:T(4,128)} %param.23) | copy-start | bytes 12292
  54.8 0.8 copy-start.2
  56.1 2.1 %copy-start.5 = (f32[2,256,288]{1,2,0:T(8,128)S(1)}, f32[2,256,288]{1,2,0:T(8,128)}, u32[]{:S(2)}) copy-start(f32[2,256,288]{1,2,0:T(8,128)} %param.28) | copy-start | bytes 1769476
  61.1 1.4 %copy-start.7 = (f32[256]{0:T(256)S(1)}, f32[256]{0:T(256)}, u32[]{:S(2)}) copy-start(f32[256]{0:T(256)} %param.29) | copy-start | bytes 3076
  78.3 10.0 %collective-permute-start.7 = (f32[3,3,3,256]{3,2,1,0:T(4,128)S(1)}, f32[3,3,3,256]{3,2,1,0:T(4,128)S(1)}, u32[]{:S(2)}, u32[]{:S(2)}) collective-permute-start(f32[3,3,3,256]{3,2,1,0:T(4,128)S(1)} %bitcast.199), channel_id=1, source_target_pairs={{64,0},{128,64},{192,128},{256,192},{320,256},{384,320},{448,384},... | collective-permute-start | bytes 82952 | tf_op jit(solution)/shard_map/ppermute | solution.py:33
  86.1 12.3 %collective-permute-start.6 = (f32[3,3,3,256]{3,2,1,0:T(4,128)S(1)}, f32[3,3,3,256]{3,2,1,0:T(4,128)S(1)}, u32[]{:S(2)}, u32[]{:S(2)}) collective-permute-start(f32[3,3,3,256]{3,2,1,0:T(4,128)S(1)} %bitcast.198), channel_id=1, source_target_pairs={{0,64},{64,128},{128,192},{192,256},{256,320},{320,384},{384,448},... | collective-permute-start | bytes 82952 | tf_op jit(solution)/shard_map/ppermute | solution.py:32
  98.4 4.3 %collective-permute-start.8 = (f32[3,3,256]{2,1,0:T(4,128)S(1)}, f32[3,3,256]{2,1,0:T(4,128)S(1)}, u32[]{:S(2)}, u32[]{:S(2)}) collective-permute-start(f32[3,3,256]{2,1,0:T(4,128)S(1)} %get-tuple-element.38), channel_id=1, source_target_pairs={{0,4},{4,8},{8,12},{12,16},{16,20},{20,24},{24,28},{28,32},{32,36}... | collective-permute-start | bytes 27656 | tf_op jit(solution)/shard_map/ppermute | solution.py:32
  98.4 4.3 %collective-permute-start.9 = (f32[3,3,256]{2,1,0:T(4,128)S(1)}, f32[3,3,256]{2,1,0:T(4,128)S(1)}, u32[]{:S(2)}, u32[]{:S(2)}) collective-permute-start(f32[3,3,256]{2,1,0:T(4,128)S(1)} %get-tuple-element.39), channel_id=1, source_target_pairs={{4,0},{8,4},{12,8},{16,12},{20,16},{24,20},{28,24},{32,28},{36,32}... | collective-permute-start | bytes 27656 | tf_op jit(solution)/shard_map/ppermute | solution.py:33

commit v4 on v3

--- a/solution.py
+++ b/solution.py
@@ -137,9 +137,11 @@
     zcount = lax.axis_size("gz")
     blocks_count = atoms_here // 128
     own_owners = owners[0, 0, 0]
+    beside_xy = extended_2(positions, (("gx", 0), ("gy", 1)), 1)
     owner_row = jnp.repeat(own_owners.astype(jnp.float32), 128)
-    carried = jnp.concatenate([positions, owner_row.reshape(1, 1, 1, 1, atoms_here)], axis=3)
-    beside_all = extended_2(carried, (("gx", 0), ("gy", 1), ("gz", 2)), 1)
+    owner_rows = jnp.broadcast_to(owner_row, beside_xy.shape[:3] + (1, atoms_here))
+    carried = jnp.concatenate([beside_xy, owner_rows], axis=3)
+    beside_all = extended_2(carried, (("gz", 2),), 1)
     extended = beside_all[:, :, :, :3].reshape(27, 3, atoms_here)
     beside_owners = beside_all[1, 1, :, 3]
     own_species = species[0, 0, 0]

time: 114 us -> 114 us (level)
  transfers between devices with their start and end apart: 10 -> 10, of which waited for: 6 -> 6; matrix products, arithmetic and copies ran while one was open for 6% -> 7% of each run, Pallas kernels for 0% -> 0%
where the time goes in v4:
time: 114 us; the launch traced here: 113 us
  starting transfers between devices  44.8 us (39%)
  matrix products  28.1 us (25%)
  waiting for transfers between devices  20.8 us (18%)
  blocking collectives  9.26 us (8%)
  other arithmetic  7.07 us (6%)
  local copies, waits for them, and re-layouts  1.73 us (2%)
  between operations  1.24 us (1%)
    ppermute x3, starting transfers between devices, extended_2(): lax.ppermute(lax.slice_in_dim(block, 0, width, axis=dim), axis, backward)  27.1 us
    dot_general x22, matrix products, matmul(): return jnp.dot(left, right, precision=precision)  21.9 us
    ppermute x2, waiting for transfers between devices, fold_halo(): from_low = lax.ppermute(grad[2], axis, forward)  11.4 us
    ppermute x2, starting transfers between devices, fold_halo(): from_high = lax.ppermute(grad[0], axis, backward)  11.3 us
    all_to_all x1, blocking collectives, per_device(): lax.all_to_all(outgoing, 'gz', split_axis=0, concat_axis=0, tiled=True)  9.26 us
    ppermute x3, waiting for transfers between devices, extended_2(): lax.ppermute(lax.slice_in_dim(block, block.shape[dim] - width, None, axis...  8.02 us
    dot_general x7, matrix products, matmul_t(): lax.dot_general(left, right, (((1,), (1,)), ((), ())), precision=precision)  6.19 us
    ppermute x3, starting transfers between devices, extended_2(): lax.ppermute(lax.slice_in_dim(block, block.shape[dim] - width, None, axis...  4.43 us
  transfers between devices with their start and end apart: 10, of which 6 were waited for; matrix products, arithmetic and copies ran while one was open for 7% of the time, Pallas kernels for 0%

profile of v4, /device:TPU:2, one launch (start us, length us, event | category | flops | bytes accessed | tf_op | source)
XLA Modules:
  0.0 113.0 jit_solution(10690701089181604313)
XLA Ops:
  0.0 10.3 %collective-permute-start.1 = (f32[1,1,1,3,256]{4,2,3,1,0:T(1,128)}, f32[1,1,1,3,256]{4,2,3,1,0:T(1,128)S(1)}, u32[]{:S(2)}, u32[]{:S(2)}) collective-permute-start(f32[1,1,1,3,256]{4,2,3,1,0:T(1,128)} %param.16), channel_id=1, source_target_pairs={{64,0},{128,64},{192,128},{256,192},{320,256},{384,320},{448,384},... | collective-permute-start | bytes 9224 | tf_op jit(solution)/shard_map/ppermute | solution.py:24
  10.3 1.9 %collective-permute-start = (f32[1,1,1,3,256]{4,2,3,1,0:T(1,128)}, f32[1,1,1,3,256]{4,2,3,1,0:T(1,128)S(1)}, u32[]{:S(2)}, u32[]{:S(2)}) collective-permute-start(f32[1,1,1,3,256]{4,2,3,1,0:T(1,128)} %param.16), channel_id=1, source_target_pairs={{0,64},{64,128},{128,192},{192,256},{256,320},{320,384},{384,448},... | collective-permute-start | bytes 9224 | tf_op jit(solution)/shard_map/ppermute | solution.py:21
  17.0 1.1 fusion.39
  18.2 1.3 %fusion.113 = f32[1536,256]{0,1:T(8,128)S(1)} fusion(f32[256,4]{0,1:T(4,128)} %param.24, s32[1536]{0:T(1024)S(1)} %get-tuple-element.26), kind=kOutput, calls=%fused_computation.178 | convolution fusion | flops 9443328 | bytes 1583104 | tf_op jit(solution)/shard_map/jvp()/dot_general | solution.py:39
  19.6 2.4 %collective-permute-done = f32[1,1,1,3,256]{4,2,3,1,0:T(1,128)S(1)} collective-permute-done((f32[1,1,1,3,256]{4,2,3,1,0:T(1,128)}, f32[1,1,1,3,256]{4,2,3,1,0:T(1,128)S(1)}, u32[]{:S(2)}, u32[]{:S(2)}) %collective-permute-start) | collective-permute-done | bytes 3104 | tf_op jit(solution)/shard_map/ppermute | solution.py:21
  22.1 13.4 %collective-permute-start.3 = (f32[3,1,1,3,256]{4,2,3,1,0:T(1,128)S(1)}, f32[3,1,1,3,256]{4,2,3,1,0:T(1,128)S(1)}, u32[]{:S(2)}, u32[]{:S(2)}) collective-permute-start(f32[3,1,1,3,256]{4,2,3,1,0:T(1,128)S(1)} %constant_dynamic-update-slice_fusion), channel_id=1, source_target_pairs={{4,0},{8,4},{12,8},{16,12},{20,16},{24,20},{28,24},{32,28},{36,32}... | collective-permute-start | bytes 27656 | tf_op jit(solution)/shard_map/ppermute | solution.py:24
  35.5 1.4 %collective-permute-done.3 = f32[3,1,1,3,256]{4,2,3,1,0:T(1,128)S(1)} collective-permute-done((f32[3,1,1,3,256]{4,2,3,1,0:T(1,128)S(1)}, f32[3,1,1,3,256]{4,2,3,1,0:T(1,128)S(1)}, u32[]{:S(2)}, u32[]{:S(2)}) %collective-permute-start.3) | collective-permute-done | bytes 9248 | tf_op jit(solution)/shard_map/ppermute | solution.py:24
  36.9 2.9 %collective-permute-done.2 = f32[3,1,1,3,256]{4,2,3,1,0:T(1,128)S(1)} collective-permute-done((f32[3,1,1,3,256]{4,2,3,1,0:T(1,128)S(1)}, f32[3,1,1,3,256]{4,2,3,1,0:T(1,128)S(1)}, u32[]{:S(2)}, u32[]{:S(2)}) %collective-permute-start.2) | collective-permute-done | bytes 9248 | tf_op jit(solution)/shard_map/ppermute | solution.py:21
  39.9 3.3 %collective-permute-start.5 = (f32[3,3,1,4,256]{4,2,3,1,0:T(1,128)S(1)}, f32[3,3,1,4,256]{4,2,3,1,0:T(1,128)S(1)}, u32[]{:S(2)}, u32[]{:S(2)}) collective-permute-start(f32[3,3,1,4,256]{4,2,3,1,0:T(1,128)S(1)} %pad_maximum_fusion.6), channel_id=1, source_target_pairs={{1,0},{2,1},{3,2},{0,3},{5,4},{6,5},{7,6},{4,7},{9,8},{10,9},{11,1... | collective-permute-start | bytes 110600 | tf_op jit(solution)/shard_map/ppermute | solution.py:24
  43.2 2.5 %collective-permute-start.4 = (f32[3,3,1,4,256]{4,2,3,1,0:T(1,128)S(1)}, f32[3,3,1,4,256]{4,2,3,1,0:T(1,128)S(1)}, u32[]{:S(2)}, u32[]{:S(2)}) collective-permute-start(f32[3,3,1,4,256]{4,2,3,1,0:T(1,128)S(1)} %pad_maximum_fusion.6), channel_id=1, source_target_pairs={{0,1},{1,2},{2,3},{3,0},{4,5},{5,6},{6,7},{7,4},{8,9},{9,10},{10,1... | collective-permute-start | bytes 110600 | tf_op jit(solution)/shard_map/ppermute | solution.py:21
  46.4 2.7 %collective-permute-done.4 = f32[3,3,1,4,256]{4,2,3,1,0:T(1,128)S(1)} collective-permute-done((f32[3,3,1,4,256]{4,2,3,1,0:T(1,128)S(1)}, f32[3,3,1,4,256]{4,2,3,1,0:T(1,128)S(1)}, u32[]{:S(2)}, u32[]{:S(2)}) %collective-permute-start.4) | collective-permute-done | bytes 36896 | tf_op jit(solution)/shard_map/ppermute | solution.py:21
  50.9 0.9 fusion.93
  52.3 1.2 %broadcast_multiply_fusion = (f32[256,1536]{1,0:T(8,128)S(1)}, f32[256,1536]{1,0:T(8,128)S(1)}) fusion(f32[1536]{0:T(1024)S(1)} %get-tuple-element.45, f32[1536,256]{0,1:T(8,128)S(1)} %fusion.113, f32[1536,256]{0,1:T(8,128)S(1)} %fusion.93, f32[4,1536]{1,0:T(4,128)S(1)} %fusion.39, f32[256,4]{0,1:T(4,128)S(1)} %copy-done.6), kind=kOutput, calls=%fused_computation.85 | convolution fusion | flops 12189696 | bytes 6326272 | tf_op jit(solution)/shard_map/jvp()/dot_general | solution.py:39
  55.5 1.4 %fusion.37 = f32[96,1536]{1,0:T(8,128)S(1)} fusion(f32[96,256]{1,0:T(8,128)S(1)} %fusion.47, s32[1536]{0:T(1024)S(1)} %get-tuple-element.28), kind=kOutput, calls=%fused_computation.62 | convolution fusion | flops 226885632 | bytes 694272 | tf_op jit(solution)/shard_map/jvp()/dot_general | solution.py:43
  57.0 1.8 %multiply_add_fusion = (f32[256,1536]{1,0:T(8,128)S(1)}, f32[256,1536]{1,0:T(8,128)S(1)}) fusion(f32[256,1536]{1,0:T(8,128)S(1)} %get-tuple-element.53, f32[1536]{0:T(1024)S(1)} %get-tuple-element.45, f32[2,256,288]{1,2,0:T(8,128)S(1)} %copy-done.5, f32[32,1536]{1,0:T(8,128)S(1)} %multiply_reduce_fusion.11), kind=kOutput, calls=%fused_computation.49 | convolution fusion | flops 682278912 | bytes 6791168 | tf_op jit(solution)/shard_map/jvp()/dot_general | solution.py:39
  59.9 1.2 %fusion.35 = f32[96,1536]{1,0:T(8,128)S(1)} fusion(f32[96,256]{1,0:T(8,128)S(1)} %fusion.48, s32[1536]{0:T(1024)S(1)} %get-tuple-element.28), kind=kOutput, calls=%fused_computation.60 | convolution fusion | flops 226885632 | bytes 694272 | tf_op jit(solution)/shard_map/jvp()/dot_general | solution.py:43
  61.3 1.7 %multiply_reduce_fusion.2 = (f32[1536]{0:T(1024)S(1)}, f32[256,1536]{1,0:T(8,128)S(1)}) fusion(f32[256]{0:T(256)S(1)} %copy-done.7, f32[2,256,288]{1,2,0:T(8,128)S(1)} %copy-done.5, f32[32,1536]{1,0:T(8,128)S(1)} %get-tuple-element.33, f32[256,1536]{1,0:T(8,128)S(1)} %get-tuple-element.57), kind=kOutput, calls=%fused_computation.44 | convolution fusion | flops 682277376 | bytes 3644416 | tf_op jit(solution)/shard_map/jvp()/dot_general | solution.py:39
  63.1 1.4 %convolution_bitcast_fusion.1 = f32[288,1536]{1,0:T(8,128)S(1)} fusion(f32[256,1536]{1,0:T(8,128)S(1)} %get-tuple-element.62, f32[256]{0:T(256)S(1)} %copy-done.7, f32[1536]{0:T(1024)S(1)} %get-tuple-element.45, f32[2,256,288]{1,2,0:T(8,128)S(1)} %copy-done.5), kind=kOutput, calls=%fused_computation.3 | convolution fusion | flops 683409408 | bytes 3646464 | tf_op jit(solution)/shard_map/transpose(jvp())/dot_general | solution.py:39
  65.2 1.2 %fusion.33 = f32[96,1536]{1,0:T(8,128)S(1)} fusion(f32[96,256]{1,0:T(8,128)S(1)} %fusion.49, s32[1536]{0:T(1024)S(1)} %get-tuple-element.28), kind=kOutput, calls=%fused_computation.58 | convolution fusion | flops 226885632 | bytes 694272 | tf_op jit(solution)/shard_map/transpose(jvp())/dot_general | solution.py:39
  66.5 1.2 %multiply_reduce_fusion.1 = (f32[1536]{0:T(1024)S(1)}, f32[256,1536]{1,0:T(8,128)S(1)}) fusion(f32[256,1536]{1,0:T(8,128)S(1)} %get-tuple-element.58, f32[32,1536]{1,0:T(8,128)S(1)} %get-tuple-element.23, f32[2,32,256]{2,1,0:T(8,128)S(1)} %copy-done.1, f32[288,1536]{1,0:T(8,128)S(1)} %convolution_bitcast_fusion.1, f32[256]{0:T(256)S(1)} %copy-done.7), kind=kOutput, calls=%fused_computation.43 | convolution fusion | flops 78641664 | bytes 4955136 | tf_op jit(solution)/shard_map/transpose(jvp())/dot_general | solution.py:39
  67.8 1.4 %convolution_bitcast_fusion = f32[288,1536]{1,0:T(8,128)S(1)} fusion(f32[256,1536]{1,0:T(8,128)S(1)} %get-tuple-element.58, f32[256,1536]{1,0:T(8,128)S(1)} %get-tuple-element.64, f32[1536]{0:T(1024)S(1)} %get-tuple-element.45, f32[2,256,288]{1,2,0:T(8,128)S(1)} %copy-done.5), kind=kOutput, calls=%fused_computation.2 | convolution fusion | flops 683409408 | bytes 5218304 | tf_op jit(solution)/shard_map/transpose(jvp())/dot_general | solution.py:39
  69.9 1.4 %fusion.31 = f32[96,1536]{1,0:T(8,128)S(1)} fusion(f32[96,256]{1,0:T(8,128)S(1)} %fusion.50, s32[1536]{0:T(1024)S(1)} %get-tuple-element.28), kind=kOutput, calls=%fused_computation.56 | convolution fusion | flops 226885632 | bytes 694272 | tf_op jit(solution)/shard_map/transpose(jvp())/dot_general | solution.py:39
  72.0 1.0 fusion.4
  73.0 1.2 %multiply_reduce_fusion = (f32[1536]{0:T(1024)S(1)}, f32[256,1536]{1,0:T(8,128)S(1)}) fusion(f32[256,1536]{1,0:T(8,128)S(1)} %get-tuple-element.54, f32[256,1536]{1,0:T(8,128)S(1)} %fusion.4, f32[32,1536]{1,0:T(8,128)S(1)} %get-tuple-element.21, f32[2,32,256]{2,1,0:T(8,128)S(1)} %copy-done.1), kind=kOutput, calls=%fused_computation.42 | convolution fusion | flops 78248448 | bytes 4954112 | tf_op jit(solution)/shard_map/transpose(jvp())/dot_general | solution.py:39
  74.2 1.1 fusion.91
  75.3 1.0 fusion.41
  77.0 8.4 %collective-permute-start.7 = (f32[3,3,3,256]{3,2,1,0:T(4,128)S(1)}, f32[3,3,3,256]{3,2,1,0:T(4,128)S(1)}, u32[]{:S(2)}, u32[]{:S(2)}) collective-permute-start(f32[3,3,3,256]{3,2,1,0:T(4,128)S(1)} %bitcast.199), channel_id=1, source_target_pairs={{64,0},{128,64},{192,128},{256,192},{320,256},{384,320},{448,384},... | collective-permute-start | bytes 82952 | tf_op jit(solution)/shard_map/ppermute | solution.py:33
  85.4 1.9 %collective-permute-start.6 = (f32[3,3,3,256]{3,2,1,0:T(4,128)S(1)}, f32[3,3,3,256]{3,2,1,0:T(4,128)S(1)}, u32[]{:S(2)}, u32[]{:S(2)}) collective-permute-start(f32[3,3,3,256]{3,2,1,0:T(4,128)S(1)} %bitcast.198), channel_id=1, source_target_pairs={{0,64},{64,128},{128,192},{192,256},{256,320},{320,384},{384,448},... | collective-permute-start | bytes 82952 | tf_op jit(solution)/shard_map/ppermute | solution.py:32
  87.6 10.1 %collective-permute-done.6 = f32[3,3,3,256]{3,2,1,0:T(4,128)S(1)} collective-permute-done((f32[3,3,3,256]{3,2,1,0:T(4,128)S(1)}, f32[3,3,3,256]{3,2,1,0:T(4,128)S(1)}, u32[]{:S(2)}, u32[]{:S(2)}) %collective-permute-start.6) | collective-permute-done | bytes 27680 | tf_op jit(solution)/shard_map/ppermute | solution.py:32
  97.7 2.9 %collective-permute-start.9 = (f32[3,3,256]{2,1,0:T(4,128)S(1)}, f32[3,3,256]{2,1,0:T(4,128)S(1)}, u32[]{:S(2)}, u32[]{:S(2)}) collective-permute-start(f32[3,3,256]{2,1,0:T(4,128)S(1)} %get-tuple-element.39), channel_id=1, source_target_pairs={{4,0},{8,4},{12,8},{16,12},{20,16},{24,20},{28,24},{32,28},{36,32}... | collective-permute-start | bytes 27656 | tf_op jit(solution)/shard_map/ppermute | solution.py:33
  100.8 1.3 %collective-permute-done.8 = f32[3,3,256]{2,1,0:T(4,128)S(1)} collective-permute-done((f32[3,3,256]{2,1,0:T(4,128)S(1)}, f32[3,3,256]{2,1,0:T(4,128)S(1)}, u32[]{:S(2)}, u32[]{:S(2)}) %collective-permute-start.8) | collective-permute-done | bytes 9248 | tf_op jit(solution)/shard_map/ppermute | solution.py:32
  102.3 9.3 %all_to_all.5 = f32[4,4,11,128]{3,1,2,0:T(4,128)S(1)} all-to-all(f32[4,4,11,128]{3,1,2,0:T(4,128)S(1)} %pad_maximum_fusion.5), channel_id=1, replica_groups=mesh['gx'=16,'gy'=16,'gz'=4] {'gz'}, dimensions={0} | all-to-all | bytes 180224 | tf_op jit(solution)/shard_map/all_to_all | solution.py:185
  (99 shorter events, 15.2 us)
Async XLA Ops:
  0.0 53.6 %copy-start = (f32[32,256]{1,0:T(8,128)S(1)}, f32[32,256]{1,0:T(8,128)}, u32[]{:S(2)}) copy-start(f32[32,256]{1,0:T(8,128)} %param.27) | copy-start | bytes 98308
  0.0 22.1 %copy-start.3 = (f32[1,1,1,3,256]{4,2,3,1,0:T(1,128)S(1)}, f32[1,1,1,3,256]{4,2,3,1,0:T(1,128)}, u32[]{:S(2)}) copy-start(f32[1,1,1,3,256]{4,2,3,1,0:T(1,128)} %param.16) | copy-start | bytes 9220
  0.0 22.1 %collective-permute-start.1 = (f32[1,1,1,3,256]{4,2,3,1,0:T(1,128)}, f32[1,1,1,3,256]{4,2,3,1,0:T(1,128)S(1)}, u32[]{:S(2)}, u32[]{:S(2)}) collective-permute-start(f32[1,1,1,3,256]{4,2,3,1,0:T(1,128)} %param.16), channel_id=1, source_target_pairs={{64,0},{128,64},{192,128},{256,192},{320,256},{384,320},{448,384},... | collective-permute-start | bytes 9224 | tf_op jit(solution)/shard_map/ppermute | solution.py:24
  10.3 11.7 %collective-permute-start = (f32[1,1,1,3,256]{4,2,3,1,0:T(1,128)}, f32[1,1,1,3,256]{4,2,3,1,0:T(1,128)S(1)}, u32[]{:S(2)}, u32[]{:S(2)}) collective-permute-start(f32[1,1,1,3,256]{4,2,3,1,0:T(1,128)} %param.16), channel_id=1, source_target_pairs={{0,64},{64,128},{128,192},{192,256},{256,320},{320,384},{384,448},... | collective-permute-start | bytes 9224 | tf_op jit(solution)/shard_map/ppermute | solution.py:21
  18.2 32.7 %copy-start.4 = (f32[256,8]{0,1:T(8,128)S(1)}, f32[256,8]{0,1:T(8,128)}, u32[]{:S(2)}) copy-start(f32[256,8]{0,1:T(8,128)} %param.22) | copy-start | bytes 24580
  22.1 14.8 %collective-permute-start.3 = (f32[3,1,1,3,256]{4,2,3,1,0:T(1,128)S(1)}, f32[3,1,1,3,256]{4,2,3,1,0:T(1,128)S(1)}, u32[]{:S(2)}, u32[]{:S(2)}) collective-permute-start(f32[3,1,1,3,256]{4,2,3,1,0:T(1,128)S(1)} %constant_dynamic-update-slice_fusion), channel_id=1, source_target_pairs={{4,0},{8,4},{12,8},{16,12},{20,16},{24,20},{28,24},{32,28},{36,32}... | collective-permute-start | bytes 27656 | tf_op jit(solution)/shard_map/ppermute | solution.py:24
  35.5 4.3 %collective-permute-start.2 = (f32[3,1,1,3,256]{4,2,3,1,0:T(1,128)S(1)}, f32[3,1,1,3,256]{4,2,3,1,0:T(1,128)S(1)}, u32[]{:S(2)}, u32[]{:S(2)}) collective-permute-start(f32[3,1,1,3,256]{4,2,3,1,0:T(1,128)S(1)} %constant_dynamic-update-slice_fusion), channel_id=1, source_target_pairs={{0,4},{4,8},{8,12},{12,16},{16,20},{20,24},{24,28},{28,32},{32,36}... | collective-permute-start | bytes 27656 | tf_op jit(solution)/shard_map/ppermute | solution.py:21
  39.9 6.5 %collective-permute-start.5 = (f32[3,3,1,4,256]{4,2,3,1,0:T(1,128)S(1)}, f32[3,3,1,4,256]{4,2,3,1,0:T(1,128)S(1)}, u32[]{:S(2)}, u32[]{:S(2)}) collective-permute-start(f32[3,3,1,4,256]{4,2,3,1,0:T(1,128)S(1)} %pad_maximum_fusion.6), channel_id=1, source_target_pairs={{1,0},{2,1},{3,2},{0,3},{5,4},{6,5},{7,6},{4,7},{9,8},{10,9},{11,1... | collective-permute-start | bytes 110600 | tf_op jit(solution)/shard_map/ppermute | solution.py:24
  43.2 5.9 %collective-permute-start.4 = (f32[3,3,1,4,256]{4,2,3,1,0:T(1,128)S(1)}, f32[3,3,1,4,256]{4,2,3,1,0:T(1,128)S(1)}, u32[]{:S(2)}, u32[]{:S(2)}) collective-permute-start(f32[3,3,1,4,256]{4,2,3,1,0:T(1,128)S(1)} %pad_maximum_fusion.6), channel_id=1, source_target_pairs={{0,1},{1,2},{2,3},{3,0},{4,5},{5,6},{6,7},{7,4},{8,9},{9,10},{10,1... | collective-permute-start | bytes 110600 | tf_op jit(solution)/shard_map/ppermute | solution.py:21
  49.2 2.7 %copy-start.2 = (f32[32,8]{0,1:T(8,128)S(1)}, f32[32,8]{0,1:T(8,128)}, u32[]{:S(2)}) copy-start(f32[32,8]{0,1:T(8,128)} %param.25) | copy-start | bytes 3076
  49.2 3.1 %copy-start.6 = (f32[256,4]{0,1:T(4,128)S(1)}, f32[256,4]{0,1:T(4,128)}, u32[]{:S(2)}) copy-start(f32[256,4]{0,1:T(4,128)} %param.23) | copy-start | bytes 12292
  53.6 0.8 copy-start.1
  55.0 2.1 %copy-start.5 = (f32[2,256,288]{1,2,0:T(8,128)S(1)}, f32[2,256,288]{1,2,0:T(8,128)}, u32[]{:S(2)}) copy-start(f32[2,256,288]{1,2,0:T(8,128)} %param.28) | copy-start | bytes 1769476
  59.9 1.4 %copy-start.7 = (f32[256]{0:T(256)S(1)}, f32[256]{0:T(256)}, u32[]{:S(2)}) copy-start(f32[256]{0:T(256)} %param.29) | copy-start | bytes 3076
  77.0 10.6 %collective-permute-start.7 = (f32[3,3,3,256]{3,2,1,0:T(4,128)S(1)}, f32[3,3,3,256]{3,2,1,0:T(4,128)S(1)}, u32[]{:S(2)}, u32[]{:S(2)}) collective-permute-start(f32[3,3,3,256]{3,2,1,0:T(4,128)S(1)} %bitcast.199), channel_id=1, source_target_pairs={{64,0},{128,64},{192,128},{256,192},{320,256},{384,320},{448,384},... | collective-permute-start | bytes 82952 | tf_op jit(solution)/shard_map/ppermute | solution.py:33
  85.4 12.3 %collective-permute-start.6 = (f32[3,3,3,256]{3,2,1,0:T(4,128)S(1)}, f32[3,3,3,256]{3,2,1,0:T(4,128)S(1)}, u32[]{:S(2)}, u32[]{:S(2)}) collective-permute-start(f32[3,3,3,256]{3,2,1,0:T(4,128)S(1)} %bitcast.198), channel_id=1, source_target_pairs={{0,64},{64,128},{128,192},{192,256},{256,320},{320,384},{384,448},... | collective-permute-start | bytes 82952 | tf_op jit(solution)/shard_map/ppermute | solution.py:32
  97.7 4.3 %collective-permute-start.8 = (f32[3,3,256]{2,1,0:T(4,128)S(1)}, f32[3,3,256]{2,1,0:T(4,128)S(1)}, u32[]{:S(2)}, u32[]{:S(2)}) collective-permute-start(f32[3,3,256]{2,1,0:T(4,128)S(1)} %get-tuple-element.38), channel_id=1, source_target_pairs={{0,4},{4,8},{8,12},{12,16},{16,20},{20,24},{24,28},{28,32},{32,36}... | collective-permute-start | bytes 27656 | tf_op jit(solution)/shard_map/ppermute | solution.py:32
  97.7 4.3 %collective-permute-start.9 = (f32[3,3,256]{2,1,0:T(4,128)S(1)}, f32[3,3,256]{2,1,0:T(4,128)S(1)}, u32[]{:S(2)}, u32[]{:S(2)}) collective-permute-start(f32[3,3,256]{2,1,0:T(4,128)S(1)} %get-tuple-element.39), channel_id=1, source_target_pairs={{4,0},{8,4},{12,8},{16,12},{20,16},{24,20},{28,24},{32,28},{36,32}... | collective-permute-start | bytes 27656 | tf_op jit(solution)/shard_map/ppermute | solution.py:33

commit v5 on v4

--- a/solution.py
+++ b/solution.py
@@ -2,6 +2,7 @@
 import jax.numpy as jnp
 from jax import lax
 from jax.sharding import PartitionSpec as P
+
 
 CUTOFF = 5.0
 ENV_SCALE = 0.4
@@ -179,16 +180,17 @@
     own_blocks = own_rows.reshape(8, blocks_count, 128).transpose(1, 0, 2)
     hits = (own_owners[:, None] == receivers[None]).astype(jnp.float32)
     own_out = jnp.sum(hits[:, :, None, None] * own_blocks[:, None], axis=0)
-    at_self = (sources == myself).astype(jnp.float32)
-    own_out = at_self[None, :, None, None] * own_out[:, None]
-    outgoing = jnp.concatenate([grad_out, own_out], axis=2)
+    outgoing = jnp.concatenate(
+        [grad_out.reshape(zcount, zcount * 3, 128), own_out], axis=1
+    )
     arrived = lax.all_to_all(outgoing, "gz", split_axis=0, concat_axis=0, tiled=True)
-    gathered = jnp.sum(arrived, axis=0)
-    forces = -gathered[:, 0:3]
-    old_pos = gathered[:, 3:6]
-    old_vel = gathered[:, 6:9]
-    arrived_mass = gathered[:, 9:10]
-    flags = gathered[:, 10, 0]
+    grad_in = jnp.sum(arrived[:, : zcount * 3], axis=0).reshape(zcount, 3, 128)
+    own_in = arrived[:, zcount * 3 :]
+    forces = -grad_in
+    old_pos = own_in[:, 0:3]
+    old_vel = own_in[:, 3:6]
+    arrived_mass = own_in[:, 6:7]
+    flags = own_in[:, 7, 0]
     new_vel = old_vel + TIME_STEP * forces * arrived_mass
     new_pos = old_pos + TIME_STEP * new_vel
     state = jnp.concatenate([new_pos, new_vel, forces], axis=1)
@@ -215,6 +217,7 @@
         P(),
     )
     out_specs = P("gx", "gy", "gz", None, None, None)
+
     return jax.shard_map(
         per_device, mesh=mesh, in_specs=in_specs, out_specs=out_specs, check_vma=False
     )

time: 114 us -> 113 us (level)
  other arithmetic: 7.07 us -> 5.8 us
where the time goes in v5:
time: 113 us; the launch traced here: 112 us
  starting transfers between devices  44.7 us (40%)
  matrix products  28.1 us (25%)
  waiting for transfers between devices  20.9 us (18%)
  blocking collectives  8.92 us (8%)
  other arithmetic  5.8 us (5%)
  local copies, waits for them, and re-layouts  2.43 us (2%)
  between operations  1.26 us (1%)
    ppermute x3, starting transfers between devices, extended_2(): lax.ppermute(lax.slice_in_dim(block, 0, width, axis=dim), axis, backward)  27.1 us
    dot_general x22, matrix products, matmul(): return jnp.dot(left, right, precision=precision)  21.9 us
    ppermute x2, waiting for transfers between devices, fold_halo(): from_low = lax.ppermute(grad[2], axis, forward)  11.4 us
    ppermute x2, starting transfers between devices, fold_halo(): from_high = lax.ppermute(grad[0], axis, backward)  11.2 us
    all_to_all x1, blocking collectives, per_device(): lax.all_to_all(outgoing, 'gz', split_axis=0, concat_axis=0, tiled=True)  8.92 us
    ppermute x3, waiting for transfers between devices, extended_2(): lax.ppermute(lax.slice_in_dim(block, block.shape[dim] - width, None, axis...  8.11 us
    dot_general x7, matrix products, matmul_t(): lax.dot_general(left, right, (((1,), (1,)), ((), ())), precision=precision)  6.19 us
    ppermute x3, starting transfers between devices, extended_2(): lax.ppermute(lax.slice_in_dim(block, block.shape[dim] - width, None, axis...  4.43 us
  transfers between devices with their start and end apart: 10, of which 6 were waited for; matrix products, arithmetic and copies ran while one was open for 7% of the time, Pallas kernels for 0%

profile of v5, /device:TPU:2, one launch (start us, length us, event | category | flops | bytes accessed | tf_op | source)
XLA Modules:
  0.0 112.1 jit_solution(10550752046060221617)
XLA Ops:
  0.0 10.3 %collective-permute-start.1 = (f32[1,1,1,3,256]{4,2,3,1,0:T(1,128)}, f32[1,1,1,3,256]{4,2,3,1,0:T(1,128)S(1)}, u32[]{:S(2)}, u32[]{:S(2)}) collective-permute-start(f32[1,1,1,3,256]{4,2,3,1,0:T(1,128)} %param.16), channel_id=1, source_target_pairs={{64,0},{128,64},{192,128},{256,192},{320,256},{384,320},{448,384},... | collective-permute-start | bytes 9224 | tf_op jit(solution)/shard_map/ppermute | solution.py:25
  10.3 1.9 %collective-permute-start = (f32[1,1,1,3,256]{4,2,3,1,0:T(1,128)}, f32[1,1,1,3,256]{4,2,3,1,0:T(1,128)S(1)}, u32[]{:S(2)}, u32[]{:S(2)}) collective-permute-start(f32[1,1,1,3,256]{4,2,3,1,0:T(1,128)} %param.16), channel_id=1, source_target_pairs={{0,64},{64,128},{128,192},{192,256},{256,320},{320,384},{384,448},... | collective-permute-start | bytes 9224 | tf_op jit(solution)/shard_map/ppermute | solution.py:22
  17.0 1.1 fusion.39
  18.1 1.3 %fusion.113 = f32[1536,256]{0,1:T(8,128)S(1)} fusion(f32[256,4]{0,1:T(4,128)} %param.24, s32[1536]{0:T(1024)S(1)} %get-tuple-element.26), kind=kOutput, calls=%fused_computation.179 | convolution fusion | flops 9443328 | bytes 1583104 | tf_op jit(solution)/shard_map/jvp()/dot_general | solution.py:40
  19.5 2.5 %collective-permute-done = f32[1,1,1,3,256]{4,2,3,1,0:T(1,128)S(1)} collective-permute-done((f32[1,1,1,3,256]{4,2,3,1,0:T(1,128)}, f32[1,1,1,3,256]{4,2,3,1,0:T(1,128)S(1)}, u32[]{:S(2)}, u32[]{:S(2)}) %collective-permute-start) | collective-permute-done | bytes 3104 | tf_op jit(solution)/shard_map/ppermute | solution.py:22
  22.1 13.4 %collective-permute-start.3 = (f32[3,1,1,3,256]{4,2,3,1,0:T(1,128)S(1)}, f32[3,1,1,3,256]{4,2,3,1,0:T(1,128)S(1)}, u32[]{:S(2)}, u32[]{:S(2)}) collective-permute-start(f32[3,1,1,3,256]{4,2,3,1,0:T(1,128)S(1)} %constant_dynamic-update-slice_fusion), channel_id=1, source_target_pairs={{4,0},{8,4},{12,8},{16,12},{20,16},{24,20},{28,24},{32,28},{36,32}... | collective-permute-start | bytes 27656 | tf_op jit(solution)/shard_map/ppermute | solution.py:25
  35.5 1.4 %collective-permute-done.3 = f32[3,1,1,3,256]{4,2,3,1,0:T(1,128)S(1)} collective-permute-done((f32[3,1,1,3,256]{4,2,3,1,0:T(1,128)S(1)}, f32[3,1,1,3,256]{4,2,3,1,0:T(1,128)S(1)}, u32[]{:S(2)}, u32[]{:S(2)}) %collective-permute-start.3) | collective-permute-done | bytes 9248 | tf_op jit(solution)/shard_map/ppermute | solution.py:25
  36.9 2.9 %collective-permute-done.2 = f32[3,1,1,3,256]{4,2,3,1,0:T(1,128)S(1)} collective-permute-done((f32[3,1,1,3,256]{4,2,3,1,0:T(1,128)S(1)}, f32[3,1,1,3,256]{4,2,3,1,0:T(1,128)S(1)}, u32[]{:S(2)}, u32[]{:S(2)}) %collective-permute-start.2) | collective-permute-done | bytes 9248 | tf_op jit(solution)/shard_map/ppermute | solution.py:22
  39.9 3.3 %collective-permute-start.5 = (f32[3,3,1,4,256]{4,2,3,1,0:T(1,128)S(1)}, f32[3,3,1,4,256]{4,2,3,1,0:T(1,128)S(1)}, u32[]{:S(2)}, u32[]{:S(2)}) collective-permute-start(f32[3,3,1,4,256]{4,2,3,1,0:T(1,128)S(1)} %pad_maximum_fusion.6), channel_id=1, source_target_pairs={{1,0},{2,1},{3,2},{0,3},{5,4},{6,5},{7,6},{4,7},{9,8},{10,9},{11,1... | collective-permute-start | bytes 110600 | tf_op jit(solution)/shard_map/ppermute | solution.py:25
  43.2 2.5 %collective-permute-start.4 = (f32[3,3,1,4,256]{4,2,3,1,0:T(1,128)S(1)}, f32[3,3,1,4,256]{4,2,3,1,0:T(1,128)S(1)}, u32[]{:S(2)}, u32[]{:S(2)}) collective-permute-start(f32[3,3,1,4,256]{4,2,3,1,0:T(1,128)S(1)} %pad_maximum_fusion.6), channel_id=1, source_target_pairs={{0,1},{1,2},{2,3},{3,0},{4,5},{5,6},{6,7},{7,4},{8,9},{9,10},{10,1... | collective-permute-start | bytes 110600 | tf_op jit(solution)/shard_map/ppermute | solution.py:22
  46.4 2.7 %collective-permute-done.4 = f32[3,3,1,4,256]{4,2,3,1,0:T(1,128)S(1)} collective-permute-done((f32[3,3,1,4,256]{4,2,3,1,0:T(1,128)S(1)}, f32[3,3,1,4,256]{4,2,3,1,0:T(1,128)S(1)}, u32[]{:S(2)}, u32[]{:S(2)}) %collective-permute-start.4) | collective-permute-done | bytes 36896 | tf_op jit(solution)/shard_map/ppermute | solution.py:22
  50.9 0.9 fusion.93
  52.3 1.2 %broadcast_multiply_fusion = (f32[256,1536]{1,0:T(8,128)S(1)}, f32[256,1536]{1,0:T(8,128)S(1)}) fusion(f32[1536]{0:T(1024)S(1)} %get-tuple-element.46, f32[1536,256]{0,1:T(8,128)S(1)} %fusion.113, f32[1536,256]{0,1:T(8,128)S(1)} %fusion.93, f32[4,1536]{1,0:T(4,128)S(1)} %fusion.39, f32[256,4]{0,1:T(4,128)S(1)} %copy-done.6), kind=kOutput, calls=%fused_computation.85 | convolution fusion | flops 12189696 | bytes 6326272 | tf_op jit(solution)/shard_map/jvp()/dot_general | solution.py:40
  55.5 1.4 %fusion.37 = f32[96,1536]{1,0:T(8,128)S(1)} fusion(f32[96,256]{1,0:T(8,128)S(1)} %fusion.47, s32[1536]{0:T(1024)S(1)} %get-tuple-element.28), kind=kOutput, calls=%fused_computation.62 | convolution fusion | flops 226885632 | bytes 694272 | tf_op jit(solution)/shard_map/jvp()/dot_general | solution.py:44
  57.0 1.8 %multiply_add_fusion = (f32[256,1536]{1,0:T(8,128)S(1)}, f32[256,1536]{1,0:T(8,128)S(1)}) fusion(f32[256,1536]{1,0:T(8,128)S(1)} %get-tuple-element.54, f32[1536]{0:T(1024)S(1)} %get-tuple-element.46, f32[2,256,288]{1,2,0:T(8,128)S(1)} %copy-done.5, f32[32,1536]{1,0:T(8,128)S(1)} %multiply_reduce_fusion.11), kind=kOutput, calls=%fused_computation.49 | convolution fusion | flops 682278912 | bytes 6791168 | tf_op jit(solution)/shard_map/jvp()/dot_general | solution.py:40
  59.9 1.2 %fusion.35 = f32[96,1536]{1,0:T(8,128)S(1)} fusion(f32[96,256]{1,0:T(8,128)S(1)} %fusion.48, s32[1536]{0:T(1024)S(1)} %get-tuple-element.28), kind=kOutput, calls=%fused_computation.60 | convolution fusion | flops 226885632 | bytes 694272 | tf_op jit(solution)/shard_map/jvp()/dot_general | solution.py:44
  61.3 1.7 %multiply_reduce_fusion.2 = (f32[1536]{0:T(1024)S(1)}, f32[256,1536]{1,0:T(8,128)S(1)}) fusion(f32[256]{0:T(256)S(1)} %copy-done.7, f32[2,256,288]{1,2,0:T(8,128)S(1)} %copy-done.5, f32[32,1536]{1,0:T(8,128)S(1)} %get-tuple-element.33, f32[256,1536]{1,0:T(8,128)S(1)} %get-tuple-element.58), kind=kOutput, calls=%fused_computation.44 | convolution fusion | flops 682277376 | bytes 3644416 | tf_op jit(solution)/shard_map/jvp()/dot_general | solution.py:40
  63.1 1.4 %convolution_bitcast_fusion.1 = f32[288,1536]{1,0:T(8,128)S(1)} fusion(f32[256,1536]{1,0:T(8,128)S(1)} %get-tuple-element.63, f32[256]{0:T(256)S(1)} %copy-done.7, f32[1536]{0:T(1024)S(1)} %get-tuple-element.46, f32[2,256,288]{1,2,0:T(8,128)S(1)} %copy-done.5), kind=kOutput, calls=%fused_computation.3 | convolution fusion | flops 683409408 | bytes 3646464 | tf_op jit(solution)/shard_map/transpose(jvp())/dot_general | solution.py:40
  65.2 1.2 %fusion.33 = f32[96,1536]{1,0:T(8,128)S(1)} fusion(f32[96,256]{1,0:T(8,128)S(1)} %fusion.49, s32[1536]{0:T(1024)S(1)} %get-tuple-element.28), kind=kOutput, calls=%fused_computation.58 | convolution fusion | flops 226885632 | bytes 694272 | tf_op jit(solution)/shard_map/transpose(jvp())/dot_general | solution.py:40
  66.5 1.2 %multiply_reduce_fusion.1 = (f32[1536]{0:T(1024)S(1)}, f32[256,1536]{1,0:T(8,128)S(1)}) fusion(f32[256,1536]{1,0:T(8,128)S(1)} %get-tuple-element.59, f32[32,1536]{1,0:T(8,128)S(1)} %get-tuple-element.23, f32[2,32,256]{2,1,0:T(8,128)S(1)} %copy-done.1, f32[288,1536]{1,0:T(8,128)S(1)} %convolution_bitcast_fusion.1, f32[256]{0:T(256)S(1)} %copy-done.7), kind=kOutput, calls=%fused_computation.43 | convolution fusion | flops 78641664 | bytes 4955136 | tf_op jit(solution)/shard_map/transpose(jvp())/dot_general | solution.py:40
  67.8 1.4 %convolution_bitcast_fusion = f32[288,1536]{1,0:T(8,128)S(1)} fusion(f32[256,1536]{1,0:T(8,128)S(1)} %get-tuple-element.59, f32[256,1536]{1,0:T(8,128)S(1)} %get-tuple-element.65, f32[1536]{0:T(1024)S(1)} %get-tuple-element.46, f32[2,256,288]{1,2,0:T(8,128)S(1)} %copy-done.5), kind=kOutput, calls=%fused_computation.2 | convolution fusion | flops 683409408 | bytes 5218304 | tf_op jit(solution)/shard_map/transpose(jvp())/dot_general | solution.py:40
  69.9 1.4 %fusion.31 = f32[96,1536]{1,0:T(8,128)S(1)} fusion(f32[96,256]{1,0:T(8,128)S(1)} %fusion.50, s32[1536]{0:T(1024)S(1)} %get-tuple-element.28), kind=kOutput, calls=%fused_computation.56 | convolution fusion | flops 226885632 | bytes 694272 | tf_op jit(solution)/shard_map/transpose(jvp())/dot_general | solution.py:40
  72.0 1.0 fusion.4
  73.0 1.1 %multiply_reduce_fusion = (f32[1536]{0:T(1024)S(1)}, f32[256,1536]{1,0:T(8,128)S(1)}) fusion(f32[256,1536]{1,0:T(8,128)S(1)} %get-tuple-element.55, f32[256,1536]{1,0:T(8,128)S(1)} %fusion.4, f32[32,1536]{1,0:T(8,128)S(1)} %get-tuple-element.21, f32[2,32,256]{2,1,0:T(8,128)S(1)} %copy-done.1), kind=kOutput, calls=%fused_computation.42 | convolution fusion | flops 78248448 | bytes 4954112 | tf_op jit(solution)/shard_map/transpose(jvp())/dot_general | solution.py:40
  74.2 1.1 fusion.91
  75.3 1.0 fusion.41
  77.0 8.3 %collective-permute-start.7 = (f32[3,3,3,256]{3,2,1,0:T(4,128)S(1)}, f32[3,3,3,256]{3,2,1,0:T(4,128)S(1)}, u32[]{:S(2)}, u32[]{:S(2)}) collective-permute-start(f32[3,3,3,256]{3,2,1,0:T(4,128)S(1)} %bitcast.197), channel_id=1, source_target_pairs={{64,0},{128,64},{192,128},{256,192},{320,256},{384,320},{448,384},... | collective-permute-start | bytes 82952 | tf_op jit(solution)/shard_map/ppermute | solution.py:34
  85.3 1.9 %collective-permute-start.6 = (f32[3,3,3,256]{3,2,1,0:T(4,128)S(1)}, f32[3,3,3,256]{3,2,1,0:T(4,128)S(1)}, u32[]{:S(2)}, u32[]{:S(2)}) collective-permute-start(f32[3,3,3,256]{3,2,1,0:T(4,128)S(1)} %bitcast.196), channel_id=1, source_target_pairs={{0,64},{64,128},{128,192},{192,256},{256,320},{320,384},{384,448},... | collective-permute-start | bytes 82952 | tf_op jit(solution)/shard_map/ppermute | solution.py:33
  87.5 10.1 %collective-permute-done.6 = f32[3,3,3,256]{3,2,1,0:T(4,128)S(1)} collective-permute-done((f32[3,3,3,256]{3,2,1,0:T(4,128)S(1)}, f32[3,3,3,256]{3,2,1,0:T(4,128)S(1)}, u32[]{:S(2)}, u32[]{:S(2)}) %collective-permute-start.6) | collective-permute-done | bytes 27680 | tf_op jit(solution)/shard_map/ppermute | solution.py:33
  97.7 2.9 %collective-permute-start.9 = (f32[3,3,256]{2,1,0:T(4,128)S(1)}, f32[3,3,256]{2,1,0:T(4,128)S(1)}, u32[]{:S(2)}, u32[]{:S(2)}) collective-permute-start(f32[3,3,256]{2,1,0:T(4,128)S(1)} %get-tuple-element.41), channel_id=1, source_target_pairs={{4,0},{8,4},{12,8},{16,12},{20,16},{24,20},{28,24},{32,28},{36,32}... | collective-permute-start | bytes 27656 | tf_op jit(solution)/shard_map/ppermute | solution.py:34
  100.7 1.3 %collective-permute-done.8 = f32[3,3,256]{2,1,0:T(4,128)S(1)} collective-permute-done((f32[3,3,256]{2,1,0:T(4,128)S(1)}, f32[3,3,256]{2,1,0:T(4,128)S(1)}, u32[]{:S(2)}, u32[]{:S(2)}) %collective-permute-start.8) | collective-permute-done | bytes 9248 | tf_op jit(solution)/shard_map/ppermute | solution.py:33
  102.3 8.9 %all_to_all.5 = f32[4,20,128]{2,1,0:T(8,128)S(1)} all-to-all(f32[4,20,128]{2,1,0:T(8,128)S(1)} %copy.65), channel_id=1, replica_groups=mesh['gx'=16,'gy'=16,'gz'=4] {'gz'}, dimensions={0} | all-to-all | bytes 81920 | tf_op jit(solution)/shard_map/all_to_all | solution.py:186
  (107 shorter events, 14.7 us)
Async XLA Ops:
  0.0 53.6 %copy-start = (f32[32,256]{1,0:T(8,128)S(1)}, f32[32,256]{1,0:T(8,128)}, u32[]{:S(2)}) copy-start(f32[32,256]{1,0:T(8,128)} %param.27) | copy-start | bytes 98308
  0.0 22.1 %copy-start.3 = (f32[1,1,1,3,256]{4,2,3,1,0:T(1,128)S(1)}, f32[1,1,1,3,256]{4,2,3,1,0:T(1,128)}, u32[]{:S(2)}) copy-start(f32[1,1,1,3,256]{4,2,3,1,0:T(1,128)} %param.16) | copy-start | bytes 9220
  0.0 22.1 %collective-permute-start.1 = (f32[1,1,1,3,256]{4,2,3,1,0:T(1,128)}, f32[1,1,1,3,256]{4,2,3,1,0:T(1,128)S(1)}, u32[]{:S(2)}, u32[]{:S(2)}) collective-permute-start(f32[1,1,1,3,256]{4,2,3,1,0:T(1,128)} %param.16), channel_id=1, source_target_pairs={{64,0},{128,64},{192,128},{256,192},{320,256},{384,320},{448,384},... | collective-permute-start | bytes 9224 | tf_op jit(solution)/shard_map/ppermute | solution.py:25
  10.3 11.7 %collective-permute-start = (f32[1,1,1,3,256]{4,2,3,1,0:T(1,128)}, f32[1,1,1,3,256]{4,2,3,1,0:T(1,128)S(1)}, u32[]{:S(2)}, u32[]{:S(2)}) collective-permute-start(f32[1,1,1,3,256]{4,2,3,1,0:T(1,128)} %param.16), channel_id=1, source_target_pairs={{0,64},{64,128},{128,192},{192,256},{256,320},{320,384},{384,448},... | collective-permute-start | bytes 9224 | tf_op jit(solution)/shard_map/ppermute | solution.py:22
  18.1 32.8 %copy-start.4 = (f32[256,8]{0,1:T(8,128)S(1)}, f32[256,8]{0,1:T(8,128)}, u32[]{:S(2)}) copy-start(f32[256,8]{0,1:T(8,128)} %param.22) | copy-start | bytes 24580
  22.1 14.8 %collective-permute-start.3 = (f32[3,1,1,3,256]{4,2,3,1,0:T(1,128)S(1)}, f32[3,1,1,3,256]{4,2,3,1,0:T(1,128)S(1)}, u32[]{:S(2)}, u32[]{:S(2)}) collective-permute-start(f32[3,1,1,3,256]{4,2,3,1,0:T(1,128)S(1)} %constant_dynamic-update-slice_fusion), channel_id=1, source_target_pairs={{4,0},{8,4},{12,8},{16,12},{20,16},{24,20},{28,24},{32,28},{36,32}... | collective-permute-start | bytes 27656 | tf_op jit(solution)/shard_map/ppermute | solution.py:25
  35.5 4.3 %collective-permute-start.2 = (f32[3,1,1,3,256]{4,2,3,1,0:T(1,128)S(1)}, f32[3,1,1,3,256]{4,2,3,1,0:T(1,128)S(1)}, u32[]{:S(2)}, u32[]{:S(2)}) collective-permute-start(f32[3,1,1,3,256]{4,2,3,1,0:T(1,128)S(1)} %constant_dynamic-update-slice_fusion), channel_id=1, source_target_pairs={{0,4},{4,8},{8,12},{12,16},{16,20},{20,24},{24,28},{28,32},{32,36}... | collective-permute-start | bytes 27656 | tf_op jit(solution)/shard_map/ppermute | solution.py:22
  39.9 6.5 %collective-permute-start.5 = (f32[3,3,1,4,256]{4,2,3,1,0:T(1,128)S(1)}, f32[3,3,1,4,256]{4,2,3,1,0:T(1,128)S(1)}, u32[]{:S(2)}, u32[]{:S(2)}) collective-permute-start(f32[3,3,1,4,256]{4,2,3,1,0:T(1,128)S(1)} %pad_maximum_fusion.6), channel_id=1, source_target_pairs={{1,0},{2,1},{3,2},{0,3},{5,4},{6,5},{7,6},{4,7},{9,8},{10,9},{11,1... | collective-permute-start | bytes 110600 | tf_op jit(solution)/shard_map/ppermute | solution.py:25
  43.2 5.9 %collective-permute-start.4 = (f32[3,3,1,4,256]{4,2,3,1,0:T(1,128)S(1)}, f32[3,3,1,4,256]{4,2,3,1,0:T(1,128)S(1)}, u32[]{:S(2)}, u32[]{:S(2)}) collective-permute-start(f32[3,3,1,4,256]{4,2,3,1,0:T(1,128)S(1)} %pad_maximum_fusion.6), channel_id=1, source_target_pairs={{0,1},{1,2},{2,3},{3,0},{4,5},{5,6},{6,7},{7,4},{8,9},{9,10},{10,1... | collective-permute-start | bytes 110600 | tf_op jit(solution)/shard_map/ppermute | solution.py:22
  49.2 2.7 %copy-start.2 = (f32[32,8]{0,1:T(8,128)S(1)}, f32[32,8]{0,1:T(8,128)}, u32[]{:S(2)}) copy-start(f32[32,8]{0,1:T(8,128)} %param.25) | copy-start | bytes 3076
  49.2 3.1 %copy-start.6 = (f32[256,4]{0,1:T(4,128)S(1)}, f32[256,4]{0,1:T(4,128)}, u32[]{:S(2)}) copy-start(f32[256,4]{0,1:T(4,128)} %param.23) | copy-start | bytes 12292
  53.6 0.8 copy-start.1
  55.0 2.1 %copy-start.5 = (f32[2,256,288]{1,2,0:T(8,128)S(1)}, f32[2,256,288]{1,2,0:T(8,128)}, u32[]{:S(2)}) copy-start(f32[2,256,288]{1,2,0:T(8,128)} %param.28) | copy-start | bytes 1769476
  59.9 1.4 %copy-start.7 = (f32[256]{0:T(256)S(1)}, f32[256]{0:T(256)}, u32[]{:S(2)}) copy-start(f32[256]{0:T(256)} %param.29) | copy-start | bytes 3076
  77.0 10.5 %collective-permute-start.7 = (f32[3,3,3,256]{3,2,1,0:T(4,128)S(1)}, f32[3,3,3,256]{3,2,1,0:T(4,128)S(1)}, u32[]{:S(2)}, u32[]{:S(2)}) collective-permute-start(f32[3,3,3,256]{3,2,1,0:T(4,128)S(1)} %bitcast.197), channel_id=1, source_target_pairs={{64,0},{128,64},{192,128},{256,192},{320,256},{384,320},{448,384},... | collective-permute-start | bytes 82952 | tf_op jit(solution)/shard_map/ppermute | solution.py:34
  85.3 12.3 %collective-permute-start.6 = (f32[3,3,3,256]{3,2,1,0:T(4,128)S(1)}, f32[3,3,3,256]{3,2,1,0:T(4,128)S(1)}, u32[]{:S(2)}, u32[]{:S(2)}) collective-permute-start(f32[3,3,3,256]{3,2,1,0:T(4,128)S(1)} %bitcast.196), channel_id=1, source_target_pairs={{0,64},{64,128},{128,192},{192,256},{256,320},{320,384},{384,448},... | collective-permute-start | bytes 82952 | tf_op jit(solution)/shard_map/ppermute | solution.py:33
  97.6 4.3 %collective-permute-start.8 = (f32[3,3,256]{2,1,0:T(4,128)S(1)}, f32[3,3,256]{2,1,0:T(4,128)S(1)}, u32[]{:S(2)}, u32[]{:S(2)}) collective-permute-start(f32[3,3,256]{2,1,0:T(4,128)S(1)} %get-tuple-element.40), channel_id=1, source_target_pairs={{0,4},{4,8},{8,12},{12,16},{16,20},{20,24},{24,28},{28,32},{32,36}... | collective-permute-start | bytes 27656 | tf_op jit(solution)/shard_map/ppermute | solution.py:33
  97.7 4.3 %collective-permute-start.9 = (f32[3,3,256]{2,1,0:T(4,128)S(1)}, f32[3,3,256]{2,1,0:T(4,128)S(1)}, u32[]{:S(2)}, u32[]{:S(2)}) collective-permute-start(f32[3,3,256]{2,1,0:T(4,128)S(1)} %get-tuple-element.41), channel_id=1, source_target_pairs={{4,0},{8,4},{12,8},{16,12},{20,16},{24,20},{28,24},{32,28},{36,32}... | collective-permute-start | bytes 27656 | tf_op jit(solution)/shard_map/ppermute | solution.py:34

commit v6 on v5

--- a/solution.py
+++ b/solution.py
@@ -42,6 +42,50 @@
 
 def matmul_t(left, right, precision=lax.Precision.HIGH):
     return lax.dot_general(left, right, (((1,), (1,)), ((), ())), precision=precision)
+
+
+def two_pass(left, right_bf16, dims):
+    high = left.astype(jnp.bfloat16)
+    low = (left - high.astype(jnp.float32)).astype(jnp.bfloat16)
+    first = lax.dot_general(high, right_bf16, dims, preferred_element_type=jnp.float32)
+    second = lax.dot_general(low, right_bf16, dims, preferred_element_type=jnp.float32)
+    return first + second
+
+
+PLAIN = (((1,), (0,)), ((), ()))
+TRANSPOSED = (((1,), (1,)), ((), ()))
+
+
+@jax.custom_vjp
+def sum_by_centre(spread, member_bf16):
+    return two_pass(spread, member_bf16, PLAIN)
+
+
+def sum_by_centre_fwd(spread, member_bf16):
+    return sum_by_centre(spread, member_bf16), member_bf16
+
+
+def sum_by_centre_bwd(member_bf16, cotangent):
+    return two_pass(cotangent, member_bf16, TRANSPOSED), None
+
+
+sum_by_centre.defvjp(sum_by_centre_fwd, sum_by_centre_bwd)
+
+
+@jax.custom_vjp
+def spread_to_pairs(environment, member_bf16):
+    return two_pass(environment, member_bf16, TRANSPOSED)
+
+
+def spread_to_pairs_fwd(environment, member_bf16):
+    return spread_to_pairs(environment, member_bf16), member_bf16
+
+
+def spread_to_pairs_bwd(member_bf16, cotangent):
+    return two_pass(cotangent, member_bf16, PLAIN), None
+
+
+spread_to_pairs.defvjp(spread_to_pairs_fwd, spread_to_pairs_bwd)
 
 
 def pair_energy(
@@ -103,11 +147,12 @@
     channels = vector_weight.shape[0]
     vectors = envelope[None, None] * matmul(vector_weight, basis)[None] * unit[:, None, :]
     n_layers = env_weight.shape[0]
+    member_bf16 = member.astype(jnp.bfloat16)
     for layer in range(n_layers):
         env_pairs = matmul(env_weight[layer], latent)
         spread = (unit[:, None, :] * env_pairs[None]).reshape(3 * channels, pair_count)
-        environment = ENV_SCALE * matmul(spread, member)
-        at_pairs = matmul_t(environment, member)
+        environment = ENV_SCALE * sum_by_centre(spread, member_bf16)
+        at_pairs = spread_to_pairs(environment, member_bf16)
         at_pairs = at_pairs.reshape(3, channels, pair_count)
         scalars = jnp.sum(vectors * at_pairs, axis=0)
         update = matmul(latent_weight[layer], jnp.concatenate([latent, scalars], axis=0))

time: 113 us -> 113 us (level)
    dot_general x0 -> x16, matrix products: none -> 7.11 us  [the longest x4 1.81 us: pair_energy(): environment = ENV_SCALE * sum_by_centre(spread, member_bf16)]
    dot_general x7 -> x3, matrix products: 6.19 us -> 2.59 us  [matmul_t(): lax.dot_general(left, right, (((1,), (1,)), ((), ())), precision=precision)]
    dot_general x22 -> x18, matrix products: 21.9 us -> 18.5 us  [matmul(): return jnp.dot(left, right, precision=precision)]
where the time goes in v6:
time: 113 us; the launch traced here: 112 us
  starting transfers between devices  44.7 us (40%)
  matrix products  28.2 us (25%)
  waiting for transfers between devices  20.9 us (18%)
  blocking collectives  8.92 us (8%)
  other arithmetic  5.89 us (5%)
  local copies, waits for them, and re-layouts  2.53 us (2%)
  between operations  1.3 us (1%)
    ppermute x3, starting transfers between devices, extended_2(): lax.ppermute(lax.slice_in_dim(block, 0, width, axis=dim), axis, backward)  27.1 us
    dot_general x18, matrix products, matmul(): return jnp.dot(left, right, precision=precision)  18.5 us
    ppermute x2, waiting for transfers between devices, fold_halo(): from_low = lax.ppermute(grad[2], axis, forward)  11.4 us
    ppermute x2, starting transfers between devices, fold_halo(): from_high = lax.ppermute(grad[0], axis, backward)  11.2 us
    all_to_all x1, blocking collectives, per_device(): lax.all_to_all(outgoing, 'gz', split_axis=0, concat_axis=0, tiled=True)  8.92 us
    ppermute x3, waiting for transfers between devices, extended_2(): lax.ppermute(lax.slice_in_dim(block, block.shape[dim] - width, None, axis...  8.11 us
    ppermute x3, starting transfers between devices, extended_2(): lax.ppermute(lax.slice_in_dim(block, block.shape[dim] - width, None, axis...  4.43 us
    dot_general x3, matrix products, matmul_t(): lax.dot_general(left, right, (((1,), (1,)), ((), ())), precision=precision)  2.59 us
  transfers between devices with their start and end apart: 10, of which 6 were waited for; matrix products, arithmetic and copies ran while one was open for 7% of the time, Pallas kernels for 0%

profile of v6, /device:TPU:2, one launch (start us, length us, event | category | flops | bytes accessed | tf_op | source)
XLA Modules:
  0.0 112.5 jit_solution(6787186637561120348)
XLA Ops:
  0.0 10.3 %collective-permute-start.1 = (f32[1,1,1,3,256]{4,2,3,1,0:T(1,128)}, f32[1,1,1,3,256]{4,2,3,1,0:T(1,128)S(1)}, u32[]{:S(2)}, u32[]{:S(2)}) collective-permute-start(f32[1,1,1,3,256]{4,2,3,1,0:T(1,128)} %param.16), channel_id=1, source_target_pairs={{64,0},{128,64},{192,128},{256,192},{320,256},{384,320},{448,384},... | collective-permute-start | bytes 9224 | tf_op jit(solution)/shard_map/ppermute | solution.py:25
  10.3 1.9 %collective-permute-start = (f32[1,1,1,3,256]{4,2,3,1,0:T(1,128)}, f32[1,1,1,3,256]{4,2,3,1,0:T(1,128)S(1)}, u32[]{:S(2)}, u32[]{:S(2)}) collective-permute-start(f32[1,1,1,3,256]{4,2,3,1,0:T(1,128)} %param.16), channel_id=1, source_target_pairs={{0,64},{64,128},{128,192},{192,256},{256,320},{320,384},{384,448},... | collective-permute-start | bytes 9224 | tf_op jit(solution)/shard_map/ppermute | solution.py:22
  12.3 0.8 convert_multiply_fusion
  13.0 0.8 slice_reduce_fusion.1
  16.1 0.8 maximum_bitcast_fusion.1
  17.0 1.1 fusion.43
  18.1 1.3 %fusion.143 = f32[1536,256]{0,1:T(8,128)S(1)} fusion(f32[256,4]{0,1:T(4,128)} %param.24, s32[1536]{0:T(1024)S(1)} %get-tuple-element.26), kind=kOutput, calls=%fused_computation.224 | convolution fusion | flops 9443328 | bytes 1583104 | tf_op jit(solution)/shard_map/jvp()/dot_general | solution.py:40
  19.5 2.5 %collective-permute-done = f32[1,1,1,3,256]{4,2,3,1,0:T(1,128)S(1)} collective-permute-done((f32[1,1,1,3,256]{4,2,3,1,0:T(1,128)}, f32[1,1,1,3,256]{4,2,3,1,0:T(1,128)S(1)}, u32[]{:S(2)}, u32[]{:S(2)}) %collective-permute-start) | collective-permute-done | bytes 3104 | tf_op jit(solution)/shard_map/ppermute | solution.py:22
  22.1 13.4 %collective-permute-start.3 = (f32[3,1,1,3,256]{4,2,3,1,0:T(1,128)S(1)}, f32[3,1,1,3,256]{4,2,3,1,0:T(1,128)S(1)}, u32[]{:S(2)}, u32[]{:S(2)}) collective-permute-start(f32[3,1,1,3,256]{4,2,3,1,0:T(1,128)S(1)} %constant_dynamic-update-slice_fusion), channel_id=1, source_target_pairs={{4,0},{8,4},{12,8},{16,12},{20,16},{24,20},{28,24},{32,28},{36,32}... | collective-permute-start | bytes 27656 | tf_op jit(solution)/shard_map/ppermute | solution.py:25
  35.5 1.4 %collective-permute-done.3 = f32[3,1,1,3,256]{4,2,3,1,0:T(1,128)S(1)} collective-permute-done((f32[3,1,1,3,256]{4,2,3,1,0:T(1,128)S(1)}, f32[3,1,1,3,256]{4,2,3,1,0:T(1,128)S(1)}, u32[]{:S(2)}, u32[]{:S(2)}) %collective-permute-start.3) | collective-permute-done | bytes 9248 | tf_op jit(solution)/shard_map/ppermute | solution.py:25
  36.9 2.9 %collective-permute-done.2 = f32[3,1,1,3,256]{4,2,3,1,0:T(1,128)S(1)} collective-permute-done((f32[3,1,1,3,256]{4,2,3,1,0:T(1,128)S(1)}, f32[3,1,1,3,256]{4,2,3,1,0:T(1,128)S(1)}, u32[]{:S(2)}, u32[]{:S(2)}) %collective-permute-start.2) | collective-permute-done | bytes 9248 | tf_op jit(solution)/shard_map/ppermute | solution.py:22
  39.9 3.3 %collective-permute-start.5 = (f32[3,3,1,4,256]{4,2,3,1,0:T(1,128)S(1)}, f32[3,3,1,4,256]{4,2,3,1,0:T(1,128)S(1)}, u32[]{:S(2)}, u32[]{:S(2)}) collective-permute-start(f32[3,3,1,4,256]{4,2,3,1,0:T(1,128)S(1)} %pad_maximum_fusion.6), channel_id=1, source_target_pairs={{1,0},{2,1},{3,2},{0,3},{5,4},{6,5},{7,6},{4,7},{9,8},{10,9},{11,1... | collective-permute-start | bytes 110600 | tf_op jit(solution)/shard_map/ppermute | solution.py:25
  43.2 2.5 %collective-permute-start.4 = (f32[3,3,1,4,256]{4,2,3,1,0:T(1,128)S(1)}, f32[3,3,1,4,256]{4,2,3,1,0:T(1,128)S(1)}, u32[]{:S(2)}, u32[]{:S(2)}) collective-permute-start(f32[3,3,1,4,256]{4,2,3,1,0:T(1,128)S(1)} %pad_maximum_fusion.6), channel_id=1, source_target_pairs={{0,1},{1,2},{2,3},{3,0},{4,5},{5,6},{6,7},{7,4},{8,9},{9,10},{10,1... | collective-permute-start | bytes 110600 | tf_op jit(solution)/shard_map/ppermute | solution.py:22
  46.4 2.7 %collective-permute-done.4 = f32[3,3,1,4,256]{4,2,3,1,0:T(1,128)S(1)} collective-permute-done((f32[3,3,1,4,256]{4,2,3,1,0:T(1,128)S(1)}, f32[3,3,1,4,256]{4,2,3,1,0:T(1,128)S(1)}, u32[]{:S(2)}, u32[]{:S(2)}) %collective-permute-start.4) | collective-permute-done | bytes 36896 | tf_op jit(solution)/shard_map/ppermute | solution.py:22
  50.0 0.9 multiply_reduce_fusion.17
  50.9 0.9 fusion.115
  52.3 1.2 %broadcast_multiply_fusion = (f32[256,1536]{1,0:T(8,128)S(1)}, f32[256,1536]{1,0:T(8,128)S(1)}) fusion(f32[1536]{0:T(1024)S(1)} %get-tuple-element.50, f32[1536,256]{0,1:T(8,128)S(1)} %fusion.143, f32[1536,256]{0,1:T(8,128)S(1)} %fusion.115, f32[4,1536]{1,0:T(4,128)S(1)} %fusion.43, f32[256,4]{0,1:T(4,128)S(1)} %copy-done.6), kind=kOutput, calls=%fused_computation.98 | convolution fusion | flops 12189696 | bytes 6326272 | tf_op jit(solution)/shard_map/jvp()/dot_general | solution.py:40
  57.0 1.8 %multiply_add_fusion = (f32[256,1536]{1,0:T(8,128)S(1)}, f32[256,1536]{1,0:T(8,128)S(1)}) fusion(f32[256,1536]{1,0:T(8,128)S(1)} %get-tuple-element.58, f32[1536]{0:T(1024)S(1)} %get-tuple-element.50, f32[2,256,288]{1,2,0:T(8,128)S(1)} %copy-done.5, f32[32,1536]{1,0:T(8,128)S(1)} %multiply_reduce_fusion.11), kind=kOutput, calls=%fused_computation.53 | convolution fusion | flops 682278912 | bytes 6791168 | tf_op jit(solution)/shard_map/jvp()/dot_general | solution.py:40
  61.5 1.7 %multiply_reduce_fusion.2 = (f32[1536]{0:T(1024)S(1)}, f32[256,1536]{1,0:T(8,128)S(1)}) fusion(f32[256]{0:T(256)S(1)} %copy-done.7, f32[2,256,288]{1,2,0:T(8,128)S(1)} %copy-done.5, f32[32,1536]{1,0:T(8,128)S(1)} %get-tuple-element.37, f32[256,1536]{1,0:T(8,128)S(1)} %get-tuple-element.62), kind=kOutput, calls=%fused_computation.48 | convolution fusion | flops 682277376 | bytes 3644416 | tf_op jit(solution)/shard_map/jvp()/dot_general | solution.py:40
  63.2 1.6 %convolution_bitcast_fusion.1 = f32[288,1536]{1,0:T(8,128)S(1)} fusion(f32[256,1536]{1,0:T(8,128)S(1)} %get-tuple-element.67, f32[256]{0:T(256)S(1)} %copy-done.7, f32[1536]{0:T(1024)S(1)} %get-tuple-element.50, f32[2,256,288]{1,2,0:T(8,128)S(1)} %copy-done.5), kind=kOutput, calls=%fused_computation.3 | convolution fusion | flops 683409408 | bytes 3646464 | tf_op jit(solution)/shard_map/transpose(jvp())/dot_general | solution.py:40
  67.0 1.2 %multiply_reduce_fusion.1 = (f32[1536]{0:T(1024)S(1)}, f32[256,1536]{1,0:T(8,128)S(1)}) fusion(f32[256,1536]{1,0:T(8,128)S(1)} %get-tuple-element.63, f32[32,1536]{1,0:T(8,128)S(1)} %get-tuple-element.23, f32[2,32,256]{2,1,0:T(8,128)S(1)} %copy-done.1, f32[288,1536]{1,0:T(8,128)S(1)} %convolution_bitcast_fusion.1, f32[256]{0:T(256)S(1)} %copy-done.7), kind=kOutput, calls=%fused_computation.47 | convolution fusion | flops 78641664 | bytes 4955136 | tf_op jit(solution)/shard_map/transpose(jvp())/dot_general | solution.py:40
  68.2 1.4 %convolution_bitcast_fusion = f32[288,1536]{1,0:T(8,128)S(1)} fusion(f32[256,1536]{1,0:T(8,128)S(1)} %get-tuple-element.63, f32[256,1536]{1,0:T(8,128)S(1)} %get-tuple-element.69, f32[1536]{0:T(1024)S(1)} %get-tuple-element.50, f32[2,256,288]{1,2,0:T(8,128)S(1)} %copy-done.5), kind=kOutput, calls=%fused_computation.2 | convolution fusion | flops 683409408 | bytes 5218304 | tf_op jit(solution)/shard_map/transpose(jvp())/dot_general | solution.py:40
  72.3 1.0 fusion.4
  73.3 1.2 %multiply_reduce_fusion = (f32[1536]{0:T(1024)S(1)}, f32[256,1536]{1,0:T(8,128)S(1)}) fusion(f32[256,1536]{1,0:T(8,128)S(1)} %get-tuple-element.59, f32[256,1536]{1,0:T(8,128)S(1)} %fusion.4, f32[32,1536]{1,0:T(8,128)S(1)} %get-tuple-element.21, f32[2,32,256]{2,1,0:T(8,128)S(1)} %copy-done.1), kind=kOutput, calls=%fused_computation.46 | convolution fusion | flops 78248448 | bytes 4954112 | tf_op jit(solution)/shard_map/transpose(jvp())/dot_general | solution.py:40
  74.5 1.1 fusion.113
  75.6 1.0 fusion.45
  77.3 8.3 %collective-permute-start.7 = (f32[3,3,3,256]{3,2,1,0:T(4,128)S(1)}, f32[3,3,3,256]{3,2,1,0:T(4,128)S(1)}, u32[]{:S(2)}, u32[]{:S(2)}) collective-permute-start(f32[3,3,3,256]{3,2,1,0:T(4,128)S(1)} %bitcast.201), channel_id=1, source_target_pairs={{64,0},{128,64},{192,128},{256,192},{320,256},{384,320},{448,384},... | collective-permute-start | bytes 82952 | tf_op jit(solution)/shard_map/ppermute | solution.py:34
  85.7 1.9 %collective-permute-start.6 = (f32[3,3,3,256]{3,2,1,0:T(4,128)S(1)}, f32[3,3,3,256]{3,2,1,0:T(4,128)S(1)}, u32[]{:S(2)}, u32[]{:S(2)}) collective-permute-start(f32[3,3,3,256]{3,2,1,0:T(4,128)S(1)} %bitcast.200), channel_id=1, source_target_pairs={{0,64},{64,128},{128,192},{192,256},{256,320},{320,384},{384,448},... | collective-permute-start | bytes 82952 | tf_op jit(solution)/shard_map/ppermute | solution.py:33
  87.8 10.1 %collective-permute-done.6 = f32[3,3,3,256]{3,2,1,0:T(4,128)S(1)} collective-permute-done((f32[3,3,3,256]{3,2,1,0:T(4,128)S(1)}, f32[3,3,3,256]{3,2,1,0:T(4,128)S(1)}, u32[]{:S(2)}, u32[]{:S(2)}) %collective-permute-start.6) | collective-permute-done | bytes 27680 | tf_op jit(solution)/shard_map/ppermute | solution.py:33
  98.0 2.9 %collective-permute-start.9 = (f32[3,3,256]{2,1,0:T(4,128)S(1)}, f32[3,3,256]{2,1,0:T(4,128)S(1)}, u32[]{:S(2)}, u32[]{:S(2)}) collective-permute-start(f32[3,3,256]{2,1,0:T(4,128)S(1)} %get-tuple-element.45), channel_id=1, source_target_pairs={{4,0},{8,4},{12,8},{16,12},{20,16},{24,20},{28,24},{32,28},{36,32}... | collective-permute-start | bytes 27656 | tf_op jit(solution)/shard_map/ppermute | solution.py:34
  101.0 1.3 %collective-permute-done.8 = f32[3,3,256]{2,1,0:T(4,128)S(1)} collective-permute-done((f32[3,3,256]{2,1,0:T(4,128)S(1)}, f32[3,3,256]{2,1,0:T(4,128)S(1)}, u32[]{:S(2)}, u32[]{:S(2)}) %collective-permute-start.8) | collective-permute-done | bytes 9248 | tf_op jit(solution)/shard_map/ppermute | solution.py:33
  102.6 8.9 %all_to_all.5 = f32[4,20,128]{2,1,0:T(8,128)S(1)} all-to-all(f32[4,20,128]{2,1,0:T(8,128)S(1)} %copy.65), channel_id=1, replica_groups=mesh['gx'=16,'gy'=16,'gz'=4] {'gz'}, dimensions={0} | all-to-all | bytes 81920 | tf_op jit(solution)/shard_map/all_to_all | solution.py:231
  (117 shorter events, 16.9 us)
Async XLA Ops:
  0.0 53.6 %copy-start = (f32[32,256]{1,0:T(8,128)S(1)}, f32[32,256]{1,0:T(8,128)}, u32[]{:S(2)}) copy-start(f32[32,256]{1,0:T(8,128)} %param.27) | copy-start | bytes 98308
  0.0 22.1 %copy-start.3 = (f32[1,1,1,3,256]{4,2,3,1,0:T(1,128)S(1)}, f32[1,1,1,3,256]{4,2,3,1,0:T(1,128)}, u32[]{:S(2)}) copy-start(f32[1,1,1,3,256]{4,2,3,1,0:T(1,128)} %param.16) | copy-start | bytes 9220
  0.0 22.1 %collective-permute-start.1 = (f32[1,1,1,3,256]{4,2,3,1,0:T(1,128)}, f32[1,1,1,3,256]{4,2,3,1,0:T(1,128)S(1)}, u32[]{:S(2)}, u32[]{:S(2)}) collective-permute-start(f32[1,1,1,3,256]{4,2,3,1,0:T(1,128)} %param.16), channel_id=1, source_target_pairs={{64,0},{128,64},{192,128},{256,192},{320,256},{384,320},{448,384},... | collective-permute-start | bytes 9224 | tf_op jit(solution)/shard_map/ppermute | solution.py:25
  10.3 11.7 %collective-permute-start = (f32[1,1,1,3,256]{4,2,3,1,0:T(1,128)}, f32[1,1,1,3,256]{4,2,3,1,0:T(1,128)S(1)}, u32[]{:S(2)}, u32[]{:S(2)}) collective-permute-start(f32[1,1,1,3,256]{4,2,3,1,0:T(1,128)} %param.16), channel_id=1, source_target_pairs={{0,64},{64,128},{128,192},{192,256},{256,320},{320,384},{384,448},... | collective-permute-start | bytes 9224 | tf_op jit(solution)/shard_map/ppermute | solution.py:22
  18.1 32.8 %copy-start.4 = (f32[256,8]{0,1:T(8,128)S(1)}, f32[256,8]{0,1:T(8,128)}, u32[]{:S(2)}) copy-start(f32[256,8]{0,1:T(8,128)} %param.22) | copy-start | bytes 24580
  22.1 14.8 %collective-permute-start.3 = (f32[3,1,1,3,256]{4,2,3,1,0:T(1,128)S(1)}, f32[3,1,1,3,256]{4,2,3,1,0:T(1,128)S(1)}, u32[]{:S(2)}, u32[]{:S(2)}) collective-permute-start(f32[3,1,1,3,256]{4,2,3,1,0:T(1,128)S(1)} %constant_dynamic-update-slice_fusion), channel_id=1, source_target_pairs={{4,0},{8,4},{12,8},{16,12},{20,16},{24,20},{28,24},{32,28},{36,32}... | collective-permute-start | bytes 27656 | tf_op jit(solution)/shard_map/ppermute | solution.py:25
  35.5 4.3 %collective-permute-start.2 = (f32[3,1,1,3,256]{4,2,3,1,0:T(1,128)S(1)}, f32[3,1,1,3,256]{4,2,3,1,0:T(1,128)S(1)}, u32[]{:S(2)}, u32[]{:S(2)}) collective-permute-start(f32[3,1,1,3,256]{4,2,3,1,0:T(1,128)S(1)} %constant_dynamic-update-slice_fusion), channel_id=1, source_target_pairs={{0,4},{4,8},{8,12},{12,16},{16,20},{20,24},{24,28},{28,32},{32,36}... | collective-permute-start | bytes 27656 | tf_op jit(solution)/shard_map/ppermute | solution.py:22
  39.9 6.5 %collective-permute-start.5 = (f32[3,3,1,4,256]{4,2,3,1,0:T(1,128)S(1)}, f32[3,3,1,4,256]{4,2,3,1,0:T(1,128)S(1)}, u32[]{:S(2)}, u32[]{:S(2)}) collective-permute-start(f32[3,3,1,4,256]{4,2,3,1,0:T(1,128)S(1)} %pad_maximum_fusion.6), channel_id=1, source_target_pairs={{1,0},{2,1},{3,2},{0,3},{5,4},{6,5},{7,6},{4,7},{9,8},{10,9},{11,1... | collective-permute-start | bytes 110600 | tf_op jit(solution)/shard_map/ppermute | solution.py:25
  43.2 5.9 %collective-permute-start.4 = (f32[3,3,1,4,256]{4,2,3,1,0:T(1,128)S(1)}, f32[3,3,1,4,256]{4,2,3,1,0:T(1,128)S(1)}, u32[]{:S(2)}, u32[]{:S(2)}) collective-permute-start(f32[3,3,1,4,256]{4,2,3,1,0:T(1,128)S(1)} %pad_maximum_fusion.6), channel_id=1, source_target_pairs={{0,1},{1,2},{2,3},{3,0},{4,5},{5,6},{6,7},{7,4},{8,9},{9,10},{10,1... | collective-permute-start | bytes 110600 | tf_op jit(solution)/shard_map/ppermute | solution.py:22
  49.2 2.7 %copy-start.2 = (f32[32,8]{0,1:T(8,128)S(1)}, f32[32,8]{0,1:T(8,128)}, u32[]{:S(2)}) copy-start(f32[32,8]{0,1:T(8,128)} %param.25) | copy-start | bytes 3076
  49.2 3.1 %copy-start.6 = (f32[256,4]{0,1:T(4,128)S(1)}, f32[256,4]{0,1:T(4,128)}, u32[]{:S(2)}) copy-start(f32[256,4]{0,1:T(4,128)} %param.23) | copy-start | bytes 12292
  53.6 0.8 copy-start.1
  56.0 1.1 copy-start.5
  60.8 0.7 copy-start.7
  77.3 10.5 %collective-permute-start.7 = (f32[3,3,3,256]{3,2,1,0:T(4,128)S(1)}, f32[3,3,3,256]{3,2,1,0:T(4,128)S(1)}, u32[]{:S(2)}, u32[]{:S(2)}) collective-permute-start(f32[3,3,3,256]{3,2,1,0:T(4,128)S(1)} %bitcast.201), channel_id=1, source_target_pairs={{64,0},{128,64},{192,128},{256,192},{320,256},{384,320},{448,384},... | collective-permute-start | bytes 82952 | tf_op jit(solution)/shard_map/ppermute | solution.py:34
  85.7 12.3 %collective-permute-start.6 = (f32[3,3,3,256]{3,2,1,0:T(4,128)S(1)}, f32[3,3,3,256]{3,2,1,0:T(4,128)S(1)}, u32[]{:S(2)}, u32[]{:S(2)}) collective-permute-start(f32[3,3,3,256]{3,2,1,0:T(4,128)S(1)} %bitcast.200), channel_id=1, source_target_pairs={{0,64},{64,128},{128,192},{192,256},{256,320},{320,384},{384,448},... | collective-permute-start | bytes 82952 | tf_op jit(solution)/shard_map/ppermute | solution.py:33
  98.0 4.3 %collective-permute-start.8 = (f32[3,3,256]{2,1,0:T(4,128)S(1)}, f32[3,3,256]{2,1,0:T(4,128)S(1)}, u32[]{:S(2)}, u32[]{:S(2)}) collective-permute-start(f32[3,3,256]{2,1,0:T(4,128)S(1)} %get-tuple-element.44), channel_id=1, source_target_pairs={{0,4},{4,8},{8,12},{12,16},{16,20},{20,24},{24,28},{28,32},{32,36}... | collective-permute-start | bytes 27656 | tf_op jit(solution)/shard_map/ppermute | solution.py:33
  98.0 4.3 %collective-permute-start.9 = (f32[3,3,256]{2,1,0:T(4,128)S(1)}, f32[3,3,256]{2,1,0:T(4,128)S(1)}, u32[]{:S(2)}, u32[]{:S(2)}) collective-permute-start(f32[3,3,256]{2,1,0:T(4,128)S(1)} %get-tuple-element.45), channel_id=1, source_target_pairs={{4,0},{8,4},{12,8},{16,12},{20,16},{24,20},{28,24},{32,28},{36,32}... | collective-permute-start | bytes 27656 | tf_op jit(solution)/shard_map/ppermute | solution.py:34

commit v7 on v5

--- a/solution.py
+++ b/solution.py
@@ -42,6 +42,38 @@
 
 def matmul_t(left, right, precision=lax.Precision.HIGH):
     return lax.dot_general(left, right, (((1,), (1,)), ((), ())), precision=precision)
+
+
+@jax.custom_vjp
+def lookup(table, hot):
+    return matmul(table, hot, lax.Precision.HIGHEST)
+
+
+def lookup_fwd(table, hot):
+    return lookup(table, hot), hot
+
+
+def lookup_bwd(hot, cotangent):
+    return matmul_t(cotangent, hot), None
+
+
+lookup.defvjp(lookup_fwd, lookup_bwd)
+
+
+@jax.custom_vjp
+def lookup_t(table, hot):
+    return matmul_t(table, hot, lax.Precision.HIGHEST)
+
+
+def lookup_t_fwd(table, hot):
+    return lookup_t(table, hot), hot
+
+
+def lookup_t_bwd(hot, cotangent):
+    return matmul(cotangent, hot), None
+
+
+lookup_t.defvjp(lookup_t_fwd, lookup_t_bwd)
 
 
 def pair_energy(
@@ -74,11 +106,9 @@
     atom_hot = (atoms[:, None] == atom_index[None]).astype(jnp.float32)
     slot_hot = (jnp.arange(slots)[:, None] == slot_index[None]).astype(jnp.float32)
     member = (centres[:, None] == atoms[None]).astype(jnp.float32)
-    by_atom = matmul(
-        extended.reshape(slots * 3, atoms_here), atom_hot, lax.Precision.HIGHEST
-    )
+    by_atom = lookup(extended.reshape(slots * 3, atoms_here), atom_hot)
     far_end = jnp.sum(by_atom.reshape(slots, 3, pair_count) * slot_hot[:, None, :], axis=0)
-    near_end = matmul_t(extended[13], member, lax.Precision.HIGHEST)
+    near_end = lookup_t(extended[13], member)
     displace = far_end + shifts - near_end
     distance = jnp.sqrt(jnp.sum(displace * displace, axis=0))
     unit = displace / distance
@@ -161,7 +191,7 @@
         energy_weight,
     )
     grad = grad.reshape(3, 3, 3, 3, atoms_here)
-    partial = fold_halo(grad, ("gx", "gy"))
+    partial = fold_halo(grad.transpose(1, 0, 2, 3, 4), ("gy", "gx"))
     myself = lax.axis_index("gz")
     receivers = jnp.arange(zcount)
     sources = jnp.arange(zcount)

time: 113 us -> 108 us (0.956)
  the two profiles are of different devices: /device:TPU:2 before, /device:TPU:112 now
where the time goes in v7:
time: 108 us; the launch traced here: 107 us
  starting transfers between devices  42.3 us (39%)
  matrix products  27.5 us (25%)
  waiting for transfers between devices  20 us (19%)
  blocking collectives  8.06 us (7%)
  other arithmetic  5.79 us (5%)
  local copies, waits for them, and re-layouts  2.42 us (2%)
  between operations  1.28 us (1%)
    ppermute x3, starting transfers between devices, extended_2(): lax.ppermute(lax.slice_in_dim(block, 0, width, axis=dim), axis, backward)  22.8 us
    dot_general x21, matrix products, matmul(): return jnp.dot(left, right, precision=precision)  21 us
    ppermute x3, starting transfers between devices, extended_2(): lax.ppermute(lax.slice_in_dim(block, block.shape[dim] - width, None, axis...  10.6 us
    ppermute x2, waiting for transfers between devices, fold_halo(): from_high = lax.ppermute(grad[0], axis, backward)  9.24 us
    all_to_all x1, blocking collectives, per_device(): lax.all_to_all(outgoing, 'gz', split_axis=0, concat_axis=0, tiled=True)  8.06 us
    ppermute x3, waiting for transfers between devices, extended_2(): lax.ppermute(lax.slice_in_dim(block, block.shape[dim] - width, None, axis...  7.96 us
    dot_general x6, matrix products, matmul_t(): lax.dot_general(left, right, (((1,), (1,)), ((), ())), precision=precision)  5.55 us
    ppermute x2, starting transfers between devices, fold_halo(): from_high = lax.ppermute(grad[0], axis, backward)  5.23 us
  transfers between devices with their start and end apart: 10, of which 5 were waited for; matrix products, arithmetic and copies ran while one was open for 7% of the time, Pallas kernels for 0%

profile of v7, /device:TPU:112, one launch (start us, length us, event | category | flops | bytes accessed | tf_op | source)
XLA Modules:
  0.0 107.4 jit_solution(11100407364679437167)
XLA Ops:
  0.0 3.3 %collective-permute-start.1 = (f32[1,1,1,3,256]{4,2,3,1,0:T(1,128)}, f32[1,1,1,3,256]{4,2,3,1,0:T(1,128)S(1)}, u32[]{:S(2)}, u32[]{:S(2)}) collective-permute-start(f32[1,1,1,3,256]{4,2,3,1,0:T(1,128)} %param.16), channel_id=1, source_target_pairs={{64,0},{128,64},{192,128},{256,192},{320,256},{384,320},{448,384},... | collective-permute-start | bytes 9224 | tf_op jit(solution)/shard_map/ppermute | solution.py:25
  3.3 8.7 %collective-permute-start = (f32[1,1,1,3,256]{4,2,3,1,0:T(1,128)}, f32[1,1,1,3,256]{4,2,3,1,0:T(1,128)S(1)}, u32[]{:S(2)}, u32[]{:S(2)}) collective-permute-start(f32[1,1,1,3,256]{4,2,3,1,0:T(1,128)} %param.16), channel_id=1, source_target_pairs={{0,64},{64,128},{128,192},{192,256},{256,320},{320,384},{384,448},... | collective-permute-start | bytes 9224 | tf_op jit(solution)/shard_map/ppermute | solution.py:22
  15.8 0.8 maximum_bitcast_fusion.1
  16.8 1.1 %fusion.39 = f32[4,1536]{1,0:T(4,128)S(1)} fusion(s32[1536]{0:T(1024)S(1)} %get-tuple-element.28, s32[256]{0:T(256)} %bitcast.218), kind=kOutput, calls=%fused_computation.64 | convolution fusion | flops 3539968 | bytes 31744 | tf_op jit(solution)/shard_map/jvp()/dot_general | solution.py:44
  17.9 1.3 %fusion.115 = f32[1536,256]{0,1:T(8,128)S(1)} fusion(f32[256,4]{0,1:T(4,128)} %param.24, s32[1536]{0:T(1024)S(1)} %get-tuple-element.26), kind=kOutput, calls=%fused_computation.183 | convolution fusion | flops 9443328 | bytes 1583104 | tf_op jit(solution)/shard_map/jvp()/dot_general | solution.py:40
  19.3 14.3 %collective-permute-start.3 = (f32[3,1,1,3,256]{4,2,3,1,0:T(1,128)S(1)}, f32[3,1,1,3,256]{4,2,3,1,0:T(1,128)S(1)}, u32[]{:S(2)}, u32[]{:S(2)}) collective-permute-start(f32[3,1,1,3,256]{4,2,3,1,0:T(1,128)S(1)} %constant_dynamic-update-slice_fusion), channel_id=1, source_target_pairs={{4,0},{8,4},{12,8},{16,12},{20,16},{24,20},{28,24},{32,28},{36,32}... | collective-permute-start | bytes 27656 | tf_op jit(solution)/shard_map/ppermute | solution.py:25
  33.6 1.4 %collective-permute-done.3 = f32[3,1,1,3,256]{4,2,3,1,0:T(1,128)S(1)} collective-permute-done((f32[3,1,1,3,256]{4,2,3,1,0:T(1,128)S(1)}, f32[3,1,1,3,256]{4,2,3,1,0:T(1,128)S(1)}, u32[]{:S(2)}, u32[]{:S(2)}) %collective-permute-start.3) | collective-permute-done | bytes 9248 | tf_op jit(solution)/shard_map/ppermute | solution.py:25
  35.0 2.9 %collective-permute-done.2 = f32[3,1,1,3,256]{4,2,3,1,0:T(1,128)S(1)} collective-permute-done((f32[3,1,1,3,256]{4,2,3,1,0:T(1,128)S(1)}, f32[3,1,1,3,256]{4,2,3,1,0:T(1,128)S(1)}, u32[]{:S(2)}, u32[]{:S(2)}) %collective-permute-start.2) | collective-permute-done | bytes 9248 | tf_op jit(solution)/shard_map/ppermute | solution.py:22
  38.0 5.3 %collective-permute-start.5 = (f32[3,3,1,4,256]{4,2,3,1,0:T(1,128)S(1)}, f32[3,3,1,4,256]{4,2,3,1,0:T(1,128)S(1)}, u32[]{:S(2)}, u32[]{:S(2)}) collective-permute-start(f32[3,3,1,4,256]{4,2,3,1,0:T(1,128)S(1)} %pad_maximum_fusion.6), channel_id=1, source_target_pairs={{1,0},{2,1},{3,2},{0,3},{5,4},{6,5},{7,6},{4,7},{9,8},{10,9},{11,1... | collective-permute-start | bytes 110600 | tf_op jit(solution)/shard_map/ppermute | solution.py:25
  43.2 1.9 %collective-permute-start.4 = (f32[3,3,1,4,256]{4,2,3,1,0:T(1,128)S(1)}, f32[3,3,1,4,256]{4,2,3,1,0:T(1,128)S(1)}, u32[]{:S(2)}, u32[]{:S(2)}) collective-permute-start(f32[3,3,1,4,256]{4,2,3,1,0:T(1,128)S(1)} %pad_maximum_fusion.6), channel_id=1, source_target_pairs={{0,1},{1,2},{2,3},{3,0},{4,5},{5,6},{6,7},{7,4},{8,9},{9,10},{10,1... | collective-permute-start | bytes 110600 | tf_op jit(solution)/shard_map/ppermute | solution.py:22
  45.8 5.0 %collective-permute-done.4 = f32[3,3,1,4,256]{4,2,3,1,0:T(1,128)S(1)} collective-permute-done((f32[3,3,1,4,256]{4,2,3,1,0:T(1,128)S(1)}, f32[3,3,1,4,256]{4,2,3,1,0:T(1,128)S(1)}, u32[]{:S(2)}, u32[]{:S(2)}) %collective-permute-start.4) | collective-permute-done | bytes 36896 | tf_op jit(solution)/shard_map/ppermute | solution.py:22
  51.8 0.9 multiply_reduce_fusion.17
  52.7 0.9 fusion.95
  54.1 1.2 %broadcast_multiply_fusion = (f32[256,1536]{1,0:T(8,128)S(1)}, f32[256,1536]{1,0:T(8,128)S(1)}) fusion(f32[1536]{0:T(1024)S(1)} %get-tuple-element.45, f32[1536,256]{0,1:T(8,128)S(1)} %fusion.115, f32[1536,256]{0,1:T(8,128)S(1)} %fusion.95, f32[4,1536]{1,0:T(4,128)S(1)} %fusion.39, f32[256,4]{0,1:T(4,128)S(1)} %copy-done.6), kind=kOutput, calls=%fused_computation.85 | convolution fusion | flops 12189696 | bytes 6326272 | tf_op jit(solution)/shard_map/jvp()/dot_general | solution.py:40
  57.3 1.4 %fusion.37 = f32[96,1536]{1,0:T(8,128)S(1)} fusion(f32[96,256]{1,0:T(8,128)S(1)} %fusion.47, s32[1536]{0:T(1024)S(1)} %get-tuple-element.28), kind=kOutput, calls=%fused_computation.62 | convolution fusion | flops 226885632 | bytes 694272 | tf_op jit(solution)/shard_map/jvp()/dot_general | solution.py:44
  58.8 1.8 %multiply_add_fusion = (f32[256,1536]{1,0:T(8,128)S(1)}, f32[256,1536]{1,0:T(8,128)S(1)}) fusion(f32[256,1536]{1,0:T(8,128)S(1)} %get-tuple-element.53, f32[1536]{0:T(1024)S(1)} %get-tuple-element.45, f32[2,256,288]{1,2,0:T(8,128)S(1)} %copy-done.5, f32[32,1536]{1,0:T(8,128)S(1)} %multiply_reduce_fusion.11), kind=kOutput, calls=%fused_computation.49 | convolution fusion | flops 682278912 | bytes 6791168 | tf_op jit(solution)/shard_map/jvp()/dot_general | solution.py:40
  61.7 1.2 %fusion.35 = f32[96,1536]{1,0:T(8,128)S(1)} fusion(f32[96,256]{1,0:T(8,128)S(1)} %fusion.48, s32[1536]{0:T(1024)S(1)} %get-tuple-element.28), kind=kOutput, calls=%fused_computation.60 | convolution fusion | flops 226885632 | bytes 694272 | tf_op jit(solution)/shard_map/jvp()/dot_general | solution.py:44
  63.1 1.7 %multiply_reduce_fusion.2 = (f32[1536]{0:T(1024)S(1)}, f32[256,1536]{1,0:T(8,128)S(1)}) fusion(f32[256]{0:T(256)S(1)} %copy-done.7, f32[2,256,288]{1,2,0:T(8,128)S(1)} %copy-done.5, f32[32,1536]{1,0:T(8,128)S(1)} %get-tuple-element.33, f32[256,1536]{1,0:T(8,128)S(1)} %get-tuple-element.57), kind=kOutput, calls=%fused_computation.44 | convolution fusion | flops 682277376 | bytes 3644416 | tf_op jit(solution)/shard_map/jvp()/dot_general | solution.py:40
  64.9 1.4 %convolution_bitcast_fusion.1 = f32[288,1536]{1,0:T(8,128)S(1)} fusion(f32[256,1536]{1,0:T(8,128)S(1)} %get-tuple-element.62, f32[256]{0:T(256)S(1)} %copy-done.7, f32[1536]{0:T(1024)S(1)} %get-tuple-element.45, f32[2,256,288]{1,2,0:T(8,128)S(1)} %copy-done.5), kind=kOutput, calls=%fused_computation.3 | convolution fusion | flops 683409408 | bytes 3646464 | tf_op jit(solution)/shard_map/transpose(jvp())/dot_general | solution.py:40
  67.0 1.2 %fusion.33 = f32[96,1536]{1,0:T(8,128)S(1)} fusion(f32[96,256]{1,0:T(8,128)S(1)} %fusion.49, s32[1536]{0:T(1024)S(1)} %get-tuple-element.28), kind=kOutput, calls=%fused_computation.58 | convolution fusion | flops 226885632 | bytes 694272 | tf_op jit(solution)/shard_map/transpose(jvp())/dot_general | solution.py:40
  68.3 1.2 %multiply_reduce_fusion.1 = (f32[1536]{0:T(1024)S(1)}, f32[256,1536]{1,0:T(8,128)S(1)}) fusion(f32[256,1536]{1,0:T(8,128)S(1)} %get-tuple-element.58, f32[32,1536]{1,0:T(8,128)S(1)} %get-tuple-element.23, f32[2,32,256]{2,1,0:T(8,128)S(1)} %copy-done.1, f32[288,1536]{1,0:T(8,128)S(1)} %convolution_bitcast_fusion.1, f32[256]{0:T(256)S(1)} %copy-done.7), kind=kOutput, calls=%fused_computation.43 | convolution fusion | flops 78641664 | bytes 4955136 | tf_op jit(solution)/shard_map/transpose(jvp())/dot_general | solution.py:40
  69.6 1.4 %convolution_bitcast_fusion = f32[288,1536]{1,0:T(8,128)S(1)} fusion(f32[256,1536]{1,0:T(8,128)S(1)} %get-tuple-element.58, f32[256,1536]{1,0:T(8,128)S(1)} %get-tuple-element.64, f32[1536]{0:T(1024)S(1)} %get-tuple-element.45, f32[2,256,288]{1,2,0:T(8,128)S(1)} %copy-done.5), kind=kOutput, calls=%fused_computation.2 | convolution fusion | flops 683409408 | bytes 5218304 | tf_op jit(solution)/shard_map/transpose(jvp())/dot_general | solution.py:40
  71.7 1.4 %fusion.31 = f32[96,1536]{1,0:T(8,128)S(1)} fusion(f32[96,256]{1,0:T(8,128)S(1)} %fusion.50, s32[1536]{0:T(1024)S(1)} %get-tuple-element.28), kind=kOutput, calls=%fused_computation.56 | convolution fusion | flops 226885632 | bytes 694272 | tf_op jit(solution)/shard_map/transpose(jvp())/dot_general | solution.py:40
  73.8 1.0 fusion.4
  74.8 1.1 %multiply_reduce_fusion = (f32[1536]{0:T(1024)S(1)}, f32[256,1536]{1,0:T(8,128)S(1)}) fusion(f32[256,1536]{1,0:T(8,128)S(1)} %get-tuple-element.54, f32[256,1536]{1,0:T(8,128)S(1)} %fusion.4, f32[32,1536]{1,0:T(8,128)S(1)} %get-tuple-element.21, f32[2,32,256]{2,1,0:T(8,128)S(1)} %copy-done.1), kind=kOutput, calls=%fused_computation.42 | convolution fusion | flops 78248448 | bytes 4954112 | tf_op jit(solution)/shard_map/transpose(jvp())/dot_general | solution.py:40
  76.0 1.1 %fusion.91 = (f32[1536]{0:T(1024)S(1)}, f32[1536]{0:T(1024)S(1)}) fusion(f32[1536]{0:T(1024)S(1)} %get-tuple-element.44, f32[1536]{0:T(1024)S(1)} %get-tuple-element.46, f32[8]{0:T(128)S(1)} %get-tuple-element.66, f32[8]{0:T(128)S(1)} %get-tuple-element.65, f32[1536,8]{0,1:T(8,128)S(1)} %fusion.85, f32[256,8]{0,1:T(8,128)S(1)} %copy-done.4, ...), kind=kOutput, calls=%fused_computation.144 | convolution fusion | flops 22950912 | bytes 3233856 | tf_op jit(solution)/shard_map/transpose(jvp())/dot_general | solution.py:40
  78.3 2.9 %collective-permute-start.7 = (f32[3,3,3,256]{3,2,1,0:T(4,128)S(1)}, f32[3,3,3,256]{3,2,1,0:T(4,128)S(1)}, u32[]{:S(2)}, u32[]{:S(2)}) collective-permute-start(f32[3,3,3,256]{3,2,1,0:T(4,128)S(1)} %get-tuple-element.36), channel_id=1, source_target_pairs={{4,0},{8,4},{12,8},{16,12},{20,16},{24,20},{28,24},{32,28},{36,32}... | collective-permute-start | bytes 82952 | tf_op jit(solution)/shard_map/ppermute | solution.py:34
  81.5 1.4 %collective-permute-done.6 = f32[3,3,3,256]{3,2,1,0:T(4,128)S(1)} collective-permute-done((f32[3,3,3,256]{3,2,1,0:T(4,128)S(1)}, f32[3,3,3,256]{3,2,1,0:T(4,128)S(1)}, u32[]{:S(2)}, u32[]{:S(2)}) %collective-permute-start.6) | collective-permute-done | bytes 27680 | tf_op jit(solution)/shard_map/ppermute | solution.py:33
  82.9 3.6 %collective-permute-start.8 = (f32[3,3,256]{2,1,0:T(4,128)S(1)}, f32[3,3,256]{2,1,0:T(4,128)S(1)}, u32[]{:S(2)}, u32[]{:S(2)}) collective-permute-start(f32[3,3,256]{2,1,0:T(4,128)S(1)} %get-tuple-element.39), channel_id=1, source_target_pairs={{0,64},{64,128},{128,192},{192,256},{256,320},{320,384},{384,448},... | collective-permute-start | bytes 27656 | tf_op jit(solution)/shard_map/ppermute | solution.py:33
  86.5 2.3 %collective-permute-start.9 = (f32[3,3,256]{2,1,0:T(4,128)S(1)}, f32[3,3,256]{2,1,0:T(4,128)S(1)}, u32[]{:S(2)}, u32[]{:S(2)}) collective-permute-start(f32[3,3,256]{2,1,0:T(4,128)S(1)} %get-tuple-element.40), channel_id=1, source_target_pairs={{64,0},{128,64},{192,128},{256,192},{320,256},{384,320},{448,384},... | collective-permute-start | bytes 27656 | tf_op jit(solution)/shard_map/ppermute | solution.py:34
  88.8 9.2 %collective-permute-done.9 = f32[3,3,256]{2,1,0:T(4,128)S(1)} collective-permute-done((f32[3,3,256]{2,1,0:T(4,128)S(1)}, f32[3,3,256]{2,1,0:T(4,128)S(1)}, u32[]{:S(2)}, u32[]{:S(2)}) %collective-permute-start.9) | collective-permute-done | bytes 9248 | tf_op jit(solution)/shard_map/ppermute | solution.py:34
  98.3 8.1 %all_to_all.5 = f32[4,20,128]{2,1,0:T(8,128)S(1)} all-to-all(f32[4,20,128]{2,1,0:T(8,128)S(1)} %copy.75), channel_id=1, replica_groups=mesh['gx'=16,'gy'=16,'gz'=4] {'gz'}, dimensions={0} | all-to-all | bytes 81920 | tf_op jit(solution)/shard_map/all_to_all | solution.py:216
  (107 shorter events, 13.4 us)
Async XLA Ops:
  0.0 55.4 %copy-start = (f32[32,256]{1,0:T(8,128)S(1)}, f32[32,256]{1,0:T(8,128)}, u32[]{:S(2)}) copy-start(f32[32,256]{1,0:T(8,128)} %param.27) | copy-start | bytes 98308
  0.0 19.3 %copy-start.3 = (f32[1,1,1,3,256]{4,2,3,1,0:T(1,128)S(1)}, f32[1,1,1,3,256]{4,2,3,1,0:T(1,128)}, u32[]{:S(2)}) copy-start(f32[1,1,1,3,256]{4,2,3,1,0:T(1,128)} %param.16) | copy-start | bytes 9220
  0.0 19.3 %collective-permute-start.1 = (f32[1,1,1,3,256]{4,2,3,1,0:T(1,128)}, f32[1,1,1,3,256]{4,2,3,1,0:T(1,128)S(1)}, u32[]{:S(2)}, u32[]{:S(2)}) collective-permute-start(f32[1,1,1,3,256]{4,2,3,1,0:T(1,128)} %param.16), channel_id=1, source_target_pairs={{64,0},{128,64},{192,128},{256,192},{320,256},{384,320},{448,384},... | collective-permute-start | bytes 9224 | tf_op jit(solution)/shard_map/ppermute | solution.py:25
  3.3 16.0 %collective-permute-start = (f32[1,1,1,3,256]{4,2,3,1,0:T(1,128)}, f32[1,1,1,3,256]{4,2,3,1,0:T(1,128)S(1)}, u32[]{:S(2)}, u32[]{:S(2)}) collective-permute-start(f32[1,1,1,3,256]{4,2,3,1,0:T(1,128)} %param.16), channel_id=1, source_target_pairs={{0,64},{64,128},{128,192},{192,256},{256,320},{320,384},{384,448},... | collective-permute-start | bytes 9224 | tf_op jit(solution)/shard_map/ppermute | solution.py:22
  17.9 34.9 %copy-start.4 = (f32[256,8]{0,1:T(8,128)S(1)}, f32[256,8]{0,1:T(8,128)}, u32[]{:S(2)}) copy-start(f32[256,8]{0,1:T(8,128)} %param.22) | copy-start | bytes 24580
  19.3 15.7 %collective-permute-start.3 = (f32[3,1,1,3,256]{4,2,3,1,0:T(1,128)S(1)}, f32[3,1,1,3,256]{4,2,3,1,0:T(1,128)S(1)}, u32[]{:S(2)}, u32[]{:S(2)}) collective-permute-start(f32[3,1,1,3,256]{4,2,3,1,0:T(1,128)S(1)} %constant_dynamic-update-slice_fusion), channel_id=1, source_target_pairs={{4,0},{8,4},{12,8},{16,12},{20,16},{24,20},{28,24},{32,28},{36,32}... | collective-permute-start | bytes 27656 | tf_op jit(solution)/shard_map/ppermute | solution.py:25
  33.6 4.3 %collective-permute-start.2 = (f32[3,1,1,3,256]{4,2,3,1,0:T(1,128)S(1)}, f32[3,1,1,3,256]{4,2,3,1,0:T(1,128)S(1)}, u32[]{:S(2)}, u32[]{:S(2)}) collective-permute-start(f32[3,1,1,3,256]{4,2,3,1,0:T(1,128)S(1)} %constant_dynamic-update-slice_fusion), channel_id=1, source_target_pairs={{0,4},{4,8},{8,12},{12,16},{16,20},{20,24},{24,28},{28,32},{32,36}... | collective-permute-start | bytes 27656 | tf_op jit(solution)/shard_map/ppermute | solution.py:22
  38.0 7.9 %collective-permute-start.5 = (f32[3,3,1,4,256]{4,2,3,1,0:T(1,128)S(1)}, f32[3,3,1,4,256]{4,2,3,1,0:T(1,128)S(1)}, u32[]{:S(2)}, u32[]{:S(2)}) collective-permute-start(f32[3,3,1,4,256]{4,2,3,1,0:T(1,128)S(1)} %pad_maximum_fusion.6), channel_id=1, source_target_pairs={{1,0},{2,1},{3,2},{0,3},{5,4},{6,5},{7,6},{4,7},{9,8},{10,9},{11,1... | collective-permute-start | bytes 110600 | tf_op jit(solution)/shard_map/ppermute | solution.py:25
  43.2 7.7 %collective-permute-start.4 = (f32[3,3,1,4,256]{4,2,3,1,0:T(1,128)S(1)}, f32[3,3,1,4,256]{4,2,3,1,0:T(1,128)S(1)}, u32[]{:S(2)}, u32[]{:S(2)}) collective-permute-start(f32[3,3,1,4,256]{4,2,3,1,0:T(1,128)S(1)} %pad_maximum_fusion.6), channel_id=1, source_target_pairs={{0,1},{1,2},{2,3},{3,0},{4,5},{5,6},{6,7},{7,4},{8,9},{9,10},{10,1... | collective-permute-start | bytes 110600 | tf_op jit(solution)/shard_map/ppermute | solution.py:22
  51.0 2.7 %copy-start.2 = (f32[32,8]{0,1:T(8,128)S(1)}, f32[32,8]{0,1:T(8,128)}, u32[]{:S(2)}) copy-start(f32[32,8]{0,1:T(8,128)} %param.25) | copy-start | bytes 3076
  51.1 3.1 %copy-start.6 = (f32[256,4]{0,1:T(4,128)S(1)}, f32[256,4]{0,1:T(4,128)}, u32[]{:S(2)}) copy-start(f32[256,4]{0,1:T(4,128)} %param.23) | copy-start | bytes 12292
  55.4 0.8 copy-start.1
  56.8 2.1 %copy-start.5 = (f32[2,256,288]{1,2,0:T(8,128)S(1)}, f32[2,256,288]{1,2,0:T(8,128)}, u32[]{:S(2)}) copy-start(f32[2,256,288]{1,2,0:T(8,128)} %param.28) | copy-start | bytes 1769476
  61.7 1.4 %copy-start.7 = (f32[256]{0:T(256)S(1)}, f32[256]{0:T(256)}, u32[]{:S(2)}) copy-start(f32[256]{0:T(256)} %param.29) | copy-start | bytes 3076
  78.3 4.6 %collective-permute-start.6 = (f32[3,3,3,256]{3,2,1,0:T(4,128)S(1)}, f32[3,3,3,256]{3,2,1,0:T(4,128)S(1)}, u32[]{:S(2)}, u32[]{:S(2)}) collective-permute-start(f32[3,3,3,256]{3,2,1,0:T(4,128)S(1)} %get-tuple-element.35), channel_id=1, source_target_pairs={{0,4},{4,8},{8,12},{12,16},{16,20},{20,24},{24,28},{28,32},{32,36}... | collective-permute-start | bytes 82952 | tf_op jit(solution)/shard_map/ppermute | solution.py:33
  78.3 4.6 %collective-permute-start.7 = (f32[3,3,3,256]{3,2,1,0:T(4,128)S(1)}, f32[3,3,3,256]{3,2,1,0:T(4,128)S(1)}, u32[]{:S(2)}, u32[]{:S(2)}) collective-permute-start(f32[3,3,3,256]{3,2,1,0:T(4,128)S(1)} %get-tuple-element.36), channel_id=1, source_target_pairs={{4,0},{8,4},{12,8},{16,12},{20,16},{24,20},{28,24},{32,28},{36,32}... | collective-permute-start | bytes 82952 | tf_op jit(solution)/shard_map/ppermute | solution.py:34
  82.9 5.9 %collective-permute-start.8 = (f32[3,3,256]{2,1,0:T(4,128)S(1)}, f32[3,3,256]{2,1,0:T(4,128)S(1)}, u32[]{:S(2)}, u32[]{:S(2)}) collective-permute-start(f32[3,3,256]{2,1,0:T(4,128)S(1)} %get-tuple-element.39), channel_id=1, source_target_pairs={{0,64},{64,128},{128,192},{192,256},{256,320},{320,384},{384,448},... | collective-permute-start | bytes 27656 | tf_op jit(solution)/shard_map/ppermute | solution.py:33
  86.5 11.6 %collective-permute-start.9 = (f32[3,3,256]{2,1,0:T(4,128)S(1)}, f32[3,3,256]{2,1,0:T(4,128)S(1)}, u32[]{:S(2)}, u32[]{:S(2)}) collective-permute-start(f32[3,3,256]{2,1,0:T(4,128)S(1)} %get-tuple-element.40), channel_id=1, source_target_pairs={{64,0},{128,64},{192,128},{256,192},{320,256},{384,320},{448,384},... | collective-permute-start | bytes 27656 | tf_op jit(solution)/shard_map/ppermute | solution.py:34
